TPU v7x, 1024 devices: a whole 4x8x16 slice. The times are simulated.
1024 devices in a mesh: section: 32 (over y, x_lo, core), mp: 16 (over z), dp: 2 (over x_hi).
Axes of the slice: x: 4 (x_hi: 2, x_lo: 2; x = x_hi * 2 + x_lo), y: 8, z: 16, core: 2. Of those that a mesh axis runs over, the one named last changes fastest.
Arguments:
- lower_out: bfloat16 [32, 2, 256, 3072], P('section', 'dp', None, 'mp'), may hold values from -6 to 6
- upper_out: bfloat16 [32, 2, 256, 3072], P('section', 'dp', None, 'mp'), may hold values from -40 to 40
- lower_grad: bfloat16 [32, 2, 256, 3072], P('section', 'dp', None, 'mp'), may hold values from -1.5 to 1.5
- upper_grad: bfloat16 [32, 2, 256, 3072], P('section', 'dp', None, 'mp'), may hold values from -6 to 6
- norm_gain: bfloat16 [32, 3072], P('section'), may hold values from 0.5 to 1.5
- query_weight: bfloat16 [32, 3072, 4096], P('section', None, 'mp'), may hold values from -1 to 1
- key_weight: bfloat16 [32, 3072, 2048], P('section', None, 'mp'), may hold values from -2 to 2
- value_projection: bfloat16 [32, 3072, 2048], P('section', None, 'mp'), may hold values from -0.109375 to 0.109375
- output_weight: bfloat16 [32, 4096, 3072], P('section', 'mp'), may hold values from -0.375 to 0.375
- key_lists: int32 [2, 2], replicated, may hold values from -1 to 1, as said below
Outputs:
- rebuilt_lower: bfloat16 [32, 2, 256, 3072], P('section', 'dp', None, 'mp')
- upper_in_grad: bfloat16 [32, 2, 256, 3072], P('section', 'dp', None, 'mp')
- gain_grad: float32 [32, 3072], P('section', 'mp')
Inputs may be any that keep to these rules, and one draw needn't show every extreme that they name: `key_lists`: row r names the key blocks that query block r attends to, in increasing order, then -1 in the remaining entries; every row names its own block; exactly one row names all 2 blocks, and every other row names exactly 1 block, its own.
All inputs are finite; a program needn't handle non-finite values.
Results may differ from a plain program's by a relative error of at most 0.024.
The roundings to bfloat16 on the way count: a program that leaves them out, or rounds other values in their place, can miss the bound.
Values may be sent and summed in bfloat16 or wider, within the bound.
No kernel may reach another device: no remote copies, remote signals or barrier semaphores. Data moves between devices by JAX's collectives and lax.ppermute only.
A program may use at most 64 MiB of HBM per device.

v0:
```python
import math

import jax
import jax.numpy as jnp
from jax import lax
from jax.sharding import PartitionSpec as P

HEAD_SIZE = 128


def from_behind(x, axis, by):
    length = lax.axis_size(axis)
    pairs = [(i, i + by) for i in range(length) if 0 <= i + by < length]
    return lax.ppermute(x, axis, pairs)


def token_mask(key_lists, length):
    blocks = key_lists.shape[0]
    columns = jnp.arange(blocks, dtype=jnp.int32)
    block_table = jnp.any(key_lists[:, :, None] == columns[None, None, :], axis=1).astype(
        jnp.float32
    )
    owner = (jnp.arange(length, dtype=jnp.int32) // (length // blocks))[:, None] == columns[None, :]
    one_hot = owner.astype(jnp.float32)
    return jnp.dot(jnp.dot(one_hot, block_table), one_hot.T) > 0.5


def local(
    lower_out,
    upper_out,
    lower_grad,
    upper_grad,
    norm_gain,
    query_weight,
    key_weight,
    value_projection,
    output_weight,
    key_lists,
):
    feature_count = upper_out.shape[3]
    mp_index = lax.axis_index("mp")
    whole_upper, whole_grad = (
        lax.all_gather(upper_out[0, 0], "mp", axis=1, tiled=True),
        lax.all_gather(lower_grad[0, 0], "mp", axis=1, tiled=True),
    )
    stream = whole_upper.astype(jnp.float32)
    inverse = lax.rsqrt(jnp.mean(stream * stream, axis=1, keepdims=True) + 1e-06)
    unit_rows = stream * inverse
    gain_rows = norm_gain[0].astype(jnp.float32)
    normed = (unit_rows * gain_rows).astype(jnp.bfloat16)
    w_query = query_weight[0]
    w_key = key_weight[0]
    w_value = value_projection[0]
    w_output = output_weight[0]
    length = normed.shape[0]
    kv_heads = w_key.shape[1] // HEAD_SIZE
    group_width = w_query.shape[1] // HEAD_SIZE // kv_heads
    query_head_split = jnp.dot(normed, w_query, preferred_element_type=jnp.float32).astype(
        jnp.bfloat16
    )
    query_head_split = query_head_split.reshape(length, kv_heads, group_width, HEAD_SIZE)
    key_head_split = (
        jnp.dot(normed, w_key, preferred_element_type=jnp.float32)
        .astype(jnp.bfloat16)
        .reshape(length, kv_heads, HEAD_SIZE)
    )
    value_head_split = (
        jnp.dot(normed, w_value, preferred_element_type=jnp.float32)
        .astype(jnp.bfloat16)
        .reshape(length, kv_heads, HEAD_SIZE)
    )
    allowed = token_mask(key_lists, length)
    raw_scores = jnp.einsum(
        "qjgd,kjd->jgqk", query_head_split, key_head_split, preferred_element_type=jnp.float32
    ) / math.sqrt(HEAD_SIZE)
    masked = jnp.where(allowed, raw_scores, -1e30)
    row_max = jnp.max(masked, axis=3, keepdims=True)
    exponent = jnp.where(allowed, jnp.exp(masked - row_max), 0.0)
    row_total = jnp.sum(exponent, axis=3, keepdims=True)
    probs_full = exponent / row_total
    probability_half = probs_full.astype(jnp.bfloat16)
    attended = jnp.einsum(
        "jgqk,kjd->qjgd", probability_half, value_head_split, preferred_element_type=jnp.float32
    )
    attended = attended.astype(jnp.bfloat16).reshape(length, -1)
    out_term = jnp.dot(attended, w_output, preferred_element_type=jnp.float32)
    out_share = lax.psum_scatter(
        out_term.astype(jnp.bfloat16), "mp", scatter_dimension=1, tiled=True
    ).astype(jnp.float32)
    rebuilt = (lower_out[0, 0].astype(jnp.float32) - out_share).astype(jnp.bfloat16)
    attention_gradient = jnp.dot(whole_grad, w_output.T, preferred_element_type=jnp.float32).astype(
        jnp.bfloat16
    )
    attention_gradient = attention_gradient.reshape(length, kv_heads, group_width, HEAD_SIZE)
    prob_grad = jnp.einsum(
        "qjgd,kjd->jgqk", attention_gradient, value_head_split, preferred_element_type=jnp.float32
    )
    score_gradient = (
        probs_full
        * (prob_grad - jnp.sum(prob_grad * probs_full, axis=3, keepdims=True))
        / math.sqrt(HEAD_SIZE)
    )
    score_gradient = score_gradient.astype(jnp.bfloat16)
    value_gradient = jnp.einsum(
        "munr,nmuy->rmy", probability_half, attention_gradient, preferred_element_type=jnp.float32
    )
    value_gradient = value_gradient.astype(jnp.bfloat16).reshape(length, -1)
    query_grad = jnp.einsum(
        "jgqk,kjd->qjgd", score_gradient, key_head_split, preferred_element_type=jnp.float32
    )
    query_grad = query_grad.astype(jnp.bfloat16).reshape(length, -1)
    key_gradient = jnp.einsum(
        "munr,nmuy->rmy", score_gradient, query_head_split, preferred_element_type=jnp.float32
    )
    key_gradient = key_gradient.astype(jnp.bfloat16).reshape(length, -1)
    normed_grad = jnp.dot(query_grad, w_query.T, preferred_element_type=jnp.float32)
    normed_grad = normed_grad + jnp.dot(key_gradient, w_key.T, preferred_element_type=jnp.float32)
    normed_grad = normed_grad + jnp.dot(
        value_gradient, w_value.T, preferred_element_type=jnp.float32
    )
    upper_rows = upper_grad[0, 0].astype(jnp.float32)
    weighted = gain_rows * normed_grad
    row_stat = jnp.mean(unit_rows * weighted, axis=1, keepdims=True)
    grad_share = lax.psum_scatter(
        ((weighted - unit_rows * row_stat) * inverse).astype(jnp.bfloat16),
        "mp",
        scatter_dimension=1,
        tiled=True,
    ).astype(jnp.float32)
    lower_rows = upper_rows + grad_share
    gain_whole = lax.psum(jnp.sum(normed_grad * unit_rows, axis=0), ("mp", "dp"))
    gain_grad = lax.dynamic_slice_in_dim(gain_whole, mp_index * feature_count, feature_count, 0)
    entering = lower_rows.astype(jnp.bfloat16)
    sent_lower, sent_grad = from_behind((rebuilt, entering), "section", -1)
    return (sent_lower[None, None], sent_grad[None, None], gain_grad[None])


def solution(mesh):
    placed = (
        P("section", "dp", None, "mp"),
        P("section", "dp", None, "mp"),
        P("section", "dp", None, "mp"),
        P("section", "dp", None, "mp"),
        P("section", None),
        P("section", None, "mp"),
        P("section", None, "mp"),
        P("section", None, "mp"),
        P("section", "mp", None),
        P(),
    )
    return jax.shard_map(
        local,
        mesh=mesh,
        in_specs=placed,
        out_specs=(
            P("section", "dp", None, "mp"),
            P("section", "dp", None, "mp"),
            P("section", "mp"),
        ),
        check_vma=False,
    )
```

profile of v0, /device:TPU:8, one launch (start us, length us, event | category | flops | bytes accessed | tf_op | source)
XLA Modules:
  0.0 497.5 jit_solution(5874479406832994217)
XLA Ops:
  7.2 0.7 all-gather.5.cloned.1.call-update
  8.0 0.7 all-gather.7.cloned.1.call-update
  8.7 0.7 mul.75
  9.4 0.8 compare_reduce_fusion
  10.2 0.5 convolution_compare_fusion
  10.9 83.5 %all-gather.5.cloned.1.call-done = bf16[1,1,256,3072]{2,3,1,0:T(8,128)(2,1)} async-done(((bf16[1,1,256,192]{2,3,1,0:T(8,128)(2,1)}), bf16[1,1,256,3072]{2,3,1,0:T(8,128)(2,1)}) %all-gather.5.cloned.1.call-update) | async-done | bytes 1572880 | tf_op jit(solution)/shard_map/all_gather | solution.py:43
  94.4 1.7 copy.37
  96.1 0.4 fusion.10
  96.5 1.8 fusion.32
  98.3 0.9 fusion.21
  99.5 0.8 copy-done.1
  100.3 0.7 fusion.42
  101.0 1.3 fusion.31
  102.3 66.8 %all-gather.7.cloned.1.call-done = bf16[1,1,256,3072]{2,3,1,0:T(8,128)(2,1)} async-done(((bf16[1,1,256,192]{2,3,1,0:T(8,128)(2,1)}), bf16[1,1,256,3072]{2,3,1,0:T(8,128)(2,1)}) %all-gather.7.cloned.1.call-update) | async-done | bytes 1572880 | tf_op jit(solution)/shard_map/all_gather | solution.py:44
  169.1 2.5 fusion.24
  172.7 2.3 fusion.15
  174.9 4.8 convolution_add_fusion.1
  179.7 5.4 %fusion.9 = (f32[3072]{0:T(1024)S(1)}, f32[256]{0:T(256)S(1)}, f32[256,3072]{1,0:T(8,128)}) fusion(bf16[1,1,256,3072]{3,2,1,0:T(8,128)(2,1)S(1)} %copy.37, f32[256]{0:T(256)S(1)} %copy-done.13, f32[3072]{0:T(1024)S(1)} %bitcast.151, f32[256,3072]{1,0:T(8,128)} %convolution_add_fusion.1, bf16[1,3072,128]{2,1,0:T(8,128)(2,1)} %param.17, ...), kind=kOutput, calls=%fused_computation.14 | convolution fusion | flops 241726208 | bytes 9402368 | tf_op jit(solution)/shard_map/dot_general | solution.py:118
  185.2 3.9 fusion.8
  189.1 2.6 copy.59
  192.1 1.1 copy-done.4
  193.2 1.9 convolution_convert_fusion
  195.3 68.5 %reduce-scatter.7.cloned.1.call-done = bf16[192,256]{1,0:T(8,128)(2,1)} async-done(((bf16[3072,256]{1,0:T(8,128)(2,1)}), bf16[192,256]{1,0:T(8,128)(2,1)}) %reduce-scatter.7.cloned.1.call-update) | async-done | bytes 98320
  263.8 1.0 copy.60
  264.8 1.9 collective-permute-start.1
  266.7 73.5 %reduce-scatter.5.cloned.1.call-done = bf16[256,192]{0,1:T(8,128)(2,1)} async-done(((bf16[256,3072]{0,1:T(8,128)(2,1)}), bf16[256,192]{0,1:T(8,128)(2,1)}) %reduce-scatter.5.cloned.1.call-update) | async-done | bytes 98320 | tf_op jit(solution)/shard_map/reduce_scatter | solution.py:87
  340.2 0.9 fusion.48
  341.2 1.9 collective-permute-start
  343.1 145.9 %psum.7 = f32[3072]{0:T(1024)S(1)} all-reduce(f32[3072]{0:T(1024)S(1)} %get-tuple-element.12), channel_id=1, replica_groups=mesh['section'=32,'mp'=16,'dp'=2] {'mp','dp'}, use_global_device_ids=true, to_apply=%region_9.10 | all-reduce | flops 3072 | bytes 24576 | tf_op jit(solution)/shard_map/psum | solution.py:131
  489.0 0.6 dynamic_slice.3
  489.6 0.7 copy.48
  490.3 0.6 copy.62
  (49 shorter events, 2.1 us)
Async XLA Ops:
  7.2 91.1 %copy-start = (bf16[1,3072,256]{2,1,0:T(8,128)(2,1)S(1)}, bf16[1,3072,256]{2,1,0:T(8,128)(2,1)}, u32[]{:S(2)}) copy-start(bf16[1,3072,256]{2,1,0:T(8,128)(2,1)} %param.15) | copy-start | bytes 4718596
  7.2 87.2 %all-gather.5.cloned.1.call-start = ((), (), s32[]{:S(2)}) async-start(), calls=%async_computation.3 | async-start | bytes 1671168 | tf_op jit(solution)/shard_map/all_gather | solution.py:43
  7.9 161.2 %all-gather.7.cloned.1.call-start = ((), (), s32[]{:S(2)}) async-start(), calls=%async_computation.4 | async-start | bytes 1671168 | tf_op jit(solution)/shard_map/all_gather | solution.py:44
  8.7 255.1 %reduce-scatter.7.cloned.1.call-start = ((), (), s32[]{:S(2)}) async-start(), calls=%async_computation.5 | async-start | bytes 1671168
  96.5 4.5 copy-start.12
  98.3 2.7 copy-start.5
  99.2 72.4 %copy-start.6 = (bf16[256,256]{0,1:T(8,128)(2,1)}, bf16[256,256]{0,1:T(8,128)(2,1)S(1)}, u32[]{:S(2)}) copy-start(bf16[256,256]{0,1:T(8,128)(2,1)S(1)} %fusion.21) | copy-start | bytes 393220
  99.5 0.8 copy-start.1
  169.1 2.5 copy-start.2
  169.1 2.6 copy-start.10
  169.1 2.6 copy-start.14
  171.6 0.6 copy-start.7
  174.9 4.8 copy-start.11
  174.9 4.8 copy-start.13
  189.1 2.7 copy-start.3
  189.1 2.7 copy-start.15
  191.7 3.4 copy-start.8
  191.7 148.5 %reduce-scatter.5.cloned.1.call-start = ((), (), s32[]{:S(2)}) async-start(), calls=%async_computation.2 | async-start | bytes 1671168 | tf_op jit(solution)/shard_map/reduce_scatter | solution.py:87
  191.8 1.4 copy-start.4
  192.1 148.1 %copy-start.9 = (bf16[1,1,256,192]{2,3,1,0:T(8,128)(2,1)S(1)}, bf16[1,1,256,192]{2,3,1,0:T(8,128)(2,1)}, u32[]{:S(2)}) copy-start(bf16[1,1,256,192]{2,3,1,0:T(8,128)(2,1)} %param.10) | copy-start | bytes 294916
  264.8 224.8 %collective-permute-start.1 = (bf16[256,192]{1,0:T(8,128)(2,1)S(1)}, bf16[256,192]{1,0:T(8,128)(2,1)S(1)}, u32[]{:S(2)}, u32[]{:S(2)}) collective-permute-start(bf16[256,192]{1,0:T(8,128)(2,1)S(1)} %fusion.44), channel_id=1, source_target_pairs={{32,0},{64,32},{96,64},{128,96},{160,128},{192,160},{224,192},{256... | collective-permute-start | bytes 294920 | tf_op jit(solution)/shard_map/ppermute | solution.py:14
  341.2 149.2 %collective-permute-start = (bf16[256,192]{0,1:T(8,128)(2,1)S(1)}, bf16[256,192]{0,1:T(8,128)(2,1)S(1)}, u32[]{:S(2)}, u32[]{:S(2)}) collective-permute-start(bf16[256,192]{0,1:T(8,128)(2,1)S(1)} %fusion.48), channel_id=1, source_target_pairs={{32,0},{64,32},{96,64},{128,96},{160,128},{192,160},{224,192},{256... | collective-permute-start | bytes 294920 | tf_op jit(solution)/shard_map/ppermute | solution.py:14
Sparse Core Ops, SparseCore 0:
  10.7 83.6 all-gather.4
  97.0 72.0 all-gather.6
  191.9 71.8 reduce-scatter.6
  267.4 72.7 reduce-scatter.4
where the time goes:
time: 498 us
  waiting for transfers between devices  294 us (59%)
  blocking collectives  146 us (29%)
  matrix products  22.4 us (4%)
  between operations  14 us (3%)
  local copies, waits for them, and re-layouts  9.97 us (2%)
  other arithmetic  7.63 us (2%)
    psum x1, blocking collectives, local(): lax.psum(jnp.sum(normed_grad * unit_rows, axis=0), ('mp', 'dp'))  146 us
    all_gather x1, waiting for transfers between devices, local(): lax.all_gather(upper_out[0, 0], 'mp', axis=1, tiled=True)  83.5 us
    reduce_scatter x1, waiting for transfers between devices, local(): lax.psum_scatter(out_term.astype(jnp.bfloat16), 'mp', scatter_dimension=1...  73.5 us
    unnamed x5, waiting for transfers between devices  69.9 us
    all_gather x1, waiting for transfers between devices, local(): lax.all_gather(lower_grad[0, 0], 'mp', axis=1, tiled=True)  66.8 us
  transfers between devices with their start and end apart: 6, of which 4 were waited for; matrix products, arithmetic and copies ran while one was open for 3% of the time, Pallas kernels for 0%

commit v1 on v0

--- a/solution.py
+++ b/solution.py
@@ -12,6 +12,68 @@
     length = lax.axis_size(axis)
     pairs = [(i, i + by) for i in range(length) if 0 <= i + by < length]
     return lax.ppermute(x, axis, pairs)
+
+
+def shift(x, axis, by):
+    length = lax.axis_size(axis)
+    return lax.ppermute(x, axis, [(i, (i + by) % length) for i in range(length)])
+
+
+def ring_gather(chunk, axis):
+    n = lax.axis_size(axis)
+    me = lax.axis_index(axis)
+    forward_steps = n // 2
+    backward_steps = n - 1 - forward_steps
+    relative = [None] * n
+    relative[0] = chunk
+    forward = chunk
+    backward = chunk
+    for step in range(forward_steps):
+        forward = shift(forward, axis, 1)
+        relative[n - 1 - step] = forward
+        if step < backward_steps:
+            backward = shift(backward, axis, -1)
+            relative[step + 1] = backward
+    stacked = jnp.stack(relative)
+    return jnp.roll(stacked, me, axis=0)
+
+
+def ring_reduce_scatter(parts, axis, extra=None):
+    n = lax.axis_size(axis)
+    me = lax.axis_index(axis)
+    forward_steps = n // 2
+    backward_steps = n - 1 - forward_steps
+
+    def pick(stack, offset):
+        return lax.dynamic_index_in_dim(stack, (me + offset) % n, 0, keepdims=False)
+
+    def part_at(offset):
+        head = pick(parts, offset).astype(jnp.float32)
+        if extra is None:
+            return (head,)
+        return (head, pick(extra, offset))
+
+    def wire(values):
+        return (values[0].astype(jnp.bfloat16),) + tuple(values[1:])
+
+    def add(received, offset):
+        own = part_at(offset)
+        return tuple(r.astype(jnp.float32) + o for r, o in zip(received, own))
+
+    forward = wire(part_at(forward_steps))
+    backward = wire(part_at(n - backward_steps))
+    for step in range(forward_steps):
+        forward = shift(forward, axis, 1)
+        if step < forward_steps - 1:
+            forward = wire(add(forward, forward_steps - 1 - step))
+        if step < backward_steps:
+            backward = shift(backward, axis, -1)
+            if step < backward_steps - 1:
+                backward = wire(add(backward, n - backward_steps + 1 + step))
+    own = part_at(0)
+    return tuple(
+        o + f.astype(jnp.float32) + b.astype(jnp.float32) for o, f, b in zip(own, forward, backward)
+    )
 
 
 def token_mask(key_lists, length):
@@ -37,12 +99,12 @@
     output_weight,
     key_lists,
 ):
-    feature_count = upper_out.shape[3]
-    mp_index = lax.axis_index("mp")
-    whole_upper, whole_grad = (
-        lax.all_gather(upper_out[0, 0], "mp", axis=1, tiled=True),
-        lax.all_gather(lower_grad[0, 0], "mp", axis=1, tiled=True),
-    )
+    n_mp = lax.axis_size("mp")
+    share = upper_out.shape[3]
+    gathered = ring_gather(jnp.stack([upper_out[0, 0], lower_grad[0, 0]]), "mp")
+    length = gathered.shape[2]
+    whole_upper = jnp.transpose(gathered[:, 0], (1, 0, 2)).reshape(length, n_mp * share)
+    whole_grad = jnp.transpose(gathered[:, 1], (1, 0, 2)).reshape(length, n_mp * share)
     stream = whole_upper.astype(jnp.float32)
     inverse = lax.rsqrt(jnp.mean(stream * stream, axis=1, keepdims=True) + 1e-06)
     unit_rows = stream * inverse
@@ -52,7 +114,6 @@
     w_key = key_weight[0]
     w_value = value_projection[0]
     w_output = output_weight[0]
-    length = normed.shape[0]
     kv_heads = w_key.shape[1] // HEAD_SIZE
     group_width = w_query.shape[1] // HEAD_SIZE // kv_heads
     query_head_split = jnp.dot(normed, w_query, preferred_element_type=jnp.float32).astype(
@@ -83,10 +144,13 @@
         "jgqk,kjd->qjgd", probability_half, value_head_split, preferred_element_type=jnp.float32
     )
     attended = attended.astype(jnp.bfloat16).reshape(length, -1)
-    out_term = jnp.dot(attended, w_output, preferred_element_type=jnp.float32)
-    out_share = lax.psum_scatter(
-        out_term.astype(jnp.bfloat16), "mp", scatter_dimension=1, tiled=True
-    ).astype(jnp.float32)
+    out_parts = jnp.einsum(
+        "lc,cmf->mlf",
+        attended,
+        w_output.reshape(w_output.shape[0], n_mp, share),
+        preferred_element_type=jnp.float32,
+    ).astype(jnp.bfloat16)
+    (out_share,) = ring_reduce_scatter(out_parts, "mp")
     rebuilt = (lower_out[0, 0].astype(jnp.float32) - out_share).astype(jnp.bfloat16)
     attention_gradient = jnp.dot(whole_grad, w_output.T, preferred_element_type=jnp.float32).astype(
         jnp.bfloat16
@@ -118,18 +182,14 @@
     normed_grad = normed_grad + jnp.dot(
         value_gradient, w_value.T, preferred_element_type=jnp.float32
     )
-    upper_rows = upper_grad[0, 0].astype(jnp.float32)
     weighted = gain_rows * normed_grad
     row_stat = jnp.mean(unit_rows * weighted, axis=1, keepdims=True)
-    grad_share = lax.psum_scatter(
-        ((weighted - unit_rows * row_stat) * inverse).astype(jnp.bfloat16),
-        "mp",
-        scatter_dimension=1,
-        tiled=True,
-    ).astype(jnp.float32)
-    lower_rows = upper_rows + grad_share
-    gain_whole = lax.psum(jnp.sum(normed_grad * unit_rows, axis=0), ("mp", "dp"))
-    gain_grad = lax.dynamic_slice_in_dim(gain_whole, mp_index * feature_count, feature_count, 0)
+    grad_parts = ((weighted - unit_rows * row_stat) * inverse).astype(jnp.bfloat16)
+    grad_parts = jnp.transpose(grad_parts.reshape(length, n_mp, share), (1, 0, 2))
+    gain_parts = jnp.sum(normed_grad * unit_rows, axis=0).reshape(n_mp, share)
+    grad_share, gain_share = ring_reduce_scatter(grad_parts, "mp", gain_parts)
+    lower_rows = upper_grad[0, 0].astype(jnp.float32) + grad_share
+    gain_grad = gain_share + shift(gain_share, "dp", 1)
     entering = lower_rows.astype(jnp.bfloat16)
     sent_lower, sent_grad = from_behind((rebuilt, entering), "section", -1)
     return (sent_lower[None, None], sent_grad[None, None], gain_grad[None])

time: 498 us -> 304 us (0.61)
  the two profiles are of different devices: /device:TPU:8 before, /device:TPU:1 now
where the time goes in v1:
time: 304 us; the launch traced here: 300 us
  starting transfers between devices  235 us (77%)
  waiting for transfers between devices  22 us (7%)
  matrix products  18.8 us (6%)
  other arithmetic  14.4 us (5%)
  local copies, waits for them, and re-layouts  7.6 us (2%)
    ppermute x61, starting transfers between devices, shift(): lax.ppermute(x, axis, [(i, (i + by) % length) for i in range(length)])  209 us
    ppermute x2, starting transfers between devices, from_behind(): return lax.ppermute(x, axis, pairs)  26.1 us
    ppermute x61, waiting for transfers between devices, shift(): lax.ppermute(x, axis, [(i, (i + by) % length) for i in range(length)])  21.9 us
  transfers between devices with their start and end apart: 63, of which 9 were waited for; matrix products, arithmetic and copies ran while one was open for 5% of the time, Pallas kernels for 0%

profile of v1, /device:TPU:1, one launch (start us, length us, event | category | flops | bytes accessed | tf_op | source)
XLA Modules:
  0.0 299.8 jit_solution(16645139166076377997)
XLA Ops:
  1.8 18.8 %collective-permute-start = (bf16[2,256,192]{1,2,0:T(8,128)(2,1)S(1)}, bf16[2,256,192]{1,2,0:T(8,128)(2,1)S(1)}, u32[]{:S(2)}, u32[]{:S(2)}) collective-permute-start(bf16[2,256,192]{1,2,0:T(8,128)(2,1)S(1)} %pad_maximum_fusion), channel_id=1, source_target_pairs={{0,30},{2,0},{4,2},{6,4},{8,6},{10,8},{12,10},{14,12},{16,14},{18,... | collective-permute-start | bytes 589832 | tf_op jit(solution)/shard_map/ppermute | solution.py:19
  26.7 4.6 %collective-permute-start.1 = (bf16[2,256,192]{1,2,0:T(8,128)(2,1)S(1)}, bf16[2,256,192]{1,2,0:T(8,128)(2,1)S(1)}, u32[]{:S(2)}, u32[]{:S(2)}) collective-permute-start(bf16[2,256,192]{1,2,0:T(8,128)(2,1)S(1)} %collective-permute-done), channel_id=1, source_target_pairs={{0,30},{2,0},{4,2},{6,4},{8,6},{10,8},{12,10},{14,12},{16,14},{18,... | collective-permute-start | bytes 589832 | tf_op jit(solution)/shard_map/ppermute | solution.py:19
  34.2 5.3 %collective-permute-start.2 = (bf16[2,256,192]{1,2,0:T(8,128)(2,1)S(1)}, bf16[2,256,192]{1,2,0:T(8,128)(2,1)S(1)}, u32[]{:S(2)}, u32[]{:S(2)}) collective-permute-start(bf16[2,256,192]{1,2,0:T(8,128)(2,1)S(1)} %collective-permute-done.1), channel_id=1, source_target_pairs={{0,30},{2,0},{4,2},{6,4},{8,6},{10,8},{12,10},{14,12},{16,14},{18,... | collective-permute-start | bytes 589832 | tf_op jit(solution)/shard_map/ppermute | solution.py:19
  42.2 5.0 %collective-permute-start.3 = (bf16[2,256,192]{1,2,0:T(8,128)(2,1)S(1)}, bf16[2,256,192]{1,2,0:T(8,128)(2,1)S(1)}, u32[]{:S(2)}, u32[]{:S(2)}) collective-permute-start(bf16[2,256,192]{1,2,0:T(8,128)(2,1)S(1)} %collective-permute-done.2), channel_id=1, source_target_pairs={{0,30},{2,0},{4,2},{6,4},{8,6},{10,8},{12,10},{14,12},{16,14},{18,... | collective-permute-start | bytes 589832 | tf_op jit(solution)/shard_map/ppermute | solution.py:19
  49.8 5.0 %collective-permute-start.4 = (bf16[2,256,192]{1,2,0:T(8,128)(2,1)S(1)}, bf16[2,256,192]{1,2,0:T(8,128)(2,1)S(1)}, u32[]{:S(2)}, u32[]{:S(2)}) collective-permute-start(bf16[2,256,192]{1,2,0:T(8,128)(2,1)S(1)} %collective-permute-done.3), channel_id=1, source_target_pairs={{0,30},{2,0},{4,2},{6,4},{8,6},{10,8},{12,10},{14,12},{16,14},{18,... | collective-permute-start | bytes 589832 | tf_op jit(solution)/shard_map/ppermute | solution.py:19
  57.4 5.0 %collective-permute-start.5 = (bf16[2,256,192]{1,2,0:T(8,128)(2,1)S(1)}, bf16[2,256,192]{1,2,0:T(8,128)(2,1)S(1)}, u32[]{:S(2)}, u32[]{:S(2)}) collective-permute-start(bf16[2,256,192]{1,2,0:T(8,128)(2,1)S(1)} %collective-permute-done.4), channel_id=1, source_target_pairs={{0,30},{2,0},{4,2},{6,4},{8,6},{10,8},{12,10},{14,12},{16,14},{18,... | collective-permute-start | bytes 589832 | tf_op jit(solution)/shard_map/ppermute | solution.py:19
  65.0 5.0 %collective-permute-start.6 = (bf16[2,256,192]{1,2,0:T(8,128)(2,1)S(1)}, bf16[2,256,192]{1,2,0:T(8,128)(2,1)S(1)}, u32[]{:S(2)}, u32[]{:S(2)}) collective-permute-start(bf16[2,256,192]{1,2,0:T(8,128)(2,1)S(1)} %collective-permute-done.5), channel_id=1, source_target_pairs={{0,30},{2,0},{4,2},{6,4},{8,6},{10,8},{12,10},{14,12},{16,14},{18,... | collective-permute-start | bytes 589832 | tf_op jit(solution)/shard_map/ppermute | solution.py:19
  72.0 6.5 %collective-permute-done.13 = bf16[2,256,192]{1,2,0:T(8,128)(2,1)S(1)} collective-permute-done((bf16[2,256,192]{1,2,0:T(8,128)(2,1)S(1)}, bf16[2,256,192]{1,2,0:T(8,128)(2,1)S(1)}, u32[]{:S(2)}, u32[]{:S(2)}) %collective-permute-start.13) | collective-permute-done | bytes 196640 | tf_op jit(solution)/shard_map/ppermute | solution.py:19
  80.4 7.8 %collective-permute-done.14 = bf16[2,256,192]{1,2,0:T(8,128)(2,1)S(1)} collective-permute-done((bf16[2,256,192]{1,2,0:T(8,128)(2,1)S(1)}, bf16[2,256,192]{1,2,0:T(8,128)(2,1)S(1)}, u32[]{:S(2)}, u32[]{:S(2)}) %collective-permute-start.14) | collective-permute-done | bytes 196640 | tf_op jit(solution)/shard_map/ppermute | solution.py:19
  106.0 5.9 %multiply_reduce_fusion = (f32[3072]{0:T(1024)S(1)}, f32[256]{0:T(256)S(1)}, f32[256,3072]{1,0:T(8,128)}) fusion(f32[256,3072]{1,0:T(8,128)} %copy.125, f32[256]{0:T(256)S(1)} %copy-done.12, f32[3072]{0:T(1024)S(1)} %bitcast.383, f32[256,3072]{1,0:T(8,128)} %convolution_add_fusion.1, bf16[1,3072,128]{2,1,0:T(8,128)(2,1)S(1)} %copy-done.4, ...), kind=kOutput, calls=%fused_computation.2 | convolution fusion | flops 240939776 | bytes 10975232 | tf_op jit(solution)/shard_map/dot_general | solution.py:182
  114.0 4.6 %collective-permute-start.55 = (f32[192]{0:T(256)S(1)}, f32[192]{0:T(256)S(1)}, u32[]{:S(2)}, u32[]{:S(2)}) collective-permute-start(f32[192]{0:T(256)S(1)} %bitcast.401), channel_id=1, source_target_pairs={{0,30},{2,0},{4,2},{6,4},{8,6},{10,8},{12,10},{14,12},{16,14},{18,... | collective-permute-start | bytes 2312 | tf_op jit(solution)/shard_map/ppermute | solution.py:19
  120.5 4.6 %collective-permute-start.56 = (f32[192]{0:T(256)S(1)}, f32[192]{0:T(256)S(1)}, u32[]{:S(2)}, u32[]{:S(2)}) collective-permute-start(f32[192]{0:T(256)S(1)} %add.500), channel_id=1, source_target_pairs={{0,30},{2,0},{4,2},{6,4},{8,6},{10,8},{12,10},{14,12},{16,14},{18,... | collective-permute-start | bytes 2312 | tf_op jit(solution)/shard_map/ppermute | solution.py:19
  127.1 5.0 %multiply_convert_fusion = bf16[256,3072]{1,0:T(8,128)(2,1)} fusion(f32[256,3072]{1,0:T(8,128)} %get-tuple-element.55, f32[256,3072]{1,0:T(8,128)} %copy.125, f32[256]{0:T(256)S(1)} %broadcast_multiply_fusion, f32[256]{0:T(256)S(1)} %copy-done.12, f32[3072]{0:T(1024)S(1)} %bitcast.384), kind=kLoop, calls=%fused_computation.3 | loop fusion | flops 4718592 | bytes 7878656 | tf_op jit(solution)/shard_map/convert_element_type | solution.py:187
  132.0 4.6 %collective-permute-start.57 = (f32[192]{0:T(256)S(1)}, f32[192]{0:T(256)S(1)}, u32[]{:S(2)}, u32[]{:S(2)}) collective-permute-start(f32[192]{0:T(256)S(1)} %add.501), channel_id=1, source_target_pairs={{0,30},{2,0},{4,2},{6,4},{8,6},{10,8},{12,10},{14,12},{16,14},{18,... | collective-permute-start | bytes 2312 | tf_op jit(solution)/shard_map/ppermute | solution.py:19
  140.6 4.8 %collective-permute-start.58 = (f32[192]{0:T(256)S(1)}, f32[192]{0:T(256)S(1)}, u32[]{:S(2)}, u32[]{:S(2)}) collective-permute-start(f32[192]{0:T(256)S(1)} %add.502), channel_id=1, source_target_pairs={{0,30},{2,0},{4,2},{6,4},{8,6},{10,8},{12,10},{14,12},{16,14},{18,... | collective-permute-start | bytes 2312 | tf_op jit(solution)/shard_map/ppermute | solution.py:19
  149.2 4.6 %collective-permute-start.39 = (bf16[256,192]{0,1:T(8,128)(2,1)S(1)}, bf16[256,192]{0,1:T(8,128)(2,1)S(1)}, u32[]{:S(2)}, u32[]{:S(2)}) collective-permute-start(bf16[256,192]{0,1:T(8,128)(2,1)S(1)} %get-tuple-element.20), channel_id=1, source_target_pairs={{0,30},{2,0},{4,2},{6,4},{8,6},{10,8},{12,10},{14,12},{16,14},{18,... | collective-permute-start | bytes 294920 | tf_op jit(solution)/shard_map/ppermute | solution.py:19
  161.5 4.6 %collective-permute-start.60 = (f32[192]{0:T(256)S(1)}, f32[192]{0:T(256)S(1)}, u32[]{:S(2)}, u32[]{:S(2)}) collective-permute-start(f32[192]{0:T(256)S(1)} %add.504), channel_id=1, source_target_pairs={{0,30},{2,0},{4,2},{6,4},{8,6},{10,8},{12,10},{14,12},{16,14},{18,... | collective-permute-start | bytes 2312 | tf_op jit(solution)/shard_map/ppermute | solution.py:19
  170.0 4.6 %collective-permute-start.23 = (bf16[256,192]{0,1:T(8,128)(2,1)S(1)}, bf16[256,192]{0,1:T(8,128)(2,1)S(1)}, u32[]{:S(2)}, u32[]{:S(2)}) collective-permute-start(bf16[256,192]{0,1:T(8,128)(2,1)S(1)} %get-tuple-element.34), channel_id=1, source_target_pairs={{0,30},{2,0},{4,2},{6,4},{8,6},{10,8},{12,10},{14,12},{16,14},{18,... | collective-permute-start | bytes 294920 | tf_op jit(solution)/shard_map/ppermute | solution.py:19
  188.5 4.6 %collective-permute-start.40 = (bf16[256,192]{0,1:T(8,128)(2,1)S(1)}, bf16[256,192]{0,1:T(8,128)(2,1)S(1)}, u32[]{:S(2)}, u32[]{:S(2)}) collective-permute-start(bf16[256,192]{0,1:T(8,128)(2,1)S(1)} %get-tuple-element.18), channel_id=1, source_target_pairs={{0,30},{2,0},{4,2},{6,4},{8,6},{10,8},{12,10},{14,12},{16,14},{18,... | collective-permute-start | bytes 294920 | tf_op jit(solution)/shard_map/ppermute | solution.py:19
  195.1 4.6 %collective-permute-start.24 = (bf16[256,192]{0,1:T(8,128)(2,1)S(1)}, bf16[256,192]{0,1:T(8,128)(2,1)S(1)}, u32[]{:S(2)}, u32[]{:S(2)}) collective-permute-start(bf16[256,192]{0,1:T(8,128)(2,1)S(1)} %get-tuple-element.32), channel_id=1, source_target_pairs={{0,30},{2,0},{4,2},{6,4},{8,6},{10,8},{12,10},{14,12},{16,14},{18,... | collective-permute-start | bytes 294920 | tf_op jit(solution)/shard_map/ppermute | solution.py:19
  201.7 4.6 %collective-permute-start.41 = (bf16[256,192]{0,1:T(8,128)(2,1)S(1)}, bf16[256,192]{0,1:T(8,128)(2,1)S(1)}, u32[]{:S(2)}, u32[]{:S(2)}) collective-permute-start(bf16[256,192]{0,1:T(8,128)(2,1)S(1)} %get-tuple-element.16), channel_id=1, source_target_pairs={{0,30},{2,0},{4,2},{6,4},{8,6},{10,8},{12,10},{14,12},{16,14},{18,... | collective-permute-start | bytes 294920 | tf_op jit(solution)/shard_map/ppermute | solution.py:19
  208.3 4.6 %collective-permute-start.25 = (bf16[256,192]{0,1:T(8,128)(2,1)S(1)}, bf16[256,192]{0,1:T(8,128)(2,1)S(1)}, u32[]{:S(2)}, u32[]{:S(2)}) collective-permute-start(bf16[256,192]{0,1:T(8,128)(2,1)S(1)} %get-tuple-element.30), channel_id=1, source_target_pairs={{0,30},{2,0},{4,2},{6,4},{8,6},{10,8},{12,10},{14,12},{16,14},{18,... | collective-permute-start | bytes 294920 | tf_op jit(solution)/shard_map/ppermute | solution.py:19
  214.9 4.6 %collective-permute-start.42 = (bf16[256,192]{0,1:T(8,128)(2,1)S(1)}, bf16[256,192]{0,1:T(8,128)(2,1)S(1)}, u32[]{:S(2)}, u32[]{:S(2)}) collective-permute-start(bf16[256,192]{0,1:T(8,128)(2,1)S(1)} %get-tuple-element.14), channel_id=1, source_target_pairs={{0,30},{2,0},{4,2},{6,4},{8,6},{10,8},{12,10},{14,12},{16,14},{18,... | collective-permute-start | bytes 294920 | tf_op jit(solution)/shard_map/ppermute | solution.py:19
  221.5 4.6 %collective-permute-start.26 = (bf16[256,192]{0,1:T(8,128)(2,1)S(1)}, bf16[256,192]{0,1:T(8,128)(2,1)S(1)}, u32[]{:S(2)}, u32[]{:S(2)}) collective-permute-start(bf16[256,192]{0,1:T(8,128)(2,1)S(1)} %get-tuple-element.28), channel_id=1, source_target_pairs={{0,30},{2,0},{4,2},{6,4},{8,6},{10,8},{12,10},{14,12},{16,14},{18,... | collective-permute-start | bytes 294920 | tf_op jit(solution)/shard_map/ppermute | solution.py:19
  228.1 4.6 %collective-permute-start.43 = (bf16[256,192]{0,1:T(8,128)(2,1)S(1)}, bf16[256,192]{0,1:T(8,128)(2,1)S(1)}, u32[]{:S(2)}, u32[]{:S(2)}) collective-permute-start(bf16[256,192]{0,1:T(8,128)(2,1)S(1)} %get-tuple-element.12), channel_id=1, source_target_pairs={{0,30},{2,0},{4,2},{6,4},{8,6},{10,8},{12,10},{14,12},{16,14},{18,... | collective-permute-start | bytes 294920 | tf_op jit(solution)/shard_map/ppermute | solution.py:19
  234.7 4.6 %collective-permute-start.27 = (bf16[256,192]{0,1:T(8,128)(2,1)S(1)}, bf16[256,192]{0,1:T(8,128)(2,1)S(1)}, u32[]{:S(2)}, u32[]{:S(2)}) collective-permute-start(bf16[256,192]{0,1:T(8,128)(2,1)S(1)} %get-tuple-element.26), channel_id=1, source_target_pairs={{0,30},{2,0},{4,2},{6,4},{8,6},{10,8},{12,10},{14,12},{16,14},{18,... | collective-permute-start | bytes 294920 | tf_op jit(solution)/shard_map/ppermute | solution.py:19
  241.3 4.6 %collective-permute-start.44 = (bf16[256,192]{0,1:T(8,128)(2,1)S(1)}, bf16[256,192]{0,1:T(8,128)(2,1)S(1)}, u32[]{:S(2)}, u32[]{:S(2)}) collective-permute-start(bf16[256,192]{0,1:T(8,128)(2,1)S(1)} %get-tuple-element.10), channel_id=1, source_target_pairs={{0,30},{2,0},{4,2},{6,4},{8,6},{10,8},{12,10},{14,12},{16,14},{18,... | collective-permute-start | bytes 294920 | tf_op jit(solution)/shard_map/ppermute | solution.py:19
  247.9 4.6 %collective-permute-start.28 = (bf16[256,192]{0,1:T(8,128)(2,1)S(1)}, bf16[256,192]{0,1:T(8,128)(2,1)S(1)}, u32[]{:S(2)}, u32[]{:S(2)}) collective-permute-start(bf16[256,192]{0,1:T(8,128)(2,1)S(1)} %get-tuple-element.24), channel_id=1, source_target_pairs={{0,30},{2,0},{4,2},{6,4},{8,6},{10,8},{12,10},{14,12},{16,14},{18,... | collective-permute-start | bytes 294920 | tf_op jit(solution)/shard_map/ppermute | solution.py:19
  254.5 4.6 %collective-permute-start.45 = (bf16[256,192]{0,1:T(8,128)(2,1)S(1)}, bf16[256,192]{0,1:T(8,128)(2,1)S(1)}, u32[]{:S(2)}, u32[]{:S(2)}) collective-permute-start(bf16[256,192]{0,1:T(8,128)(2,1)S(1)} %get-tuple-element.8), channel_id=1, source_target_pairs={{0,30},{2,0},{4,2},{6,4},{8,6},{10,8},{12,10},{14,12},{16,14},{18,... | collective-permute-start | bytes 294920 | tf_op jit(solution)/shard_map/ppermute | solution.py:19
  261.1 4.6 %collective-permute-start.29 = (bf16[256,192]{0,1:T(8,128)(2,1)S(1)}, bf16[256,192]{0,1:T(8,128)(2,1)S(1)}, u32[]{:S(2)}, u32[]{:S(2)}) collective-permute-start(bf16[256,192]{0,1:T(8,128)(2,1)S(1)} %get-tuple-element.22), channel_id=1, source_target_pairs={{0,30},{2,0},{4,2},{6,4},{8,6},{10,8},{12,10},{14,12},{16,14},{18,... | collective-permute-start | bytes 294920 | tf_op jit(solution)/shard_map/ppermute | solution.py:19
  265.8 24.0 %collective-permute-start.46 = (bf16[256,192]{0,1:T(8,128)(2,1)S(1)}, bf16[256,192]{0,1:T(8,128)(2,1)S(1)}, u32[]{:S(2)}, u32[]{:S(2)}) collective-permute-start(bf16[256,192]{0,1:T(8,128)(2,1)S(1)} %fusion.50), channel_id=1, source_target_pairs={{32,0},{64,32},{96,64},{128,96},{160,128},{192,160},{224,192},{256... | collective-permute-start | bytes 294920 | tf_op jit(solution)/shard_map/ppermute | solution.py:14
  292.0 4.6 %collective-permute-start.62 = (f32[192]{0:T(256)S(1)}, f32[192]{0:T(256)S(1)}, u32[]{:S(2)}, u32[]{:S(2)}) collective-permute-start(f32[192]{0:T(256)S(1)} %add_add_fusion), channel_id=1, source_target_pairs={{0,1},{1,0},{2,3},{3,2},{4,5},{5,4},{6,7},{7,6},{8,9},{9,8},{10,11... | collective-permute-start | bytes 2312 | tf_op jit(solution)/shard_map/ppermute | solution.py:19
  (220 shorter events, 107.8 us)
Async XLA Ops:
  1.8 25.0 %collective-permute-start = (bf16[2,256,192]{1,2,0:T(8,128)(2,1)S(1)}, bf16[2,256,192]{1,2,0:T(8,128)(2,1)S(1)}, u32[]{:S(2)}, u32[]{:S(2)}) collective-permute-start(bf16[2,256,192]{1,2,0:T(8,128)(2,1)S(1)} %pad_maximum_fusion), channel_id=1, source_target_pairs={{0,30},{2,0},{4,2},{6,4},{8,6},{10,8},{12,10},{14,12},{16,14},{18,... | collective-permute-start | bytes 589832 | tf_op jit(solution)/shard_map/ppermute | solution.py:19
  20.5 10.8 %collective-permute-start.7 = (bf16[2,256,192]{1,2,0:T(8,128)(2,1)S(1)}, bf16[2,256,192]{1,2,0:T(8,128)(2,1)S(1)}, u32[]{:S(2)}, u32[]{:S(2)}) collective-permute-start(bf16[2,256,192]{1,2,0:T(8,128)(2,1)S(1)} %pad_maximum_fusion), channel_id=1, source_target_pairs={{0,2},{2,4},{4,6},{6,8},{8,10},{10,12},{12,14},{14,16},{16,18},{18... | collective-permute-start | bytes 589832 | tf_op jit(solution)/shard_map/ppermute | solution.py:19
  65.0 15.4 %collective-permute-start.6 = (bf16[2,256,192]{1,2,0:T(8,128)(2,1)S(1)}, bf16[2,256,192]{1,2,0:T(8,128)(2,1)S(1)}, u32[]{:S(2)}, u32[]{:S(2)}) collective-permute-start(bf16[2,256,192]{1,2,0:T(8,128)(2,1)S(1)} %collective-permute-done.5), channel_id=1, source_target_pairs={{0,30},{2,0},{4,2},{6,4},{8,6},{10,8},{12,10},{14,12},{16,14},{18,... | collective-permute-start | bytes 589832 | tf_op jit(solution)/shard_map/ppermute | solution.py:19
  78.5 9.7 %collective-permute-start.14 = (bf16[2,256,192]{1,2,0:T(8,128)(2,1)S(1)}, bf16[2,256,192]{1,2,0:T(8,128)(2,1)S(1)}, u32[]{:S(2)}, u32[]{:S(2)}) collective-permute-start(bf16[2,256,192]{1,2,0:T(8,128)(2,1)S(1)} %collective-permute-done.13), channel_id=1, source_target_pairs={{0,2},{2,4},{4,6},{6,8},{8,10},{10,12},{12,14},{14,16},{16,18},{18... | collective-permute-start | bytes 589832 | tf_op jit(solution)/shard_map/ppermute | solution.py:19
  120.5 11.5 %collective-permute-start.56 = (f32[192]{0:T(256)S(1)}, f32[192]{0:T(256)S(1)}, u32[]{:S(2)}, u32[]{:S(2)}) collective-permute-start(f32[192]{0:T(256)S(1)} %add.500), channel_id=1, source_target_pairs={{0,30},{2,0},{4,2},{6,4},{8,6},{10,8},{12,10},{14,12},{16,14},{18,... | collective-permute-start | bytes 2312 | tf_op jit(solution)/shard_map/ppermute | solution.py:19
  125.1 11.5 %collective-permute-start.49 = (f32[192]{0:T(256)S(1)}, f32[192]{0:T(256)S(1)}, u32[]{:S(2)}, u32[]{:S(2)}) collective-permute-start(f32[192]{0:T(256)S(1)} %add.493), channel_id=1, source_target_pairs={{0,2},{2,4},{4,6},{6,8},{8,10},{10,12},{12,14},{14,16},{16,18},{18... | collective-permute-start | bytes 2312 | tf_op jit(solution)/shard_map/ppermute | solution.py:19
  136.6 8.7 %collective-permute-start.50 = (f32[192]{0:T(256)S(1)}, f32[192]{0:T(256)S(1)}, u32[]{:S(2)}, u32[]{:S(2)}) collective-permute-start(f32[192]{0:T(256)S(1)} %add.494), channel_id=1, source_target_pairs={{0,2},{2,4},{4,6},{6,8},{8,10},{10,12},{12,14},{14,16},{16,18},{18... | collective-permute-start | bytes 2312 | tf_op jit(solution)/shard_map/ppermute | solution.py:19
  140.6 13.3 %collective-permute-start.58 = (f32[192]{0:T(256)S(1)}, f32[192]{0:T(256)S(1)}, u32[]{:S(2)}, u32[]{:S(2)}) collective-permute-start(f32[192]{0:T(256)S(1)} %add.502), channel_id=1, source_target_pairs={{0,30},{2,0},{4,2},{6,4},{8,6},{10,8},{12,10},{14,12},{16,14},{18,... | collective-permute-start | bytes 2312 | tf_op jit(solution)/shard_map/ppermute | solution.py:19
  145.4 11.9 %collective-permute-start.51 = (f32[192]{0:T(256)S(1)}, f32[192]{0:T(256)S(1)}, u32[]{:S(2)}, u32[]{:S(2)}) collective-permute-start(f32[192]{0:T(256)S(1)} %add.495), channel_id=1, source_target_pairs={{0,2},{2,4},{4,6},{6,8},{8,10},{10,12},{12,14},{14,16},{16,18},{18... | collective-permute-start | bytes 2312 | tf_op jit(solution)/shard_map/ppermute | solution.py:19
  147.3 30.6 %collective-permute-start.31 = (bf16[256,192]{0,1:T(8,128)(2,1)S(1)}, bf16[256,192]{0,1:T(8,128)(2,1)S(1)}, u32[]{:S(2)}, u32[]{:S(2)}) collective-permute-start(bf16[256,192]{0,1:T(8,128)(2,1)S(1)} %get-tuple-element.19), channel_id=1, source_target_pairs={{0,2},{2,4},{4,6},{6,8},{8,10},{10,12},{12,14},{14,16},{16,18},{18... | collective-permute-start | bytes 294920 | tf_op jit(solution)/shard_map/ppermute | solution.py:19
  149.2 32.7 %collective-permute-start.39 = (bf16[256,192]{0,1:T(8,128)(2,1)S(1)}, bf16[256,192]{0,1:T(8,128)(2,1)S(1)}, u32[]{:S(2)}, u32[]{:S(2)}) collective-permute-start(bf16[256,192]{0,1:T(8,128)(2,1)S(1)} %get-tuple-element.20), channel_id=1, source_target_pairs={{0,30},{2,0},{4,2},{6,4},{8,6},{10,8},{12,10},{14,12},{16,14},{18,... | collective-permute-start | bytes 294920 | tf_op jit(solution)/shard_map/ppermute | solution.py:19
  157.2 8.8 %collective-permute-start.52 = (f32[192]{0:T(256)S(1)}, f32[192]{0:T(256)S(1)}, u32[]{:S(2)}, u32[]{:S(2)}) collective-permute-start(f32[192]{0:T(256)S(1)} %add.496), channel_id=1, source_target_pairs={{0,2},{2,4},{4,6},{6,8},{8,10},{10,12},{12,14},{14,16},{16,18},{18... | collective-permute-start | bytes 2312 | tf_op jit(solution)/shard_map/ppermute | solution.py:19
  168.0 11.9 %collective-permute-start.15 = (bf16[256,192]{0,1:T(8,128)(2,1)S(1)}, bf16[256,192]{0,1:T(8,128)(2,1)S(1)}, u32[]{:S(2)}, u32[]{:S(2)}) collective-permute-start(bf16[256,192]{0,1:T(8,128)(2,1)S(1)} %get-tuple-element.33), channel_id=1, source_target_pairs={{0,2},{2,4},{4,6},{6,8},{8,10},{10,12},{12,14},{14,16},{16,18},{18... | collective-permute-start | bytes 294920 | tf_op jit(solution)/shard_map/ppermute | solution.py:19
  170.0 18.5 %collective-permute-start.23 = (bf16[256,192]{0,1:T(8,128)(2,1)S(1)}, bf16[256,192]{0,1:T(8,128)(2,1)S(1)}, u32[]{:S(2)}, u32[]{:S(2)}) collective-permute-start(bf16[256,192]{0,1:T(8,128)(2,1)S(1)} %get-tuple-element.34), channel_id=1, source_target_pairs={{0,30},{2,0},{4,2},{6,4},{8,6},{10,8},{12,10},{14,12},{16,14},{18,... | collective-permute-start | bytes 294920 | tf_op jit(solution)/shard_map/ppermute | solution.py:19
  174.6 117.4 %collective-permute-start.61 = (f32[192]{0:T(256)S(1)}, f32[192]{0:T(256)S(1)}, u32[]{:S(2)}, u32[]{:S(2)}) collective-permute-start(f32[192]{0:T(256)S(1)} %add.505), channel_id=1, source_target_pairs={{0,30},{2,0},{4,2},{6,4},{8,6},{10,8},{12,10},{14,12},{16,14},{18,... | collective-permute-start | bytes 2312 | tf_op jit(solution)/shard_map/ppermute | solution.py:19
  178.0 114.0 %collective-permute-start.54 = (f32[192]{0:T(256)S(1)}, f32[192]{0:T(256)S(1)}, u32[]{:S(2)}, u32[]{:S(2)}) collective-permute-start(f32[192]{0:T(256)S(1)} %add.498), channel_id=1, source_target_pairs={{0,2},{2,4},{4,6},{6,8},{8,10},{10,12},{12,14},{14,16},{16,18},{18... | collective-permute-start | bytes 2312 | tf_op jit(solution)/shard_map/ppermute | solution.py:19
  181.9 11.2 %collective-permute-start.16 = (bf16[256,192]{0,1:T(8,128)(2,1)S(1)}, bf16[256,192]{0,1:T(8,128)(2,1)S(1)}, u32[]{:S(2)}, u32[]{:S(2)}) collective-permute-start(bf16[256,192]{0,1:T(8,128)(2,1)S(1)} %fusion.63), channel_id=1, source_target_pairs={{0,2},{2,4},{4,6},{6,8},{8,10},{10,12},{12,14},{14,16},{16,18},{18... | collective-permute-start | bytes 294920 | tf_op jit(solution)/shard_map/ppermute | solution.py:19
  188.5 11.2 %collective-permute-start.40 = (bf16[256,192]{0,1:T(8,128)(2,1)S(1)}, bf16[256,192]{0,1:T(8,128)(2,1)S(1)}, u32[]{:S(2)}, u32[]{:S(2)}) collective-permute-start(bf16[256,192]{0,1:T(8,128)(2,1)S(1)} %get-tuple-element.18), channel_id=1, source_target_pairs={{0,30},{2,0},{4,2},{6,4},{8,6},{10,8},{12,10},{14,12},{16,14},{18,... | collective-permute-start | bytes 294920 | tf_op jit(solution)/shard_map/ppermute | solution.py:19
  195.1 11.2 %collective-permute-start.24 = (bf16[256,192]{0,1:T(8,128)(2,1)S(1)}, bf16[256,192]{0,1:T(8,128)(2,1)S(1)}, u32[]{:S(2)}, u32[]{:S(2)}) collective-permute-start(bf16[256,192]{0,1:T(8,128)(2,1)S(1)} %get-tuple-element.32), channel_id=1, source_target_pairs={{0,30},{2,0},{4,2},{6,4},{8,6},{10,8},{12,10},{14,12},{16,14},{18,... | collective-permute-start | bytes 294920 | tf_op jit(solution)/shard_map/ppermute | solution.py:19
  201.7 11.2 %collective-permute-start.41 = (bf16[256,192]{0,1:T(8,128)(2,1)S(1)}, bf16[256,192]{0,1:T(8,128)(2,1)S(1)}, u32[]{:S(2)}, u32[]{:S(2)}) collective-permute-start(bf16[256,192]{0,1:T(8,128)(2,1)S(1)} %get-tuple-element.16), channel_id=1, source_target_pairs={{0,30},{2,0},{4,2},{6,4},{8,6},{10,8},{12,10},{14,12},{16,14},{18,... | collective-permute-start | bytes 294920 | tf_op jit(solution)/shard_map/ppermute | solution.py:19
  208.3 11.2 %collective-permute-start.25 = (bf16[256,192]{0,1:T(8,128)(2,1)S(1)}, bf16[256,192]{0,1:T(8,128)(2,1)S(1)}, u32[]{:S(2)}, u32[]{:S(2)}) collective-permute-start(bf16[256,192]{0,1:T(8,128)(2,1)S(1)} %get-tuple-element.30), channel_id=1, source_target_pairs={{0,30},{2,0},{4,2},{6,4},{8,6},{10,8},{12,10},{14,12},{16,14},{18,... | collective-permute-start | bytes 294920 | tf_op jit(solution)/shard_map/ppermute | solution.py:19
  214.9 11.2 %collective-permute-start.42 = (bf16[256,192]{0,1:T(8,128)(2,1)S(1)}, bf16[256,192]{0,1:T(8,128)(2,1)S(1)}, u32[]{:S(2)}, u32[]{:S(2)}) collective-permute-start(bf16[256,192]{0,1:T(8,128)(2,1)S(1)} %get-tuple-element.14), channel_id=1, source_target_pairs={{0,30},{2,0},{4,2},{6,4},{8,6},{10,8},{12,10},{14,12},{16,14},{18,... | collective-permute-start | bytes 294920 | tf_op jit(solution)/shard_map/ppermute | solution.py:19
  221.5 11.2 %collective-permute-start.26 = (bf16[256,192]{0,1:T(8,128)(2,1)S(1)}, bf16[256,192]{0,1:T(8,128)(2,1)S(1)}, u32[]{:S(2)}, u32[]{:S(2)}) collective-permute-start(bf16[256,192]{0,1:T(8,128)(2,1)S(1)} %get-tuple-element.28), channel_id=1, source_target_pairs={{0,30},{2,0},{4,2},{6,4},{8,6},{10,8},{12,10},{14,12},{16,14},{18,... | collective-permute-start | bytes 294920 | tf_op jit(solution)/shard_map/ppermute | solution.py:19
  228.1 11.2 %collective-permute-start.43 = (bf16[256,192]{0,1:T(8,128)(2,1)S(1)}, bf16[256,192]{0,1:T(8,128)(2,1)S(1)}, u32[]{:S(2)}, u32[]{:S(2)}) collective-permute-start(bf16[256,192]{0,1:T(8,128)(2,1)S(1)} %get-tuple-element.12), channel_id=1, source_target_pairs={{0,30},{2,0},{4,2},{6,4},{8,6},{10,8},{12,10},{14,12},{16,14},{18,... | collective-permute-start | bytes 294920 | tf_op jit(solution)/shard_map/ppermute | solution.py:19
  234.7 11.2 %collective-permute-start.27 = (bf16[256,192]{0,1:T(8,128)(2,1)S(1)}, bf16[256,192]{0,1:T(8,128)(2,1)S(1)}, u32[]{:S(2)}, u32[]{:S(2)}) collective-permute-start(bf16[256,192]{0,1:T(8,128)(2,1)S(1)} %get-tuple-element.26), channel_id=1, source_target_pairs={{0,30},{2,0},{4,2},{6,4},{8,6},{10,8},{12,10},{14,12},{16,14},{18,... | collective-permute-start | bytes 294920 | tf_op jit(solution)/shard_map/ppermute | solution.py:19
  241.3 11.2 %collective-permute-start.44 = (bf16[256,192]{0,1:T(8,128)(2,1)S(1)}, bf16[256,192]{0,1:T(8,128)(2,1)S(1)}, u32[]{:S(2)}, u32[]{:S(2)}) collective-permute-start(bf16[256,192]{0,1:T(8,128)(2,1)S(1)} %get-tuple-element.10), channel_id=1, source_target_pairs={{0,30},{2,0},{4,2},{6,4},{8,6},{10,8},{12,10},{14,12},{16,14},{18,... | collective-permute-start | bytes 294920 | tf_op jit(solution)/shard_map/ppermute | solution.py:19
  247.9 11.2 %collective-permute-start.28 = (bf16[256,192]{0,1:T(8,128)(2,1)S(1)}, bf16[256,192]{0,1:T(8,128)(2,1)S(1)}, u32[]{:S(2)}, u32[]{:S(2)}) collective-permute-start(bf16[256,192]{0,1:T(8,128)(2,1)S(1)} %get-tuple-element.24), channel_id=1, source_target_pairs={{0,30},{2,0},{4,2},{6,4},{8,6},{10,8},{12,10},{14,12},{16,14},{18,... | collective-permute-start | bytes 294920 | tf_op jit(solution)/shard_map/ppermute | solution.py:19
  254.5 11.2 %collective-permute-start.45 = (bf16[256,192]{0,1:T(8,128)(2,1)S(1)}, bf16[256,192]{0,1:T(8,128)(2,1)S(1)}, u32[]{:S(2)}, u32[]{:S(2)}) collective-permute-start(bf16[256,192]{0,1:T(8,128)(2,1)S(1)} %get-tuple-element.8), channel_id=1, source_target_pairs={{0,30},{2,0},{4,2},{6,4},{8,6},{10,8},{12,10},{14,12},{16,14},{18,... | collective-permute-start | bytes 294920 | tf_op jit(solution)/shard_map/ppermute | solution.py:19
  259.2 30.6 %collective-permute-start.22 = (bf16[256,192]{0,1:T(8,128)(2,1)S(1)}, bf16[256,192]{0,1:T(8,128)(2,1)S(1)}, u32[]{:S(2)}, u32[]{:S(2)}) collective-permute-start(bf16[256,192]{0,1:T(8,128)(2,1)S(1)} %get-tuple-element.21), channel_id=1, source_target_pairs={{0,2},{2,4},{4,6},{6,8},{8,10},{10,12},{12,14},{14,16},{16,18},{18... | collective-permute-start | bytes 294920 | tf_op jit(solution)/shard_map/ppermute | solution.py:19
  261.1 28.7 %collective-permute-start.29 = (bf16[256,192]{0,1:T(8,128)(2,1)S(1)}, bf16[256,192]{0,1:T(8,128)(2,1)S(1)}, u32[]{:S(2)}, u32[]{:S(2)}) collective-permute-start(bf16[256,192]{0,1:T(8,128)(2,1)S(1)} %get-tuple-element.22), channel_id=1, source_target_pairs={{0,30},{2,0},{4,2},{6,4},{8,6},{10,8},{12,10},{14,12},{16,14},{18,... | collective-permute-start | bytes 294920 | tf_op jit(solution)/shard_map/ppermute | solution.py:19
  265.8 32.7 %collective-permute-start.46 = (bf16[256,192]{0,1:T(8,128)(2,1)S(1)}, bf16[256,192]{0,1:T(8,128)(2,1)S(1)}, u32[]{:S(2)}, u32[]{:S(2)}) collective-permute-start(bf16[256,192]{0,1:T(8,128)(2,1)S(1)} %fusion.50), channel_id=1, source_target_pairs={{32,0},{64,32},{96,64},{128,96},{160,128},{192,160},{224,192},{256... | collective-permute-start | bytes 294920 | tf_op jit(solution)/shard_map/ppermute | solution.py:14
  289.9 8.6 %collective-permute-start.30 = (bf16[256,192]{0,1:T(8,128)(2,1)S(1)}, bf16[256,192]{0,1:T(8,128)(2,1)S(1)}, u32[]{:S(2)}, u32[]{:S(2)}) collective-permute-start(bf16[256,192]{0,1:T(8,128)(2,1)S(1)} %fusion.66), channel_id=1, source_target_pairs={{32,0},{64,32},{96,64},{128,96},{160,128},{192,160},{224,192},{256... | collective-permute-start | bytes 294920 | tf_op jit(solution)/shard_map/ppermute | solution.py:14
  (44 other events, 764.5 us)

commit v2 on v1

--- a/solution.py
+++ b/solution.py
@@ -38,30 +38,40 @@
     return jnp.roll(stacked, me, axis=0)
 
 
-def ring_reduce_scatter(parts, axis, extra=None):
+def ring_reduce_scatter(parts, exact, axis):
     n = lax.axis_size(axis)
     me = lax.axis_index(axis)
+    rows, columns = parts.shape[1], parts.shape[2]
+    pad = 16 - 2
     forward_steps = n // 2
     backward_steps = n - 1 - forward_steps
 
     def pick(stack, offset):
         return lax.dynamic_index_in_dim(stack, (me + offset) % n, 0, keepdims=False)
 
-    def part_at(offset):
-        head = pick(parts, offset).astype(jnp.float32)
-        if extra is None:
-            return (head,)
-        return (head, pick(extra, offset))
+    def own(offset):
+        return pick(parts, offset).astype(jnp.float32), pick(exact, offset)
 
     def wire(values):
-        return (values[0].astype(jnp.bfloat16),) + tuple(values[1:])
-
-    def add(received, offset):
-        own = part_at(offset)
-        return tuple(r.astype(jnp.float32) + o for r, o in zip(received, own))
-
-    forward = wire(part_at(forward_steps))
-    backward = wire(part_at(n - backward_steps))
+        main, extra = values
+        high = extra.astype(jnp.bfloat16)
+        low = (extra - high.astype(jnp.float32)).astype(jnp.bfloat16)
+        return jnp.concatenate(
+            [main.astype(jnp.bfloat16), high[None], low[None], jnp.zeros((pad, columns), jnp.bfloat16)]
+        )
+
+    def unwire(packet):
+        main = packet[:rows].astype(jnp.float32)
+        extra = packet[rows].astype(jnp.float32) + packet[rows + 1].astype(jnp.float32)
+        return main, extra
+
+    def add(packet, offset):
+        main, extra = unwire(packet)
+        own_main, own_extra = own(offset)
+        return main + own_main, extra + own_extra
+
+    forward = wire(own(forward_steps))
+    backward = wire(own(n - backward_steps))
     for step in range(forward_steps):
         forward = shift(forward, axis, 1)
         if step < forward_steps - 1:
@@ -70,10 +80,10 @@
             backward = shift(backward, axis, -1)
             if step < backward_steps - 1:
                 backward = wire(add(backward, n - backward_steps + 1 + step))
-    own = part_at(0)
-    return tuple(
-        o + f.astype(jnp.float32) + b.astype(jnp.float32) for o, f, b in zip(own, forward, backward)
-    )
+    own_main, own_extra = own(0)
+    forward_main, forward_extra = unwire(forward)
+    backward_main, backward_extra = unwire(backward)
+    return own_main + forward_main + backward_main, own_extra + forward_extra + backward_extra
 
 
 def token_mask(key_lists, length):
@@ -150,8 +160,6 @@
         w_output.reshape(w_output.shape[0], n_mp, share),
         preferred_element_type=jnp.float32,
     ).astype(jnp.bfloat16)
-    (out_share,) = ring_reduce_scatter(out_parts, "mp")
-    rebuilt = (lower_out[0, 0].astype(jnp.float32) - out_share).astype(jnp.bfloat16)
     attention_gradient = jnp.dot(whole_grad, w_output.T, preferred_element_type=jnp.float32).astype(
         jnp.bfloat16
     )
@@ -187,12 +195,16 @@
     grad_parts = ((weighted - unit_rows * row_stat) * inverse).astype(jnp.bfloat16)
     grad_parts = jnp.transpose(grad_parts.reshape(length, n_mp, share), (1, 0, 2))
     gain_parts = jnp.sum(normed_grad * unit_rows, axis=0).reshape(n_mp, share)
-    grad_share, gain_share = ring_reduce_scatter(grad_parts, "mp", gain_parts)
+    shares, gain_share = ring_reduce_scatter(
+        jnp.concatenate([out_parts, grad_parts], axis=1), gain_parts, "mp"
+    )
+    out_share, grad_share = shares[:length], shares[length:]
+    rebuilt = (lower_out[0, 0].astype(jnp.float32) - out_share).astype(jnp.bfloat16)
     lower_rows = upper_grad[0, 0].astype(jnp.float32) + grad_share
     gain_grad = gain_share + shift(gain_share, "dp", 1)
     entering = lower_rows.astype(jnp.bfloat16)
-    sent_lower, sent_grad = from_behind((rebuilt, entering), "section", -1)
-    return (sent_lower[None, None], sent_grad[None, None], gain_grad[None])
+    sent = from_behind(jnp.stack([rebuilt, entering]), "section", -1)
+    return (sent[0][None, None], sent[1][None, None], gain_grad[None])
 
 
 def solution(mesh):

time: 304 us -> 321 us (1.056)
  starting transfers between devices: 235 us -> 139 us
  waiting for transfers between devices: 22 us -> 105 us
  other arithmetic: 14.4 us -> 37.1 us
  local copies, waits for them, and re-layouts: 7.6 us -> 15.7 us
    ppermute x61 -> x31, starting transfers between devices: 209 us -> 112 us  [shift(): lax.ppermute(x, axis, [(i, (i + by) % length) for i in range(length)])]
    ppermute x61 -> x31, waiting for transfers between devices: 21.9 us -> 105 us  [shift(): lax.ppermute(x, axis, [(i, (i + by) % length) for i in range(length)])]
    convert_element_type x17 -> x39, other arithmetic: 1.22 us -> 17.2 us  [the longest x12 12.8 us: wire(): main.astype(jnp.bfloat16)]
    dot_general x0 -> x1, local copies, waits for them, and re-layouts: none -> 4.34 us  [local(): jnp.einsum('lc,cmf->mlf', attended, w_output.reshape(w_output.shape[0], n...]
    ppermute x2 -> x1, starting transfers between devices: 26.1 us -> 26.5 us  [from_behind(): return lax.ppermute(x, axis, pairs)]
  transfers between devices with their start and end apart: 63 -> 32, of which waited for: 9 -> 22; matrix products, arithmetic and copies ran while one was open for 5% -> 2% of each run, Pallas kernels for 0% -> 0%
where the time goes in v2:
time: 321 us; the launch traced here: 319 us
  starting transfers between devices  139 us (43%)
  waiting for transfers between devices  105 us (33%)
  other arithmetic  37.1 us (12%)
  matrix products  20.6 us (6%)
  local copies, waits for them, and re-layouts  15.7 us (5%)
    ppermute x31, starting transfers between devices, shift(): lax.ppermute(x, axis, [(i, (i + by) % length) for i in range(length)])  112 us
    ppermute x31, waiting for transfers between devices, shift(): lax.ppermute(x, axis, [(i, (i + by) % length) for i in range(length)])  105 us
    ppermute x1, starting transfers between devices, from_behind(): return lax.ppermute(x, axis, pairs)  26.5 us
    convert_element_type x12, other arithmetic, wire(): main.astype(jnp.bfloat16)  12.8 us
  transfers between devices with their start and end apart: 32, of which 22 were waited for; matrix products, arithmetic and copies ran while one was open for 2% of the time, Pallas kernels for 0%

profile of v2, /device:TPU:1, one launch (start us, length us, event | category | flops | bytes accessed | tf_op | source)
XLA Modules:
  0.0 318.8 jit_solution(11916461096111470581)
XLA Ops:
  1.8 18.8 %collective-permute-start = (bf16[2,256,192]{1,2,0:T(8,128)(2,1)S(1)}, bf16[2,256,192]{1,2,0:T(8,128)(2,1)S(1)}, u32[]{:S(2)}, u32[]{:S(2)}) collective-permute-start(bf16[2,256,192]{1,2,0:T(8,128)(2,1)S(1)} %pad_maximum_fusion.1), channel_id=1, source_target_pairs={{0,30},{2,0},{4,2},{6,4},{8,6},{10,8},{12,10},{14,12},{16,14},{18,... | collective-permute-start | bytes 589832 | tf_op jit(solution)/shard_map/ppermute | solution.py:19
  26.6 4.6 %collective-permute-start.1 = (bf16[2,256,192]{1,2,0:T(8,128)(2,1)S(1)}, bf16[2,256,192]{1,2,0:T(8,128)(2,1)S(1)}, u32[]{:S(2)}, u32[]{:S(2)}) collective-permute-start(bf16[2,256,192]{1,2,0:T(8,128)(2,1)S(1)} %collective-permute-done), channel_id=1, source_target_pairs={{0,30},{2,0},{4,2},{6,4},{8,6},{10,8},{12,10},{14,12},{16,14},{18,... | collective-permute-start | bytes 589832 | tf_op jit(solution)/shard_map/ppermute | solution.py:19
  34.1 5.3 %collective-permute-start.2 = (bf16[2,256,192]{1,2,0:T(8,128)(2,1)S(1)}, bf16[2,256,192]{1,2,0:T(8,128)(2,1)S(1)}, u32[]{:S(2)}, u32[]{:S(2)}) collective-permute-start(bf16[2,256,192]{1,2,0:T(8,128)(2,1)S(1)} %collective-permute-done.1), channel_id=1, source_target_pairs={{0,30},{2,0},{4,2},{6,4},{8,6},{10,8},{12,10},{14,12},{16,14},{18,... | collective-permute-start | bytes 589832 | tf_op jit(solution)/shard_map/ppermute | solution.py:19
  42.0 5.0 %collective-permute-start.3 = (bf16[2,256,192]{1,2,0:T(8,128)(2,1)S(1)}, bf16[2,256,192]{1,2,0:T(8,128)(2,1)S(1)}, u32[]{:S(2)}, u32[]{:S(2)}) collective-permute-start(bf16[2,256,192]{1,2,0:T(8,128)(2,1)S(1)} %collective-permute-done.2), channel_id=1, source_target_pairs={{0,30},{2,0},{4,2},{6,4},{8,6},{10,8},{12,10},{14,12},{16,14},{18,... | collective-permute-start | bytes 589832 | tf_op jit(solution)/shard_map/ppermute | solution.py:19
  49.6 5.0 %collective-permute-start.4 = (bf16[2,256,192]{1,2,0:T(8,128)(2,1)S(1)}, bf16[2,256,192]{1,2,0:T(8,128)(2,1)S(1)}, u32[]{:S(2)}, u32[]{:S(2)}) collective-permute-start(bf16[2,256,192]{1,2,0:T(8,128)(2,1)S(1)} %collective-permute-done.3), channel_id=1, source_target_pairs={{0,30},{2,0},{4,2},{6,4},{8,6},{10,8},{12,10},{14,12},{16,14},{18,... | collective-permute-start | bytes 589832 | tf_op jit(solution)/shard_map/ppermute | solution.py:19
  57.2 5.0 %collective-permute-start.5 = (bf16[2,256,192]{1,2,0:T(8,128)(2,1)S(1)}, bf16[2,256,192]{1,2,0:T(8,128)(2,1)S(1)}, u32[]{:S(2)}, u32[]{:S(2)}) collective-permute-start(bf16[2,256,192]{1,2,0:T(8,128)(2,1)S(1)} %collective-permute-done.4), channel_id=1, source_target_pairs={{0,30},{2,0},{4,2},{6,4},{8,6},{10,8},{12,10},{14,12},{16,14},{18,... | collective-permute-start | bytes 589832 | tf_op jit(solution)/shard_map/ppermute | solution.py:19
  64.8 5.0 %collective-permute-start.6 = (bf16[2,256,192]{1,2,0:T(8,128)(2,1)S(1)}, bf16[2,256,192]{1,2,0:T(8,128)(2,1)S(1)}, u32[]{:S(2)}, u32[]{:S(2)}) collective-permute-start(bf16[2,256,192]{1,2,0:T(8,128)(2,1)S(1)} %collective-permute-done.5), channel_id=1, source_target_pairs={{0,30},{2,0},{4,2},{6,4},{8,6},{10,8},{12,10},{14,12},{16,14},{18,... | collective-permute-start | bytes 589832 | tf_op jit(solution)/shard_map/ppermute | solution.py:19
  71.8 6.5 %collective-permute-done.13 = bf16[2,256,192]{1,2,0:T(8,128)(2,1)S(1)} collective-permute-done((bf16[2,256,192]{1,2,0:T(8,128)(2,1)S(1)}, bf16[2,256,192]{1,2,0:T(8,128)(2,1)S(1)}, u32[]{:S(2)}, u32[]{:S(2)}) %collective-permute-start.13) | collective-permute-done | bytes 196640 | tf_op jit(solution)/shard_map/ppermute | solution.py:19
  80.3 7.8 %collective-permute-done.14 = bf16[2,256,192]{1,2,0:T(8,128)(2,1)S(1)} collective-permute-done((bf16[2,256,192]{1,2,0:T(8,128)(2,1)S(1)}, bf16[2,256,192]{1,2,0:T(8,128)(2,1)S(1)}, u32[]{:S(2)}, u32[]{:S(2)}) %collective-permute-start.14) | collective-permute-done | bytes 196640 | tf_op jit(solution)/shard_map/ppermute | solution.py:19
  104.7 4.4 %convolution_add_fusion.1 = f32[256,3072]{1,0:T(8,128)} fusion(f32[256,3072]{1,0:T(8,128)} %fusion.5, bf16[256,2,128]{0,2,1:T(8,128)(2,1)S(1)} %bitcast.347, bf16[2,256,256]{1,2,0:T(8,128)(2,1)S(1)} %fusion.61, bf16[1,3072,128]{2,1,0:T(8,128)(2,1)S(1)} %copy-done.3), kind=kOutput, calls=%fused_computation.33 | convolution fusion | flops 235700224 | bytes 7471104 | tf_op jit(solution)/shard_map/dot_general | solution.py:189
  109.2 6.2 %multiply_reduce_fusion.1 = (f32[256]{0:T(256)S(1)}, f32[3072]{0:T(1024)S(1)}, f32[256,3072]{1,0:T(8,128)}) fusion(f32[256,3072]{1,0:T(8,128)} %copy.234, f32[256]{0:T(256)S(1)} %add_rsqrt_fusion, f32[3072]{0:T(1024)S(1)} %bitcast.352, f32[256,3072]{1,0:T(8,128)} %convolution_add_fusion.1, bf16[1,3072,128]{2,1,0:T(8,128)(2,1)} %param.17, ...), kind=kOutput, calls=%fused_computation.36 | convolution fusion | flops 240939776 | bytes 10975232 | tf_op jit(solution)/shard_map/dot_general | solution.py:190
  115.4 4.9 %multiply_convert_fusion = bf16[256,3072]{1,0:T(8,128)(2,1)} fusion(f32[256,3072]{1,0:T(8,128)} %get-tuple-element.56, f32[256,3072]{1,0:T(8,128)} %copy.234, f32[256]{0:T(256)S(1)} %broadcast_multiply_fusion, f32[256]{0:T(256)S(1)} %add_rsqrt_fusion, f32[3072]{0:T(1024)S(1)} %bitcast.353), kind=kLoop, calls=%fused_computation.35 | loop fusion | flops 4718592 | bytes 7878656 | tf_op jit(solution)/shard_map/convert_element_type | solution.py:195
  124.6 3.7 %fusion.3 = f32[256,3072]{0,1} fusion(bf16[256,256]{0,1:T(8,128)(2,1)S(1)} %bitcast.349, bf16[1,256,3072]{2,1,0:T(8,128)(2,1)} %param.18), kind=kOutput, calls=%fused_computation.44 | convolution fusion | flops 402653184 | bytes 4849664
  128.3 4.3 %copy.228 = bf16[256,16,192]{2,0,1:T(8,128)(2,1)} copy(f32[256,16,192]{0,2,1:T(8,128)} %bitcast.333) | data formatting | bytes 4718592 | tf_op jit(solution)/shard_map/lc,cmf->mlf/dot_general | solution.py:157
  135.9 6.5 %collective-permute-done.15 = bf16[528,192]{1,0:T(8,128)(2,1)S(1)} collective-permute-done((bf16[528,192]{1,0:T(8,128)(2,1)S(1)}, bf16[528,192]{1,0:T(8,128)(2,1)S(1)}, u32[]{:S(2)}, u32[]{:S(2)}) %collective-permute-start.15) | collective-permute-done | bytes 202784 | tf_op jit(solution)/shard_map/ppermute | solution.py:19
  146.2 8.7 %collective-permute-done.16 = bf16[528,192]{1,0:T(8,128)(2,1)S(1)} collective-permute-done((bf16[528,192]{1,0:T(8,128)(2,1)S(1)}, bf16[528,192]{1,0:T(8,128)(2,1)S(1)}, u32[]{:S(2)}, u32[]{:S(2)}) %collective-permute-start.16) | collective-permute-done | bytes 202784 | tf_op jit(solution)/shard_map/ppermute | solution.py:19
  158.8 9.3 %collective-permute-done.17 = bf16[528,192]{1,0:T(8,128)(2,1)S(1)} collective-permute-done((bf16[528,192]{1,0:T(8,128)(2,1)S(1)}, bf16[528,192]{1,0:T(8,128)(2,1)S(1)}, u32[]{:S(2)}, u32[]{:S(2)}) %collective-permute-start.17) | collective-permute-done | bytes 202784 | tf_op jit(solution)/shard_map/ppermute | solution.py:19
  171.9 8.4 %collective-permute-done.18 = bf16[528,192]{1,0:T(8,128)(2,1)S(1)} collective-permute-done((bf16[528,192]{1,0:T(8,128)(2,1)S(1)}, bf16[528,192]{1,0:T(8,128)(2,1)S(1)}, u32[]{:S(2)}, u32[]{:S(2)}) %collective-permute-start.18) | collective-permute-done | bytes 202784 | tf_op jit(solution)/shard_map/ppermute | solution.py:19
  184.3 7.3 %collective-permute-done.19 = bf16[528,192]{1,0:T(8,128)(2,1)S(1)} collective-permute-done((bf16[528,192]{1,0:T(8,128)(2,1)S(1)}, bf16[528,192]{1,0:T(8,128)(2,1)S(1)}, u32[]{:S(2)}, u32[]{:S(2)}) %collective-permute-start.19) | collective-permute-done | bytes 202784 | tf_op jit(solution)/shard_map/ppermute | solution.py:19
  195.4 6.5 %collective-permute-done.20 = bf16[528,192]{1,0:T(8,128)(2,1)S(1)} collective-permute-done((bf16[528,192]{1,0:T(8,128)(2,1)S(1)}, bf16[528,192]{1,0:T(8,128)(2,1)S(1)}, u32[]{:S(2)}, u32[]{:S(2)}) %collective-permute-start.20) | collective-permute-done | bytes 202784 | tf_op jit(solution)/shard_map/ppermute | solution.py:19
  205.8 6.5 %collective-permute-done.21 = bf16[528,192]{1,0:T(8,128)(2,1)S(1)} collective-permute-done((bf16[528,192]{1,0:T(8,128)(2,1)S(1)}, bf16[528,192]{1,0:T(8,128)(2,1)S(1)}, u32[]{:S(2)}, u32[]{:S(2)}) %collective-permute-start.21) | collective-permute-done | bytes 202784 | tf_op jit(solution)/shard_map/ppermute | solution.py:19
  214.3 5.3 %collective-permute-done.23 = bf16[528,192]{1,0:T(8,128)(2,1)S(1)} collective-permute-done((bf16[528,192]{1,0:T(8,128)(2,1)S(1)}, bf16[528,192]{1,0:T(8,128)(2,1)S(1)}, u32[]{:S(2)}, u32[]{:S(2)}) %collective-permute-start.23) | collective-permute-done | bytes 202784 | tf_op jit(solution)/shard_map/ppermute | solution.py:19
  224.2 4.0 %collective-permute-done.24 = bf16[528,192]{1,0:T(8,128)(2,1)S(1)} collective-permute-done((bf16[528,192]{1,0:T(8,128)(2,1)S(1)}, bf16[528,192]{1,0:T(8,128)(2,1)S(1)}, u32[]{:S(2)}, u32[]{:S(2)}) %collective-permute-start.24) | collective-permute-done | bytes 202784 | tf_op jit(solution)/shard_map/ppermute | solution.py:19
  229.5 4.3 %collective-permute-start.25 = (bf16[528,192]{1,0:T(8,128)(2,1)S(1)}, bf16[528,192]{1,0:T(8,128)(2,1)S(1)}, u32[]{:S(2)}, u32[]{:S(2)}) collective-permute-start(bf16[528,192]{1,0:T(8,128)(2,1)S(1)} %maximum_maximum_fusion.10), channel_id=1, source_target_pairs={{0,30},{2,0},{4,2},{6,4},{8,6},{10,8},{12,10},{14,12},{16,14},{18,... | collective-permute-start | bytes 608264 | tf_op jit(solution)/shard_map/ppermute | solution.py:19
  233.9 5.5 %collective-permute-done.25 = bf16[528,192]{1,0:T(8,128)(2,1)S(1)} collective-permute-done((bf16[528,192]{1,0:T(8,128)(2,1)S(1)}, bf16[528,192]{1,0:T(8,128)(2,1)S(1)}, u32[]{:S(2)}, u32[]{:S(2)}) %collective-permute-start.25) | collective-permute-done | bytes 202784 | tf_op jit(solution)/shard_map/ppermute | solution.py:19
  243.5 6.4 %collective-permute-done.26 = bf16[528,192]{1,0:T(8,128)(2,1)S(1)} collective-permute-done((bf16[528,192]{1,0:T(8,128)(2,1)S(1)}, bf16[528,192]{1,0:T(8,128)(2,1)S(1)}, u32[]{:S(2)}, u32[]{:S(2)}) %collective-permute-start.26) | collective-permute-done | bytes 202784 | tf_op jit(solution)/shard_map/ppermute | solution.py:19
  251.1 4.9 %collective-permute-start.27 = (bf16[528,192]{1,0:T(8,128)(2,1)S(1)}, bf16[528,192]{1,0:T(8,128)(2,1)S(1)}, u32[]{:S(2)}, u32[]{:S(2)}) collective-permute-start(bf16[528,192]{1,0:T(8,128)(2,1)S(1)} %maximum_maximum_fusion.12), channel_id=1, source_target_pairs={{0,30},{2,0},{4,2},{6,4},{8,6},{10,8},{12,10},{14,12},{16,14},{18,... | collective-permute-start | bytes 608264 | tf_op jit(solution)/shard_map/ppermute | solution.py:19
  256.1 5.4 %collective-permute-done.27 = bf16[528,192]{1,0:T(8,128)(2,1)S(1)} collective-permute-done((bf16[528,192]{1,0:T(8,128)(2,1)S(1)}, bf16[528,192]{1,0:T(8,128)(2,1)S(1)}, u32[]{:S(2)}, u32[]{:S(2)}) %collective-permute-start.27) | collective-permute-done | bytes 202784 | tf_op jit(solution)/shard_map/ppermute | solution.py:19
  262.7 5.3 %collective-permute-start.28 = (bf16[528,192]{1,0:T(8,128)(2,1)S(1)}, bf16[528,192]{1,0:T(8,128)(2,1)S(1)}, u32[]{:S(2)}, u32[]{:S(2)}) collective-permute-start(bf16[528,192]{1,0:T(8,128)(2,1)S(1)} %maximum_maximum_fusion.13), channel_id=1, source_target_pairs={{0,30},{2,0},{4,2},{6,4},{8,6},{10,8},{12,10},{14,12},{16,14},{18,... | collective-permute-start | bytes 608264 | tf_op jit(solution)/shard_map/ppermute | solution.py:19
  273.9 5.3 %collective-permute-start.29 = (bf16[528,192]{1,0:T(8,128)(2,1)S(1)}, bf16[528,192]{1,0:T(8,128)(2,1)S(1)}, u32[]{:S(2)}, u32[]{:S(2)}) collective-permute-start(bf16[528,192]{1,0:T(8,128)(2,1)S(1)} %maximum_maximum_fusion.14), channel_id=1, source_target_pairs={{0,30},{2,0},{4,2},{6,4},{8,6},{10,8},{12,10},{14,12},{16,14},{18,... | collective-permute-start | bytes 608264 | tf_op jit(solution)/shard_map/ppermute | solution.py:19
  284.1 26.5 %collective-permute-start.30 = (bf16[2,256,192]{2,1,0:T(8,128)(2,1)S(1)}, bf16[2,256,192]{2,1,0:T(8,128)(2,1)S(1)}, u32[]{:S(2)}, u32[]{:S(2)}) collective-permute-start(bf16[2,256,192]{2,1,0:T(8,128)(2,1)S(1)} %pad_maximum_fusion), channel_id=1, source_target_pairs={{32,0},{64,32},{96,64},{128,96},{160,128},{192,160},{224,192},{256... | collective-permute-start | bytes 589832 | tf_op jit(solution)/shard_map/ppermute | solution.py:14
  310.6 4.7 %collective-permute-start.31 = (f32[192]{0:T(256)S(1)}, f32[192]{0:T(256)S(1)}, u32[]{:S(2)}, u32[]{:S(2)}) collective-permute-start(f32[192]{0:T(256)S(1)} %bitcast.354), channel_id=1, source_target_pairs={{0,1},{1,0},{2,3},{3,2},{4,5},{5,4},{6,7},{7,6},{8,9},{9,8},{10,11... | collective-permute-start | bytes 2312 | tf_op jit(solution)/shard_map/ppermute | solution.py:19
  (190 shorter events, 99.6 us)
Async XLA Ops:
  1.8 24.8 %collective-permute-start = (bf16[2,256,192]{1,2,0:T(8,128)(2,1)S(1)}, bf16[2,256,192]{1,2,0:T(8,128)(2,1)S(1)}, u32[]{:S(2)}, u32[]{:S(2)}) collective-permute-start(bf16[2,256,192]{1,2,0:T(8,128)(2,1)S(1)} %pad_maximum_fusion.1), channel_id=1, source_target_pairs={{0,30},{2,0},{4,2},{6,4},{8,6},{10,8},{12,10},{14,12},{16,14},{18,... | collective-permute-start | bytes 589832 | tf_op jit(solution)/shard_map/ppermute | solution.py:19
  20.5 10.6 %collective-permute-start.7 = (bf16[2,256,192]{1,2,0:T(8,128)(2,1)S(1)}, bf16[2,256,192]{1,2,0:T(8,128)(2,1)S(1)}, u32[]{:S(2)}, u32[]{:S(2)}) collective-permute-start(bf16[2,256,192]{1,2,0:T(8,128)(2,1)S(1)} %pad_maximum_fusion.1), channel_id=1, source_target_pairs={{0,2},{2,4},{4,6},{6,8},{8,10},{10,12},{12,14},{14,16},{16,18},{18... | collective-permute-start | bytes 589832 | tf_op jit(solution)/shard_map/ppermute | solution.py:19
  26.6 7.5 %collective-permute-start.1 = (bf16[2,256,192]{1,2,0:T(8,128)(2,1)S(1)}, bf16[2,256,192]{1,2,0:T(8,128)(2,1)S(1)}, u32[]{:S(2)}, u32[]{:S(2)}) collective-permute-start(bf16[2,256,192]{1,2,0:T(8,128)(2,1)S(1)} %collective-permute-done), channel_id=1, source_target_pairs={{0,30},{2,0},{4,2},{6,4},{8,6},{10,8},{12,10},{14,12},{16,14},{18,... | collective-permute-start | bytes 589832 | tf_op jit(solution)/shard_map/ppermute | solution.py:19
  31.2 8.2 %collective-permute-start.8 = (bf16[2,256,192]{1,2,0:T(8,128)(2,1)S(1)}, bf16[2,256,192]{1,2,0:T(8,128)(2,1)S(1)}, u32[]{:S(2)}, u32[]{:S(2)}) collective-permute-start(bf16[2,256,192]{1,2,0:T(8,128)(2,1)S(1)} %collective-permute-done.7), channel_id=1, source_target_pairs={{0,2},{2,4},{4,6},{6,8},{8,10},{10,12},{12,14},{14,16},{16,18},{18... | collective-permute-start | bytes 589832 | tf_op jit(solution)/shard_map/ppermute | solution.py:19
  34.1 7.9 %collective-permute-start.2 = (bf16[2,256,192]{1,2,0:T(8,128)(2,1)S(1)}, bf16[2,256,192]{1,2,0:T(8,128)(2,1)S(1)}, u32[]{:S(2)}, u32[]{:S(2)}) collective-permute-start(bf16[2,256,192]{1,2,0:T(8,128)(2,1)S(1)} %collective-permute-done.1), channel_id=1, source_target_pairs={{0,30},{2,0},{4,2},{6,4},{8,6},{10,8},{12,10},{14,12},{16,14},{18,... | collective-permute-start | bytes 589832 | tf_op jit(solution)/shard_map/ppermute | solution.py:19
  39.4 7.6 %collective-permute-start.9 = (bf16[2,256,192]{1,2,0:T(8,128)(2,1)S(1)}, bf16[2,256,192]{1,2,0:T(8,128)(2,1)S(1)}, u32[]{:S(2)}, u32[]{:S(2)}) collective-permute-start(bf16[2,256,192]{1,2,0:T(8,128)(2,1)S(1)} %collective-permute-done.8), channel_id=1, source_target_pairs={{0,2},{2,4},{4,6},{6,8},{8,10},{10,12},{12,14},{14,16},{16,18},{18... | collective-permute-start | bytes 589832 | tf_op jit(solution)/shard_map/ppermute | solution.py:19
  42.0 7.6 %collective-permute-start.3 = (bf16[2,256,192]{1,2,0:T(8,128)(2,1)S(1)}, bf16[2,256,192]{1,2,0:T(8,128)(2,1)S(1)}, u32[]{:S(2)}, u32[]{:S(2)}) collective-permute-start(bf16[2,256,192]{1,2,0:T(8,128)(2,1)S(1)} %collective-permute-done.2), channel_id=1, source_target_pairs={{0,30},{2,0},{4,2},{6,4},{8,6},{10,8},{12,10},{14,12},{16,14},{18,... | collective-permute-start | bytes 589832 | tf_op jit(solution)/shard_map/ppermute | solution.py:19
  47.0 7.6 %collective-permute-start.10 = (bf16[2,256,192]{1,2,0:T(8,128)(2,1)S(1)}, bf16[2,256,192]{1,2,0:T(8,128)(2,1)S(1)}, u32[]{:S(2)}, u32[]{:S(2)}) collective-permute-start(bf16[2,256,192]{1,2,0:T(8,128)(2,1)S(1)} %collective-permute-done.9), channel_id=1, source_target_pairs={{0,2},{2,4},{4,6},{6,8},{8,10},{10,12},{12,14},{14,16},{16,18},{18... | collective-permute-start | bytes 589832 | tf_op jit(solution)/shard_map/ppermute | solution.py:19
  49.6 7.6 %collective-permute-start.4 = (bf16[2,256,192]{1,2,0:T(8,128)(2,1)S(1)}, bf16[2,256,192]{1,2,0:T(8,128)(2,1)S(1)}, u32[]{:S(2)}, u32[]{:S(2)}) collective-permute-start(bf16[2,256,192]{1,2,0:T(8,128)(2,1)S(1)} %collective-permute-done.3), channel_id=1, source_target_pairs={{0,30},{2,0},{4,2},{6,4},{8,6},{10,8},{12,10},{14,12},{16,14},{18,... | collective-permute-start | bytes 589832 | tf_op jit(solution)/shard_map/ppermute | solution.py:19
  54.7 7.6 %collective-permute-start.11 = (bf16[2,256,192]{1,2,0:T(8,128)(2,1)S(1)}, bf16[2,256,192]{1,2,0:T(8,128)(2,1)S(1)}, u32[]{:S(2)}, u32[]{:S(2)}) collective-permute-start(bf16[2,256,192]{1,2,0:T(8,128)(2,1)S(1)} %collective-permute-done.10), channel_id=1, source_target_pairs={{0,2},{2,4},{4,6},{6,8},{8,10},{10,12},{12,14},{14,16},{16,18},{18... | collective-permute-start | bytes 589832 | tf_op jit(solution)/shard_map/ppermute | solution.py:19
  57.2 7.6 %collective-permute-start.5 = (bf16[2,256,192]{1,2,0:T(8,128)(2,1)S(1)}, bf16[2,256,192]{1,2,0:T(8,128)(2,1)S(1)}, u32[]{:S(2)}, u32[]{:S(2)}) collective-permute-start(bf16[2,256,192]{1,2,0:T(8,128)(2,1)S(1)} %collective-permute-done.4), channel_id=1, source_target_pairs={{0,30},{2,0},{4,2},{6,4},{8,6},{10,8},{12,10},{14,12},{16,14},{18,... | collective-permute-start | bytes 589832 | tf_op jit(solution)/shard_map/ppermute | solution.py:19
  62.3 7.6 %collective-permute-start.12 = (bf16[2,256,192]{1,2,0:T(8,128)(2,1)S(1)}, bf16[2,256,192]{1,2,0:T(8,128)(2,1)S(1)}, u32[]{:S(2)}, u32[]{:S(2)}) collective-permute-start(bf16[2,256,192]{1,2,0:T(8,128)(2,1)S(1)} %collective-permute-done.11), channel_id=1, source_target_pairs={{0,2},{2,4},{4,6},{6,8},{8,10},{10,12},{12,14},{14,16},{16,18},{18... | collective-permute-start | bytes 589832 | tf_op jit(solution)/shard_map/ppermute | solution.py:19
  64.8 15.4 %collective-permute-start.6 = (bf16[2,256,192]{1,2,0:T(8,128)(2,1)S(1)}, bf16[2,256,192]{1,2,0:T(8,128)(2,1)S(1)}, u32[]{:S(2)}, u32[]{:S(2)}) collective-permute-start(bf16[2,256,192]{1,2,0:T(8,128)(2,1)S(1)} %collective-permute-done.5), channel_id=1, source_target_pairs={{0,30},{2,0},{4,2},{6,4},{8,6},{10,8},{12,10},{14,12},{16,14},{18,... | collective-permute-start | bytes 589832 | tf_op jit(solution)/shard_map/ppermute | solution.py:19
  69.9 8.5 %collective-permute-start.13 = (bf16[2,256,192]{1,2,0:T(8,128)(2,1)S(1)}, bf16[2,256,192]{1,2,0:T(8,128)(2,1)S(1)}, u32[]{:S(2)}, u32[]{:S(2)}) collective-permute-start(bf16[2,256,192]{1,2,0:T(8,128)(2,1)S(1)} %collective-permute-done.12), channel_id=1, source_target_pairs={{0,2},{2,4},{4,6},{6,8},{8,10},{10,12},{12,14},{14,16},{16,18},{18... | collective-permute-start | bytes 589832 | tf_op jit(solution)/shard_map/ppermute | solution.py:19
  78.3 9.7 %collective-permute-start.14 = (bf16[2,256,192]{1,2,0:T(8,128)(2,1)S(1)}, bf16[2,256,192]{1,2,0:T(8,128)(2,1)S(1)}, u32[]{:S(2)}, u32[]{:S(2)}) collective-permute-start(bf16[2,256,192]{1,2,0:T(8,128)(2,1)S(1)} %collective-permute-done.13), channel_id=1, source_target_pairs={{0,2},{2,4},{4,6},{6,8},{8,10},{10,12},{12,14},{14,16},{16,18},{18... | collective-permute-start | bytes 589832 | tf_op jit(solution)/shard_map/ppermute | solution.py:19
  134.0 8.4 %collective-permute-start.15 = (bf16[528,192]{1,0:T(8,128)(2,1)S(1)}, bf16[528,192]{1,0:T(8,128)(2,1)S(1)}, u32[]{:S(2)}, u32[]{:S(2)}) collective-permute-start(bf16[528,192]{1,0:T(8,128)(2,1)S(1)} %maximum_maximum_fusion), channel_id=1, source_target_pairs={{0,2},{2,4},{4,6},{6,8},{8,10},{10,12},{12,14},{14,16},{16,18},{18... | collective-permute-start | bytes 608264 | tf_op jit(solution)/shard_map/ppermute | solution.py:19
  144.3 10.6 %collective-permute-start.16 = (bf16[528,192]{1,0:T(8,128)(2,1)S(1)}, bf16[528,192]{1,0:T(8,128)(2,1)S(1)}, u32[]{:S(2)}, u32[]{:S(2)}) collective-permute-start(bf16[528,192]{1,0:T(8,128)(2,1)S(1)} %maximum_maximum_fusion.1), channel_id=1, source_target_pairs={{0,2},{2,4},{4,6},{6,8},{8,10},{10,12},{12,14},{14,16},{16,18},{18... | collective-permute-start | bytes 608264 | tf_op jit(solution)/shard_map/ppermute | solution.py:19
  156.8 11.2 %collective-permute-start.17 = (bf16[528,192]{1,0:T(8,128)(2,1)S(1)}, bf16[528,192]{1,0:T(8,128)(2,1)S(1)}, u32[]{:S(2)}, u32[]{:S(2)}) collective-permute-start(bf16[528,192]{1,0:T(8,128)(2,1)S(1)} %maximum_maximum_fusion.2), channel_id=1, source_target_pairs={{0,2},{2,4},{4,6},{6,8},{8,10},{10,12},{12,14},{14,16},{16,18},{18... | collective-permute-start | bytes 608264 | tf_op jit(solution)/shard_map/ppermute | solution.py:19
  169.9 10.3 %collective-permute-start.18 = (bf16[528,192]{1,0:T(8,128)(2,1)S(1)}, bf16[528,192]{1,0:T(8,128)(2,1)S(1)}, u32[]{:S(2)}, u32[]{:S(2)}) collective-permute-start(bf16[528,192]{1,0:T(8,128)(2,1)S(1)} %maximum_maximum_fusion.3), channel_id=1, source_target_pairs={{0,2},{2,4},{4,6},{6,8},{8,10},{10,12},{12,14},{14,16},{16,18},{18... | collective-permute-start | bytes 608264 | tf_op jit(solution)/shard_map/ppermute | solution.py:19
  182.2 9.4 %collective-permute-start.19 = (bf16[528,192]{1,0:T(8,128)(2,1)S(1)}, bf16[528,192]{1,0:T(8,128)(2,1)S(1)}, u32[]{:S(2)}, u32[]{:S(2)}) collective-permute-start(bf16[528,192]{1,0:T(8,128)(2,1)S(1)} %maximum_maximum_fusion.4), channel_id=1, source_target_pairs={{0,2},{2,4},{4,6},{6,8},{8,10},{10,12},{12,14},{14,16},{16,18},{18... | collective-permute-start | bytes 608264 | tf_op jit(solution)/shard_map/ppermute | solution.py:19
  193.5 8.4 %collective-permute-start.20 = (bf16[528,192]{1,0:T(8,128)(2,1)S(1)}, bf16[528,192]{1,0:T(8,128)(2,1)S(1)}, u32[]{:S(2)}, u32[]{:S(2)}) collective-permute-start(bf16[528,192]{1,0:T(8,128)(2,1)S(1)} %maximum_maximum_fusion.5), channel_id=1, source_target_pairs={{0,2},{2,4},{4,6},{6,8},{8,10},{10,12},{12,14},{14,16},{16,18},{18... | collective-permute-start | bytes 608264 | tf_op jit(solution)/shard_map/ppermute | solution.py:19
  203.8 8.4 %collective-permute-start.21 = (bf16[528,192]{1,0:T(8,128)(2,1)S(1)}, bf16[528,192]{1,0:T(8,128)(2,1)S(1)}, u32[]{:S(2)}, u32[]{:S(2)}) collective-permute-start(bf16[528,192]{1,0:T(8,128)(2,1)S(1)} %maximum_maximum_fusion.6), channel_id=1, source_target_pairs={{0,2},{2,4},{4,6},{6,8},{8,10},{10,12},{12,14},{14,16},{16,18},{18... | collective-permute-start | bytes 608264 | tf_op jit(solution)/shard_map/ppermute | solution.py:19
  212.4 7.2 %collective-permute-start.23 = (bf16[528,192]{1,0:T(8,128)(2,1)S(1)}, bf16[528,192]{1,0:T(8,128)(2,1)S(1)}, u32[]{:S(2)}, u32[]{:S(2)}) collective-permute-start(bf16[528,192]{1,0:T(8,128)(2,1)S(1)} %maximum_maximum_fusion.8), channel_id=1, source_target_pairs={{0,30},{2,0},{4,2},{6,4},{8,6},{10,8},{12,10},{14,12},{16,14},{18,... | collective-permute-start | bytes 608264 | tf_op jit(solution)/shard_map/ppermute | solution.py:19
  221.1 7.2 %collective-permute-start.24 = (bf16[528,192]{1,0:T(8,128)(2,1)S(1)}, bf16[528,192]{1,0:T(8,128)(2,1)S(1)}, u32[]{:S(2)}, u32[]{:S(2)}) collective-permute-start(bf16[528,192]{1,0:T(8,128)(2,1)S(1)} %get-tuple-element.51), channel_id=1, source_target_pairs={{0,30},{2,0},{4,2},{6,4},{8,6},{10,8},{12,10},{14,12},{16,14},{18,... | collective-permute-start | bytes 608264 | tf_op jit(solution)/shard_map/ppermute | solution.py:19
  229.5 9.9 %collective-permute-start.25 = (bf16[528,192]{1,0:T(8,128)(2,1)S(1)}, bf16[528,192]{1,0:T(8,128)(2,1)S(1)}, u32[]{:S(2)}, u32[]{:S(2)}) collective-permute-start(bf16[528,192]{1,0:T(8,128)(2,1)S(1)} %maximum_maximum_fusion.10), channel_id=1, source_target_pairs={{0,30},{2,0},{4,2},{6,4},{8,6},{10,8},{12,10},{14,12},{16,14},{18,... | collective-permute-start | bytes 608264 | tf_op jit(solution)/shard_map/ppermute | solution.py:19
  240.6 9.3 %collective-permute-start.26 = (bf16[528,192]{1,0:T(8,128)(2,1)S(1)}, bf16[528,192]{1,0:T(8,128)(2,1)S(1)}, u32[]{:S(2)}, u32[]{:S(2)}) collective-permute-start(bf16[528,192]{1,0:T(8,128)(2,1)S(1)} %maximum_maximum_fusion.11), channel_id=1, source_target_pairs={{0,30},{2,0},{4,2},{6,4},{8,6},{10,8},{12,10},{14,12},{16,14},{18,... | collective-permute-start | bytes 608264 | tf_op jit(solution)/shard_map/ppermute | solution.py:19
  251.1 10.4 %collective-permute-start.27 = (bf16[528,192]{1,0:T(8,128)(2,1)S(1)}, bf16[528,192]{1,0:T(8,128)(2,1)S(1)}, u32[]{:S(2)}, u32[]{:S(2)}) collective-permute-start(bf16[528,192]{1,0:T(8,128)(2,1)S(1)} %maximum_maximum_fusion.12), channel_id=1, source_target_pairs={{0,30},{2,0},{4,2},{6,4},{8,6},{10,8},{12,10},{14,12},{16,14},{18,... | collective-permute-start | bytes 608264 | tf_op jit(solution)/shard_map/ppermute | solution.py:19
  262.7 9.9 %collective-permute-start.28 = (bf16[528,192]{1,0:T(8,128)(2,1)S(1)}, bf16[528,192]{1,0:T(8,128)(2,1)S(1)}, u32[]{:S(2)}, u32[]{:S(2)}) collective-permute-start(bf16[528,192]{1,0:T(8,128)(2,1)S(1)} %maximum_maximum_fusion.13), channel_id=1, source_target_pairs={{0,30},{2,0},{4,2},{6,4},{8,6},{10,8},{12,10},{14,12},{16,14},{18,... | collective-permute-start | bytes 608264 | tf_op jit(solution)/shard_map/ppermute | solution.py:19
  268.1 11.4 %collective-permute-start.22 = (bf16[528,192]{1,0:T(8,128)(2,1)S(1)}, bf16[528,192]{1,0:T(8,128)(2,1)S(1)}, u32[]{:S(2)}, u32[]{:S(2)}) collective-permute-start(bf16[528,192]{1,0:T(8,128)(2,1)S(1)} %get-tuple-element.50), channel_id=1, source_target_pairs={{0,2},{2,4},{4,6},{6,8},{8,10},{10,12},{12,14},{14,16},{16,18},{18... | collective-permute-start | bytes 608264 | tf_op jit(solution)/shard_map/ppermute | solution.py:19
  273.9 9.0 %collective-permute-start.29 = (bf16[528,192]{1,0:T(8,128)(2,1)S(1)}, bf16[528,192]{1,0:T(8,128)(2,1)S(1)}, u32[]{:S(2)}, u32[]{:S(2)}) collective-permute-start(bf16[528,192]{1,0:T(8,128)(2,1)S(1)} %maximum_maximum_fusion.14), channel_id=1, source_target_pairs={{0,30},{2,0},{4,2},{6,4},{8,6},{10,8},{12,10},{14,12},{16,14},{18,... | collective-permute-start | bytes 608264 | tf_op jit(solution)/shard_map/ppermute | solution.py:19
  284.1 33.2 %collective-permute-start.30 = (bf16[2,256,192]{2,1,0:T(8,128)(2,1)S(1)}, bf16[2,256,192]{2,1,0:T(8,128)(2,1)S(1)}, u32[]{:S(2)}, u32[]{:S(2)}) collective-permute-start(bf16[2,256,192]{2,1,0:T(8,128)(2,1)S(1)} %pad_maximum_fusion), channel_id=1, source_target_pairs={{32,0},{64,32},{96,64},{128,96},{160,128},{192,160},{224,192},{256... | collective-permute-start | bytes 589832 | tf_op jit(solution)/shard_map/ppermute | solution.py:14
  310.6 6.1 %collective-permute-start.31 = (f32[192]{0:T(256)S(1)}, f32[192]{0:T(256)S(1)}, u32[]{:S(2)}, u32[]{:S(2)}) collective-permute-start(f32[192]{0:T(256)S(1)} %bitcast.354), channel_id=1, source_target_pairs={{0,1},{1,0},{2,3},{3,2},{4,5},{5,4},{6,7},{7,6},{8,9},{9,8},{10,11... | collective-permute-start | bytes 2312 | tf_op jit(solution)/shard_map/ppermute | solution.py:19
  (13 other events, 352.0 us)

commit v3 on v2

--- a/solution.py
+++ b/solution.py
@@ -74,12 +74,13 @@
     backward = wire(own(n - backward_steps))
     for step in range(forward_steps):
         forward = shift(forward, axis, 1)
+        if step < backward_steps:
+            backward = shift(backward, axis, -1)
+            forward, backward = lax.optimization_barrier((forward, backward))
+            if step < backward_steps - 1:
+                backward = wire(add(backward, n - backward_steps + 1 + step))
         if step < forward_steps - 1:
             forward = wire(add(forward, forward_steps - 1 - step))
-        if step < backward_steps:
-            backward = shift(backward, axis, -1)
-            if step < backward_steps - 1:
-                backward = wire(add(backward, n - backward_steps + 1 + step))
     own_main, own_extra = own(0)
     forward_main, forward_extra = unwire(forward)
     backward_main, backward_extra = unwire(backward)

time: 321 us -> 264 us (0.82)
  waiting for transfers between devices: 105 us -> 57.4 us
  other arithmetic: 37.1 us -> 28 us
    ppermute x31, waiting for transfers between devices: 105 us -> 57.4 us  [shift(): lax.ppermute(x, axis, [(i, (i + by) % length) for i in range(length)])]
    ppermute x31, starting transfers between devices: 112 us -> 120 us  [shift(): lax.ppermute(x, axis, [(i, (i + by) % length) for i in range(length)])]
    ppermute x1, starting transfers between devices: 26.5 us -> 19.4 us  [from_behind(): return lax.ppermute(x, axis, pairs)]
    convert_element_type x12 -> x7, other arithmetic: 12.8 us -> 8.6 us  [wire(): main.astype(jnp.bfloat16)]
    convert_element_type x13 -> x7, other arithmetic: 4.29 us -> 0.08 us  [wire(): high = extra.astype(jnp.bfloat16)]
  transfers between devices with their start and end apart: 32 -> 32, of which waited for: 22 -> 23; matrix products, arithmetic and copies ran while one was open for 2% -> 2% of each run, Pallas kernels for 0% -> 0%
where the time goes in v3:
time: 264 us; the launch traced here: 263 us
  starting transfers between devices  139 us (53%)
  waiting for transfers between devices  57.4 us (22%)
  other arithmetic  28 us (11%)
  matrix products  20.6 us (8%)
  local copies, waits for them, and re-layouts  15.5 us (6%)
    ppermute x31, starting transfers between devices, shift(): lax.ppermute(x, axis, [(i, (i + by) % length) for i in range(length)])  120 us
    ppermute x31, waiting for transfers between devices, shift(): lax.ppermute(x, axis, [(i, (i + by) % length) for i in range(length)])  57.4 us
    ppermute x1, starting transfers between devices, from_behind(): return lax.ppermute(x, axis, pairs)  19.4 us
    convert_element_type x7, other arithmetic, wire(): main.astype(jnp.bfloat16)  8.6 us
    dot_general x1, matrix products, local(): jnp.dot(value_gradient, w_value.T, preferred_element_type=jnp.float32)  6.17 us
  transfers between devices with their start and end apart: 32, of which 23 were waited for; matrix products, arithmetic and copies ran while one was open for 2% of the time, Pallas kernels for 0%

profile of v3, /device:TPU:1, one launch (start us, length us, event | category | flops | bytes accessed | tf_op | source)
XLA Modules:
  0.0 262.7 jit_solution(11239541974920918968)
XLA Ops:
  1.8 18.8 %collective-permute-start = (bf16[2,256,192]{1,2,0:T(8,128)(2,1)S(1)}, bf16[2,256,192]{1,2,0:T(8,128)(2,1)S(1)}, u32[]{:S(2)}, u32[]{:S(2)}) collective-permute-start(bf16[2,256,192]{1,2,0:T(8,128)(2,1)S(1)} %pad_maximum_fusion.1), channel_id=1, source_target_pairs={{0,30},{2,0},{4,2},{6,4},{8,6},{10,8},{12,10},{14,12},{16,14},{18,... | collective-permute-start | bytes 589832 | tf_op jit(solution)/shard_map/ppermute | solution.py:19
  26.6 4.6 %collective-permute-start.1 = (bf16[2,256,192]{1,2,0:T(8,128)(2,1)S(1)}, bf16[2,256,192]{1,2,0:T(8,128)(2,1)S(1)}, u32[]{:S(2)}, u32[]{:S(2)}) collective-permute-start(bf16[2,256,192]{1,2,0:T(8,128)(2,1)S(1)} %collective-permute-done), channel_id=1, source_target_pairs={{0,30},{2,0},{4,2},{6,4},{8,6},{10,8},{12,10},{14,12},{16,14},{18,... | collective-permute-start | bytes 589832 | tf_op jit(solution)/shard_map/ppermute | solution.py:19
  34.1 5.3 %collective-permute-start.2 = (bf16[2,256,192]{1,2,0:T(8,128)(2,1)S(1)}, bf16[2,256,192]{1,2,0:T(8,128)(2,1)S(1)}, u32[]{:S(2)}, u32[]{:S(2)}) collective-permute-start(bf16[2,256,192]{1,2,0:T(8,128)(2,1)S(1)} %collective-permute-done.1), channel_id=1, source_target_pairs={{0,30},{2,0},{4,2},{6,4},{8,6},{10,8},{12,10},{14,12},{16,14},{18,... | collective-permute-start | bytes 589832 | tf_op jit(solution)/shard_map/ppermute | solution.py:19
  42.0 5.0 %collective-permute-start.3 = (bf16[2,256,192]{1,2,0:T(8,128)(2,1)S(1)}, bf16[2,256,192]{1,2,0:T(8,128)(2,1)S(1)}, u32[]{:S(2)}, u32[]{:S(2)}) collective-permute-start(bf16[2,256,192]{1,2,0:T(8,128)(2,1)S(1)} %collective-permute-done.2), channel_id=1, source_target_pairs={{0,30},{2,0},{4,2},{6,4},{8,6},{10,8},{12,10},{14,12},{16,14},{18,... | collective-permute-start | bytes 589832 | tf_op jit(solution)/shard_map/ppermute | solution.py:19
  49.6 5.0 %collective-permute-start.4 = (bf16[2,256,192]{1,2,0:T(8,128)(2,1)S(1)}, bf16[2,256,192]{1,2,0:T(8,128)(2,1)S(1)}, u32[]{:S(2)}, u32[]{:S(2)}) collective-permute-start(bf16[2,256,192]{1,2,0:T(8,128)(2,1)S(1)} %collective-permute-done.3), channel_id=1, source_target_pairs={{0,30},{2,0},{4,2},{6,4},{8,6},{10,8},{12,10},{14,12},{16,14},{18,... | collective-permute-start | bytes 589832 | tf_op jit(solution)/shard_map/ppermute | solution.py:19
  57.2 5.0 %collective-permute-start.5 = (bf16[2,256,192]{1,2,0:T(8,128)(2,1)S(1)}, bf16[2,256,192]{1,2,0:T(8,128)(2,1)S(1)}, u32[]{:S(2)}, u32[]{:S(2)}) collective-permute-start(bf16[2,256,192]{1,2,0:T(8,128)(2,1)S(1)} %collective-permute-done.4), channel_id=1, source_target_pairs={{0,30},{2,0},{4,2},{6,4},{8,6},{10,8},{12,10},{14,12},{16,14},{18,... | collective-permute-start | bytes 589832 | tf_op jit(solution)/shard_map/ppermute | solution.py:19
  64.8 5.0 %collective-permute-start.6 = (bf16[2,256,192]{1,2,0:T(8,128)(2,1)S(1)}, bf16[2,256,192]{1,2,0:T(8,128)(2,1)S(1)}, u32[]{:S(2)}, u32[]{:S(2)}) collective-permute-start(bf16[2,256,192]{1,2,0:T(8,128)(2,1)S(1)} %collective-permute-done.5), channel_id=1, source_target_pairs={{0,30},{2,0},{4,2},{6,4},{8,6},{10,8},{12,10},{14,12},{16,14},{18,... | collective-permute-start | bytes 589832 | tf_op jit(solution)/shard_map/ppermute | solution.py:19
  71.8 6.5 %collective-permute-done.13 = bf16[2,256,192]{1,2,0:T(8,128)(2,1)S(1)} collective-permute-done((bf16[2,256,192]{1,2,0:T(8,128)(2,1)S(1)}, bf16[2,256,192]{1,2,0:T(8,128)(2,1)S(1)}, u32[]{:S(2)}, u32[]{:S(2)}) %collective-permute-start.13) | collective-permute-done | bytes 196640 | tf_op jit(solution)/shard_map/ppermute | solution.py:19
  80.3 7.8 %collective-permute-done.14 = bf16[2,256,192]{1,2,0:T(8,128)(2,1)S(1)} collective-permute-done((bf16[2,256,192]{1,2,0:T(8,128)(2,1)S(1)}, bf16[2,256,192]{1,2,0:T(8,128)(2,1)S(1)}, u32[]{:S(2)}, u32[]{:S(2)}) %collective-permute-start.14) | collective-permute-done | bytes 196640 | tf_op jit(solution)/shard_map/ppermute | solution.py:19
  89.1 3.0 %fusion = (f32[16,256,192]{1,2,0:T(8,128)}, bf16[16,1,256,192]{2,3,0,1:T(8,128)(2,1)}) fusion(bf16[32,2,256,192]{2,3,0,1:T(8,128)(2,1)S(1)} %bitcast_dynamic-update-slice_fusion.31, s32[]{:T(128)S(6)} %select_n.194, s32[]{:T(128)S(6)} %add.522), kind=kLoop, calls=%fused_computation.41 | loop fusion | flops 786432 | bytes 7864328 | tf_op jit(solution)/shard_map/convert_element_type | solution.py:119
  92.7 3.7 %copy.234 = f32[256,3072]{1,0:T(8,128)} copy(f32[256,3072]{0,1:T(8,128)} %bitcast.327) | data formatting | bytes 6291456 | tf_op jit(solution)/shard_map/convert_element_type | solution.py:119
  104.4 4.4 %convolution_add_fusion.1 = f32[256,3072]{1,0:T(8,128)} fusion(f32[256,3072]{1,0:T(8,128)} %fusion.5, bf16[256,2,128]{0,2,1:T(8,128)(2,1)S(1)} %bitcast.337, bf16[2,256,256]{1,2,0:T(8,128)(2,1)S(1)} %fusion.61, bf16[1,3072,128]{2,1,0:T(8,128)(2,1)S(1)} %copy-done.3), kind=kOutput, calls=%fused_computation.33 | convolution fusion | flops 235700224 | bytes 7471104 | tf_op jit(solution)/shard_map/dot_general | solution.py:190
  108.8 6.2 %multiply_reduce_fusion.1 = (f32[256]{0:T(256)S(1)}, f32[3072]{0:T(1024)S(1)}, f32[256,3072]{1,0:T(8,128)}) fusion(f32[256,3072]{1,0:T(8,128)} %copy.234, f32[256]{0:T(256)} %copy-done.14, f32[3072]{0:T(1024)S(1)} %bitcast.342, f32[256,3072]{1,0:T(8,128)} %convolution_add_fusion.1, bf16[1,3072,128]{2,1,0:T(8,128)(2,1)} %param.17, ...), kind=kOutput, calls=%fused_computation.36 | convolution fusion | flops 240939776 | bytes 10975232 | tf_op jit(solution)/shard_map/dot_general | solution.py:191
  115.4 4.9 %multiply_convert_fusion = bf16[256,3072]{1,0:T(8,128)(2,1)} fusion(f32[256,3072]{1,0:T(8,128)} %get-tuple-element.119, f32[256,3072]{1,0:T(8,128)} %copy.234, f32[256]{0:T(256)S(1)} %broadcast_multiply_fusion, f32[256]{0:T(256)S(1)} %copy-done.15, f32[3072]{0:T(1024)S(1)} %bitcast.343), kind=kLoop, calls=%fused_computation.35 | loop fusion | flops 4718592 | bytes 7878656 | tf_op jit(solution)/shard_map/convert_element_type | solution.py:196
  122.1 2.5 copy.236
  124.6 3.7 %fusion.3 = f32[256,3072]{0,1} fusion(bf16[256,256]{0,1:T(8,128)(2,1)S(1)} %bitcast.341, bf16[1,256,3072]{2,1,0:T(8,128)(2,1)} %param.18), kind=kOutput, calls=%fused_computation.44 | convolution fusion | flops 402653184 | bytes 4849664
  128.3 4.3 %copy.228 = bf16[256,16,192]{2,0,1:T(8,128)(2,1)} copy(f32[256,16,192]{0,2,1:T(8,128)} %bitcast.323) | data formatting | bytes 4718592 | tf_op jit(solution)/shard_map/lc,cmf->mlf/dot_general | solution.py:158
  135.9 4.6 %collective-permute-start.16 = (bf16[528,192]{1,0:T(8,128)(2,1)S(1)}, bf16[528,192]{1,0:T(8,128)(2,1)S(1)}, u32[]{:S(2)}, u32[]{:S(2)}) collective-permute-start(bf16[528,192]{1,0:T(8,128)(2,1)S(1)} %get-tuple-element.113), channel_id=1, source_target_pairs={{0,30},{2,0},{4,2},{6,4},{8,6},{10,8},{12,10},{14,12},{16,14},{18,... | collective-permute-start | bytes 608264 | tf_op jit(solution)/shard_map/ppermute | solution.py:19
  147.3 5.0 %collective-permute-start.18 = (bf16[528,192]{1,0:T(8,128)(2,1)S(1)}, bf16[528,192]{1,0:T(8,128)(2,1)S(1)}, u32[]{:S(2)}, u32[]{:S(2)}) collective-permute-start(bf16[528,192]{1,0:T(8,128)(2,1)S(1)} %get-tuple-element.111), channel_id=1, source_target_pairs={{0,30},{2,0},{4,2},{6,4},{8,6},{10,8},{12,10},{14,12},{16,14},{18,... | collective-permute-start | bytes 608264 | tf_op jit(solution)/shard_map/ppermute | solution.py:19
  152.3 2.6 collective-permute-done.17
  160.1 5.2 %collective-permute-start.20 = (bf16[528,192]{1,0:T(8,128)(2,1)S(1)}, bf16[528,192]{1,0:T(8,128)(2,1)S(1)}, u32[]{:S(2)}, u32[]{:S(2)}) collective-permute-start(bf16[528,192]{1,0:T(8,128)(2,1)S(1)} %get-tuple-element.109), channel_id=1, source_target_pairs={{0,30},{2,0},{4,2},{6,4},{8,6},{10,8},{12,10},{14,12},{16,14},{18,... | collective-permute-start | bytes 608264 | tf_op jit(solution)/shard_map/ppermute | solution.py:19
  165.3 3.5 %collective-permute-done.19 = bf16[528,192]{1,0:T(8,128)(2,1)S(1)} collective-permute-done((bf16[528,192]{1,0:T(8,128)(2,1)S(1)}, bf16[528,192]{1,0:T(8,128)(2,1)S(1)}, u32[]{:S(2)}, u32[]{:S(2)}) %collective-permute-start.19) | collective-permute-done | bytes 202784 | tf_op jit(solution)/shard_map/ppermute | solution.py:19
  173.9 5.0 %collective-permute-start.22 = (bf16[528,192]{1,0:T(8,128)(2,1)S(1)}, bf16[528,192]{1,0:T(8,128)(2,1)S(1)}, u32[]{:S(2)}, u32[]{:S(2)}) collective-permute-start(bf16[528,192]{1,0:T(8,128)(2,1)S(1)} %get-tuple-element.107), channel_id=1, source_target_pairs={{0,30},{2,0},{4,2},{6,4},{8,6},{10,8},{12,10},{14,12},{16,14},{18,... | collective-permute-start | bytes 608264 | tf_op jit(solution)/shard_map/ppermute | solution.py:19
  179.0 5.0 %collective-permute-done.21 = bf16[528,192]{1,0:T(8,128)(2,1)S(1)} collective-permute-done((bf16[528,192]{1,0:T(8,128)(2,1)S(1)}, bf16[528,192]{1,0:T(8,128)(2,1)S(1)}, u32[]{:S(2)}, u32[]{:S(2)}) %collective-permute-start.21) | collective-permute-done | bytes 202784 | tf_op jit(solution)/shard_map/ppermute | solution.py:19
  188.3 5.3 %collective-permute-start.24 = (bf16[528,192]{1,0:T(8,128)(2,1)S(1)}, bf16[528,192]{1,0:T(8,128)(2,1)S(1)}, u32[]{:S(2)}, u32[]{:S(2)}) collective-permute-start(bf16[528,192]{1,0:T(8,128)(2,1)S(1)} %get-tuple-element.105), channel_id=1, source_target_pairs={{0,30},{2,0},{4,2},{6,4},{8,6},{10,8},{12,10},{14,12},{16,14},{18,... | collective-permute-start | bytes 608264 | tf_op jit(solution)/shard_map/ppermute | solution.py:19
  193.7 4.2 %collective-permute-done.23 = bf16[528,192]{1,0:T(8,128)(2,1)S(1)} collective-permute-done((bf16[528,192]{1,0:T(8,128)(2,1)S(1)}, bf16[528,192]{1,0:T(8,128)(2,1)S(1)}, u32[]{:S(2)}, u32[]{:S(2)}) %collective-permute-start.23) | collective-permute-done | bytes 202784 | tf_op jit(solution)/shard_map/ppermute | solution.py:19
  202.2 5.3 %collective-permute-start.26 = (bf16[528,192]{1,0:T(8,128)(2,1)S(1)}, bf16[528,192]{1,0:T(8,128)(2,1)S(1)}, u32[]{:S(2)}, u32[]{:S(2)}) collective-permute-start(bf16[528,192]{1,0:T(8,128)(2,1)S(1)} %get-tuple-element.103), channel_id=1, source_target_pairs={{0,30},{2,0},{4,2},{6,4},{8,6},{10,8},{12,10},{14,12},{16,14},{18,... | collective-permute-start | bytes 608264 | tf_op jit(solution)/shard_map/ppermute | solution.py:19
  207.5 3.2 %collective-permute-done.25 = bf16[528,192]{1,0:T(8,128)(2,1)S(1)} collective-permute-done((bf16[528,192]{1,0:T(8,128)(2,1)S(1)}, bf16[528,192]{1,0:T(8,128)(2,1)S(1)}, u32[]{:S(2)}, u32[]{:S(2)}) %collective-permute-start.25) | collective-permute-done | bytes 202784 | tf_op jit(solution)/shard_map/ppermute | solution.py:19
  215.1 5.3 %collective-permute-start.28 = (bf16[528,192]{1,0:T(8,128)(2,1)S(1)}, bf16[528,192]{1,0:T(8,128)(2,1)S(1)}, u32[]{:S(2)}, u32[]{:S(2)}) collective-permute-start(bf16[528,192]{1,0:T(8,128)(2,1)S(1)} %get-tuple-element.101), channel_id=1, source_target_pairs={{0,30},{2,0},{4,2},{6,4},{8,6},{10,8},{12,10},{14,12},{16,14},{18,... | collective-permute-start | bytes 608264 | tf_op jit(solution)/shard_map/ppermute | solution.py:19
  227.2 6.7 %collective-permute-done.29 = bf16[528,192]{1,0:T(8,128)(2,1)S(1)} collective-permute-done((bf16[528,192]{1,0:T(8,128)(2,1)S(1)}, bf16[528,192]{1,0:T(8,128)(2,1)S(1)}, u32[]{:S(2)}, u32[]{:S(2)}) %collective-permute-start.29) | collective-permute-done | bytes 202784 | tf_op jit(solution)/shard_map/ppermute | solution.py:19
  235.1 19.4 %collective-permute-start.30 = (bf16[2,256,192]{2,1,0:T(8,128)(2,1)S(1)}, bf16[2,256,192]{2,1,0:T(8,128)(2,1)S(1)}, u32[]{:S(2)}, u32[]{:S(2)}) collective-permute-start(bf16[2,256,192]{2,1,0:T(8,128)(2,1)S(1)} %pad_maximum_fusion), channel_id=1, source_target_pairs={{32,0},{64,32},{96,64},{128,96},{160,128},{192,160},{224,192},{256... | collective-permute-start | bytes 589832 | tf_op jit(solution)/shard_map/ppermute | solution.py:14
  254.5 4.6 %collective-permute-start.31 = (f32[192]{0:T(256)S(1)}, f32[192]{0:T(256)S(1)}, u32[]{:S(2)}, u32[]{:S(2)}) collective-permute-start(f32[192]{0:T(256)S(1)} %bitcast.344), channel_id=1, source_target_pairs={{0,1},{1,0},{2,3},{3,2},{4,5},{5,4},{6,7},{7,6},{8,9},{9,8},{10,11... | collective-permute-start | bytes 2312 | tf_op jit(solution)/shard_map/ppermute | solution.py:19
  (178 shorter events, 79.9 us)
Async XLA Ops:
  1.8 24.8 %collective-permute-start = (bf16[2,256,192]{1,2,0:T(8,128)(2,1)S(1)}, bf16[2,256,192]{1,2,0:T(8,128)(2,1)S(1)}, u32[]{:S(2)}, u32[]{:S(2)}) collective-permute-start(bf16[2,256,192]{1,2,0:T(8,128)(2,1)S(1)} %pad_maximum_fusion.1), channel_id=1, source_target_pairs={{0,30},{2,0},{4,2},{6,4},{8,6},{10,8},{12,10},{14,12},{16,14},{18,... | collective-permute-start | bytes 589832 | tf_op jit(solution)/shard_map/ppermute | solution.py:19
  20.5 10.6 %collective-permute-start.7 = (bf16[2,256,192]{1,2,0:T(8,128)(2,1)S(1)}, bf16[2,256,192]{1,2,0:T(8,128)(2,1)S(1)}, u32[]{:S(2)}, u32[]{:S(2)}) collective-permute-start(bf16[2,256,192]{1,2,0:T(8,128)(2,1)S(1)} %pad_maximum_fusion.1), channel_id=1, source_target_pairs={{0,2},{2,4},{4,6},{6,8},{8,10},{10,12},{12,14},{14,16},{16,18},{18... | collective-permute-start | bytes 589832 | tf_op jit(solution)/shard_map/ppermute | solution.py:19
  26.6 7.5 %collective-permute-start.1 = (bf16[2,256,192]{1,2,0:T(8,128)(2,1)S(1)}, bf16[2,256,192]{1,2,0:T(8,128)(2,1)S(1)}, u32[]{:S(2)}, u32[]{:S(2)}) collective-permute-start(bf16[2,256,192]{1,2,0:T(8,128)(2,1)S(1)} %collective-permute-done), channel_id=1, source_target_pairs={{0,30},{2,0},{4,2},{6,4},{8,6},{10,8},{12,10},{14,12},{16,14},{18,... | collective-permute-start | bytes 589832 | tf_op jit(solution)/shard_map/ppermute | solution.py:19
  31.2 8.2 %collective-permute-start.8 = (bf16[2,256,192]{1,2,0:T(8,128)(2,1)S(1)}, bf16[2,256,192]{1,2,0:T(8,128)(2,1)S(1)}, u32[]{:S(2)}, u32[]{:S(2)}) collective-permute-start(bf16[2,256,192]{1,2,0:T(8,128)(2,1)S(1)} %collective-permute-done.7), channel_id=1, source_target_pairs={{0,2},{2,4},{4,6},{6,8},{8,10},{10,12},{12,14},{14,16},{16,18},{18... | collective-permute-start | bytes 589832 | tf_op jit(solution)/shard_map/ppermute | solution.py:19
  34.1 7.9 %collective-permute-start.2 = (bf16[2,256,192]{1,2,0:T(8,128)(2,1)S(1)}, bf16[2,256,192]{1,2,0:T(8,128)(2,1)S(1)}, u32[]{:S(2)}, u32[]{:S(2)}) collective-permute-start(bf16[2,256,192]{1,2,0:T(8,128)(2,1)S(1)} %collective-permute-done.1), channel_id=1, source_target_pairs={{0,30},{2,0},{4,2},{6,4},{8,6},{10,8},{12,10},{14,12},{16,14},{18,... | collective-permute-start | bytes 589832 | tf_op jit(solution)/shard_map/ppermute | solution.py:19
  39.4 7.6 %collective-permute-start.9 = (bf16[2,256,192]{1,2,0:T(8,128)(2,1)S(1)}, bf16[2,256,192]{1,2,0:T(8,128)(2,1)S(1)}, u32[]{:S(2)}, u32[]{:S(2)}) collective-permute-start(bf16[2,256,192]{1,2,0:T(8,128)(2,1)S(1)} %collective-permute-done.8), channel_id=1, source_target_pairs={{0,2},{2,4},{4,6},{6,8},{8,10},{10,12},{12,14},{14,16},{16,18},{18... | collective-permute-start | bytes 589832 | tf_op jit(solution)/shard_map/ppermute | solution.py:19
  42.0 7.6 %collective-permute-start.3 = (bf16[2,256,192]{1,2,0:T(8,128)(2,1)S(1)}, bf16[2,256,192]{1,2,0:T(8,128)(2,1)S(1)}, u32[]{:S(2)}, u32[]{:S(2)}) collective-permute-start(bf16[2,256,192]{1,2,0:T(8,128)(2,1)S(1)} %collective-permute-done.2), channel_id=1, source_target_pairs={{0,30},{2,0},{4,2},{6,4},{8,6},{10,8},{12,10},{14,12},{16,14},{18,... | collective-permute-start | bytes 589832 | tf_op jit(solution)/shard_map/ppermute | solution.py:19
  47.0 7.6 %collective-permute-start.10 = (bf16[2,256,192]{1,2,0:T(8,128)(2,1)S(1)}, bf16[2,256,192]{1,2,0:T(8,128)(2,1)S(1)}, u32[]{:S(2)}, u32[]{:S(2)}) collective-permute-start(bf16[2,256,192]{1,2,0:T(8,128)(2,1)S(1)} %collective-permute-done.9), channel_id=1, source_target_pairs={{0,2},{2,4},{4,6},{6,8},{8,10},{10,12},{12,14},{14,16},{16,18},{18... | collective-permute-start | bytes 589832 | tf_op jit(solution)/shard_map/ppermute | solution.py:19
  49.6 7.6 %collective-permute-start.4 = (bf16[2,256,192]{1,2,0:T(8,128)(2,1)S(1)}, bf16[2,256,192]{1,2,0:T(8,128)(2,1)S(1)}, u32[]{:S(2)}, u32[]{:S(2)}) collective-permute-start(bf16[2,256,192]{1,2,0:T(8,128)(2,1)S(1)} %collective-permute-done.3), channel_id=1, source_target_pairs={{0,30},{2,0},{4,2},{6,4},{8,6},{10,8},{12,10},{14,12},{16,14},{18,... | collective-permute-start | bytes 589832 | tf_op jit(solution)/shard_map/ppermute | solution.py:19
  54.7 7.6 %collective-permute-start.11 = (bf16[2,256,192]{1,2,0:T(8,128)(2,1)S(1)}, bf16[2,256,192]{1,2,0:T(8,128)(2,1)S(1)}, u32[]{:S(2)}, u32[]{:S(2)}) collective-permute-start(bf16[2,256,192]{1,2,0:T(8,128)(2,1)S(1)} %collective-permute-done.10), channel_id=1, source_target_pairs={{0,2},{2,4},{4,6},{6,8},{8,10},{10,12},{12,14},{14,16},{16,18},{18... | collective-permute-start | bytes 589832 | tf_op jit(solution)/shard_map/ppermute | solution.py:19
  57.2 7.6 %collective-permute-start.5 = (bf16[2,256,192]{1,2,0:T(8,128)(2,1)S(1)}, bf16[2,256,192]{1,2,0:T(8,128)(2,1)S(1)}, u32[]{:S(2)}, u32[]{:S(2)}) collective-permute-start(bf16[2,256,192]{1,2,0:T(8,128)(2,1)S(1)} %collective-permute-done.4), channel_id=1, source_target_pairs={{0,30},{2,0},{4,2},{6,4},{8,6},{10,8},{12,10},{14,12},{16,14},{18,... | collective-permute-start | bytes 589832 | tf_op jit(solution)/shard_map/ppermute | solution.py:19
  62.3 7.6 %collective-permute-start.12 = (bf16[2,256,192]{1,2,0:T(8,128)(2,1)S(1)}, bf16[2,256,192]{1,2,0:T(8,128)(2,1)S(1)}, u32[]{:S(2)}, u32[]{:S(2)}) collective-permute-start(bf16[2,256,192]{1,2,0:T(8,128)(2,1)S(1)} %collective-permute-done.11), channel_id=1, source_target_pairs={{0,2},{2,4},{4,6},{6,8},{8,10},{10,12},{12,14},{14,16},{16,18},{18... | collective-permute-start | bytes 589832 | tf_op jit(solution)/shard_map/ppermute | solution.py:19
  64.8 15.4 %collective-permute-start.6 = (bf16[2,256,192]{1,2,0:T(8,128)(2,1)S(1)}, bf16[2,256,192]{1,2,0:T(8,128)(2,1)S(1)}, u32[]{:S(2)}, u32[]{:S(2)}) collective-permute-start(bf16[2,256,192]{1,2,0:T(8,128)(2,1)S(1)} %collective-permute-done.5), channel_id=1, source_target_pairs={{0,30},{2,0},{4,2},{6,4},{8,6},{10,8},{12,10},{14,12},{16,14},{18,... | collective-permute-start | bytes 589832 | tf_op jit(solution)/shard_map/ppermute | solution.py:19
  69.9 8.5 %collective-permute-start.13 = (bf16[2,256,192]{1,2,0:T(8,128)(2,1)S(1)}, bf16[2,256,192]{1,2,0:T(8,128)(2,1)S(1)}, u32[]{:S(2)}, u32[]{:S(2)}) collective-permute-start(bf16[2,256,192]{1,2,0:T(8,128)(2,1)S(1)} %collective-permute-done.12), channel_id=1, source_target_pairs={{0,2},{2,4},{4,6},{6,8},{8,10},{10,12},{12,14},{14,16},{16,18},{18... | collective-permute-start | bytes 589832 | tf_op jit(solution)/shard_map/ppermute | solution.py:19
  78.3 9.7 %collective-permute-start.14 = (bf16[2,256,192]{1,2,0:T(8,128)(2,1)S(1)}, bf16[2,256,192]{1,2,0:T(8,128)(2,1)S(1)}, u32[]{:S(2)}, u32[]{:S(2)}) collective-permute-start(bf16[2,256,192]{1,2,0:T(8,128)(2,1)S(1)} %collective-permute-done.13), channel_id=1, source_target_pairs={{0,2},{2,4},{4,6},{6,8},{8,10},{10,12},{12,14},{14,16},{16,18},{18... | collective-permute-start | bytes 589832 | tf_op jit(solution)/shard_map/ppermute | solution.py:19
  134.0 8.4 %collective-permute-start.15 = (bf16[528,192]{1,0:T(8,128)(2,1)S(1)}, bf16[528,192]{1,0:T(8,128)(2,1)S(1)}, u32[]{:S(2)}, u32[]{:S(2)}) collective-permute-start(bf16[528,192]{1,0:T(8,128)(2,1)S(1)} %get-tuple-element.114), channel_id=1, source_target_pairs={{0,2},{2,4},{4,6},{6,8},{8,10},{10,12},{12,14},{14,16},{16,18},{18... | collective-permute-start | bytes 608264 | tf_op jit(solution)/shard_map/ppermute | solution.py:19
  135.9 8.0 %collective-permute-start.16 = (bf16[528,192]{1,0:T(8,128)(2,1)S(1)}, bf16[528,192]{1,0:T(8,128)(2,1)S(1)}, u32[]{:S(2)}, u32[]{:S(2)}) collective-permute-start(bf16[528,192]{1,0:T(8,128)(2,1)S(1)} %get-tuple-element.113), channel_id=1, source_target_pairs={{0,30},{2,0},{4,2},{6,4},{8,6},{10,8},{12,10},{14,12},{16,14},{18,... | collective-permute-start | bytes 608264 | tf_op jit(solution)/shard_map/ppermute | solution.py:19
  145.3 9.6 %collective-permute-start.17 = (bf16[528,192]{1,0:T(8,128)(2,1)S(1)}, bf16[528,192]{1,0:T(8,128)(2,1)S(1)}, u32[]{:S(2)}, u32[]{:S(2)}) collective-permute-start(bf16[528,192]{1,0:T(8,128)(2,1)S(1)} %get-tuple-element.112), channel_id=1, source_target_pairs={{0,2},{2,4},{4,6},{6,8},{8,10},{10,12},{12,14},{14,16},{16,18},{18... | collective-permute-start | bytes 608264 | tf_op jit(solution)/shard_map/ppermute | solution.py:19
  147.3 9.4 %collective-permute-start.18 = (bf16[528,192]{1,0:T(8,128)(2,1)S(1)}, bf16[528,192]{1,0:T(8,128)(2,1)S(1)}, u32[]{:S(2)}, u32[]{:S(2)}) collective-permute-start(bf16[528,192]{1,0:T(8,128)(2,1)S(1)} %get-tuple-element.111), channel_id=1, source_target_pairs={{0,30},{2,0},{4,2},{6,4},{8,6},{10,8},{12,10},{14,12},{16,14},{18,... | collective-permute-start | bytes 608264 | tf_op jit(solution)/shard_map/ppermute | solution.py:19
  158.1 10.6 %collective-permute-start.19 = (bf16[528,192]{1,0:T(8,128)(2,1)S(1)}, bf16[528,192]{1,0:T(8,128)(2,1)S(1)}, u32[]{:S(2)}, u32[]{:S(2)}) collective-permute-start(bf16[528,192]{1,0:T(8,128)(2,1)S(1)} %get-tuple-element.110), channel_id=1, source_target_pairs={{0,2},{2,4},{4,6},{6,8},{8,10},{10,12},{12,14},{14,16},{16,18},{18... | collective-permute-start | bytes 608264 | tf_op jit(solution)/shard_map/ppermute | solution.py:19
  160.1 10.5 %collective-permute-start.20 = (bf16[528,192]{1,0:T(8,128)(2,1)S(1)}, bf16[528,192]{1,0:T(8,128)(2,1)S(1)}, u32[]{:S(2)}, u32[]{:S(2)}) collective-permute-start(bf16[528,192]{1,0:T(8,128)(2,1)S(1)} %get-tuple-element.109), channel_id=1, source_target_pairs={{0,30},{2,0},{4,2},{6,4},{8,6},{10,8},{12,10},{14,12},{16,14},{18,... | collective-permute-start | bytes 608264 | tf_op jit(solution)/shard_map/ppermute | solution.py:19
  172.0 12.0 %collective-permute-start.21 = (bf16[528,192]{1,0:T(8,128)(2,1)S(1)}, bf16[528,192]{1,0:T(8,128)(2,1)S(1)}, u32[]{:S(2)}, u32[]{:S(2)}) collective-permute-start(bf16[528,192]{1,0:T(8,128)(2,1)S(1)} %get-tuple-element.108), channel_id=1, source_target_pairs={{0,2},{2,4},{4,6},{6,8},{8,10},{10,12},{12,14},{14,16},{16,18},{18... | collective-permute-start | bytes 608264 | tf_op jit(solution)/shard_map/ppermute | solution.py:19
  173.9 11.0 %collective-permute-start.22 = (bf16[528,192]{1,0:T(8,128)(2,1)S(1)}, bf16[528,192]{1,0:T(8,128)(2,1)S(1)}, u32[]{:S(2)}, u32[]{:S(2)}) collective-permute-start(bf16[528,192]{1,0:T(8,128)(2,1)S(1)} %get-tuple-element.107), channel_id=1, source_target_pairs={{0,30},{2,0},{4,2},{6,4},{8,6},{10,8},{12,10},{14,12},{16,14},{18,... | collective-permute-start | bytes 608264 | tf_op jit(solution)/shard_map/ppermute | solution.py:19
  186.4 11.5 %collective-permute-start.23 = (bf16[528,192]{1,0:T(8,128)(2,1)S(1)}, bf16[528,192]{1,0:T(8,128)(2,1)S(1)}, u32[]{:S(2)}, u32[]{:S(2)}) collective-permute-start(bf16[528,192]{1,0:T(8,128)(2,1)S(1)} %get-tuple-element.106), channel_id=1, source_target_pairs={{0,2},{2,4},{4,6},{6,8},{8,10},{10,12},{12,14},{14,16},{16,18},{18... | collective-permute-start | bytes 608264 | tf_op jit(solution)/shard_map/ppermute | solution.py:19
  188.3 10.4 %collective-permute-start.24 = (bf16[528,192]{1,0:T(8,128)(2,1)S(1)}, bf16[528,192]{1,0:T(8,128)(2,1)S(1)}, u32[]{:S(2)}, u32[]{:S(2)}) collective-permute-start(bf16[528,192]{1,0:T(8,128)(2,1)S(1)} %get-tuple-element.105), channel_id=1, source_target_pairs={{0,30},{2,0},{4,2},{6,4},{8,6},{10,8},{12,10},{14,12},{16,14},{18,... | collective-permute-start | bytes 608264 | tf_op jit(solution)/shard_map/ppermute | solution.py:19
  200.2 10.5 %collective-permute-start.25 = (bf16[528,192]{1,0:T(8,128)(2,1)S(1)}, bf16[528,192]{1,0:T(8,128)(2,1)S(1)}, u32[]{:S(2)}, u32[]{:S(2)}) collective-permute-start(bf16[528,192]{1,0:T(8,128)(2,1)S(1)} %get-tuple-element.104), channel_id=1, source_target_pairs={{0,2},{2,4},{4,6},{6,8},{8,10},{10,12},{12,14},{14,16},{16,18},{18... | collective-permute-start | bytes 608264 | tf_op jit(solution)/shard_map/ppermute | solution.py:19
  202.2 9.5 %collective-permute-start.26 = (bf16[528,192]{1,0:T(8,128)(2,1)S(1)}, bf16[528,192]{1,0:T(8,128)(2,1)S(1)}, u32[]{:S(2)}, u32[]{:S(2)}) collective-permute-start(bf16[528,192]{1,0:T(8,128)(2,1)S(1)} %get-tuple-element.103), channel_id=1, source_target_pairs={{0,30},{2,0},{4,2},{6,4},{8,6},{10,8},{12,10},{14,12},{16,14},{18,... | collective-permute-start | bytes 608264 | tf_op jit(solution)/shard_map/ppermute | solution.py:19
  213.2 9.6 %collective-permute-start.27 = (bf16[528,192]{1,0:T(8,128)(2,1)S(1)}, bf16[528,192]{1,0:T(8,128)(2,1)S(1)}, u32[]{:S(2)}, u32[]{:S(2)}) collective-permute-start(bf16[528,192]{1,0:T(8,128)(2,1)S(1)} %get-tuple-element.102), channel_id=1, source_target_pairs={{0,2},{2,4},{4,6},{6,8},{8,10},{10,12},{12,14},{14,16},{16,18},{18... | collective-permute-start | bytes 608264 | tf_op jit(solution)/shard_map/ppermute | solution.py:19
  215.1 8.7 %collective-permute-start.28 = (bf16[528,192]{1,0:T(8,128)(2,1)S(1)}, bf16[528,192]{1,0:T(8,128)(2,1)S(1)}, u32[]{:S(2)}, u32[]{:S(2)}) collective-permute-start(bf16[528,192]{1,0:T(8,128)(2,1)S(1)} %get-tuple-element.101), channel_id=1, source_target_pairs={{0,30},{2,0},{4,2},{6,4},{8,6},{10,8},{12,10},{14,12},{16,14},{18,... | collective-permute-start | bytes 608264 | tf_op jit(solution)/shard_map/ppermute | solution.py:19
  225.0 8.9 %collective-permute-start.29 = (bf16[528,192]{1,0:T(8,128)(2,1)S(1)}, bf16[528,192]{1,0:T(8,128)(2,1)S(1)}, u32[]{:S(2)}, u32[]{:S(2)}) collective-permute-start(bf16[528,192]{1,0:T(8,128)(2,1)S(1)} %maximum_maximum_fusion.14), channel_id=1, source_target_pairs={{0,2},{2,4},{4,6},{6,8},{8,10},{10,12},{12,14},{14,16},{16,18},{18... | collective-permute-start | bytes 608264 | tf_op jit(solution)/shard_map/ppermute | solution.py:19
  235.1 26.1 %collective-permute-start.30 = (bf16[2,256,192]{2,1,0:T(8,128)(2,1)S(1)}, bf16[2,256,192]{2,1,0:T(8,128)(2,1)S(1)}, u32[]{:S(2)}, u32[]{:S(2)}) collective-permute-start(bf16[2,256,192]{2,1,0:T(8,128)(2,1)S(1)} %pad_maximum_fusion), channel_id=1, source_target_pairs={{32,0},{64,32},{96,64},{128,96},{160,128},{192,160},{224,192},{256... | collective-permute-start | bytes 589832 | tf_op jit(solution)/shard_map/ppermute | solution.py:14
  254.5 6.1 %collective-permute-start.31 = (f32[192]{0:T(256)S(1)}, f32[192]{0:T(256)S(1)}, u32[]{:S(2)}, u32[]{:S(2)}) collective-permute-start(f32[192]{0:T(256)S(1)} %bitcast.344), channel_id=1, source_target_pairs={{0,1},{1,0},{2,3},{3,2},{4,5},{5,4},{6,7},{7,6},{8,9},{9,8},{10,11... | collective-permute-start | bytes 2312 | tf_op jit(solution)/shard_map/ppermute | solution.py:19
  (16 other events, 342.4 us)

commit v4 on v2

--- a/solution.py
+++ b/solution.py
@@ -73,13 +73,19 @@
     forward = wire(own(forward_steps))
     backward = wire(own(n - backward_steps))
     for step in range(forward_steps):
-        forward = shift(forward, axis, 1)
+        received = shift(forward, axis, 1)
         if step < forward_steps - 1:
-            forward = wire(add(forward, forward_steps - 1 - step))
+            received = lax.optimization_barrier((received, backward))[0]
+            forward = wire(add(received, forward_steps - 1 - step))
+        else:
+            forward = received
         if step < backward_steps:
-            backward = shift(backward, axis, -1)
+            received = shift(backward, axis, -1)
+            received = lax.optimization_barrier((received, forward))[0]
             if step < backward_steps - 1:
-                backward = wire(add(backward, n - backward_steps + 1 + step))
+                backward = wire(add(received, n - backward_steps + 1 + step))
+            else:
+                backward = received
     own_main, own_extra = own(0)
     forward_main, forward_extra = unwire(forward)
     backward_main, backward_extra = unwire(backward)

time: 321 us -> 239 us (0.74)
  waiting for transfers between devices: 105 us -> 41.5 us
  other arithmetic: 37.1 us -> 22.1 us
    ppermute x31, waiting for transfers between devices: 105 us -> 41.5 us  [shift(): lax.ppermute(x, axis, [(i, (i + by) % length) for i in range(length)])]
    convert_element_type x12 -> x13, other arithmetic: 12.8 us -> 2.04 us  [wire(): main.astype(jnp.bfloat16)]
    ppermute x1, starting transfers between devices: 26.5 us -> 19.5 us  [from_behind(): return lax.ppermute(x, axis, pairs)]
    ppermute x31, starting transfers between devices: 112 us -> 117 us  [shift(): lax.ppermute(x, axis, [(i, (i + by) % length) for i in range(length)])]
    convert_element_type x13, other arithmetic: 4.29 us -> 0.15 us  [wire(): high = extra.astype(jnp.bfloat16)]
  transfers between devices with their start and end apart: 32 -> 32, of which waited for: 22 -> 16; matrix products, arithmetic and copies ran while one was open for 2% -> 4% of each run, Pallas kernels for 0% -> 0%
where the time goes in v4:
time: 239 us; the launch traced here: 238 us
  starting transfers between devices  136 us (57%)
  waiting for transfers between devices  41.5 us (17%)
  other arithmetic  22.1 us (9%)
  matrix products  20.5 us (9%)
  local copies, waits for them, and re-layouts  15.6 us (7%)
    ppermute x31, starting transfers between devices, shift(): lax.ppermute(x, axis, [(i, (i + by) % length) for i in range(length)])  117 us
    ppermute x31, waiting for transfers between devices, shift(): lax.ppermute(x, axis, [(i, (i + by) % length) for i in range(length)])  41.5 us
    ppermute x1, starting transfers between devices, from_behind(): return lax.ppermute(x, axis, pairs)  19.5 us
    dot_general x1, matrix products, local(): jnp.dot(value_gradient, w_value.T, preferred_element_type=jnp.float32)  6.17 us
    convert_element_type x1, other arithmetic, local(): ((weighted - unit_rows * row_stat) * inverse).astype(jnp.bfloat16)  4.92 us
  transfers between devices with their start and end apart: 32, of which 16 were waited for; matrix products, arithmetic and copies ran while one was open for 4% of the time, Pallas kernels for 0%

profile of v4, /device:TPU:1, one launch (start us, length us, event | category | flops | bytes accessed | tf_op | source)
XLA Modules:
  0.0 237.9 jit_solution(2023931508166680448)
XLA Ops:
  1.8 18.8 %collective-permute-start = (bf16[2,256,192]{1,2,0:T(8,128)(2,1)S(1)}, bf16[2,256,192]{1,2,0:T(8,128)(2,1)S(1)}, u32[]{:S(2)}, u32[]{:S(2)}) collective-permute-start(bf16[2,256,192]{1,2,0:T(8,128)(2,1)S(1)} %pad_maximum_fusion.1), channel_id=1, source_target_pairs={{0,30},{2,0},{4,2},{6,4},{8,6},{10,8},{12,10},{14,12},{16,14},{18,... | collective-permute-start | bytes 589832 | tf_op jit(solution)/shard_map/ppermute | solution.py:19
  26.6 4.6 %collective-permute-start.1 = (bf16[2,256,192]{1,2,0:T(8,128)(2,1)S(1)}, bf16[2,256,192]{1,2,0:T(8,128)(2,1)S(1)}, u32[]{:S(2)}, u32[]{:S(2)}) collective-permute-start(bf16[2,256,192]{1,2,0:T(8,128)(2,1)S(1)} %collective-permute-done), channel_id=1, source_target_pairs={{0,30},{2,0},{4,2},{6,4},{8,6},{10,8},{12,10},{14,12},{16,14},{18,... | collective-permute-start | bytes 589832 | tf_op jit(solution)/shard_map/ppermute | solution.py:19
  34.1 5.3 %collective-permute-start.2 = (bf16[2,256,192]{1,2,0:T(8,128)(2,1)S(1)}, bf16[2,256,192]{1,2,0:T(8,128)(2,1)S(1)}, u32[]{:S(2)}, u32[]{:S(2)}) collective-permute-start(bf16[2,256,192]{1,2,0:T(8,128)(2,1)S(1)} %collective-permute-done.1), channel_id=1, source_target_pairs={{0,30},{2,0},{4,2},{6,4},{8,6},{10,8},{12,10},{14,12},{16,14},{18,... | collective-permute-start | bytes 589832 | tf_op jit(solution)/shard_map/ppermute | solution.py:19
  42.0 5.0 %collective-permute-start.3 = (bf16[2,256,192]{1,2,0:T(8,128)(2,1)S(1)}, bf16[2,256,192]{1,2,0:T(8,128)(2,1)S(1)}, u32[]{:S(2)}, u32[]{:S(2)}) collective-permute-start(bf16[2,256,192]{1,2,0:T(8,128)(2,1)S(1)} %collective-permute-done.2), channel_id=1, source_target_pairs={{0,30},{2,0},{4,2},{6,4},{8,6},{10,8},{12,10},{14,12},{16,14},{18,... | collective-permute-start | bytes 589832 | tf_op jit(solution)/shard_map/ppermute | solution.py:19
  49.6 5.0 %collective-permute-start.4 = (bf16[2,256,192]{1,2,0:T(8,128)(2,1)S(1)}, bf16[2,256,192]{1,2,0:T(8,128)(2,1)S(1)}, u32[]{:S(2)}, u32[]{:S(2)}) collective-permute-start(bf16[2,256,192]{1,2,0:T(8,128)(2,1)S(1)} %collective-permute-done.3), channel_id=1, source_target_pairs={{0,30},{2,0},{4,2},{6,4},{8,6},{10,8},{12,10},{14,12},{16,14},{18,... | collective-permute-start | bytes 589832 | tf_op jit(solution)/shard_map/ppermute | solution.py:19
  57.2 5.0 %collective-permute-start.5 = (bf16[2,256,192]{1,2,0:T(8,128)(2,1)S(1)}, bf16[2,256,192]{1,2,0:T(8,128)(2,1)S(1)}, u32[]{:S(2)}, u32[]{:S(2)}) collective-permute-start(bf16[2,256,192]{1,2,0:T(8,128)(2,1)S(1)} %collective-permute-done.4), channel_id=1, source_target_pairs={{0,30},{2,0},{4,2},{6,4},{8,6},{10,8},{12,10},{14,12},{16,14},{18,... | collective-permute-start | bytes 589832 | tf_op jit(solution)/shard_map/ppermute | solution.py:19
  64.8 5.0 %collective-permute-start.6 = (bf16[2,256,192]{1,2,0:T(8,128)(2,1)S(1)}, bf16[2,256,192]{1,2,0:T(8,128)(2,1)S(1)}, u32[]{:S(2)}, u32[]{:S(2)}) collective-permute-start(bf16[2,256,192]{1,2,0:T(8,128)(2,1)S(1)} %collective-permute-done.5), channel_id=1, source_target_pairs={{0,30},{2,0},{4,2},{6,4},{8,6},{10,8},{12,10},{14,12},{16,14},{18,... | collective-permute-start | bytes 589832 | tf_op jit(solution)/shard_map/ppermute | solution.py:19
  71.8 6.5 %collective-permute-done.13 = bf16[2,256,192]{1,2,0:T(8,128)(2,1)S(1)} collective-permute-done((bf16[2,256,192]{1,2,0:T(8,128)(2,1)S(1)}, bf16[2,256,192]{1,2,0:T(8,128)(2,1)S(1)}, u32[]{:S(2)}, u32[]{:S(2)}) %collective-permute-start.13) | collective-permute-done | bytes 196640 | tf_op jit(solution)/shard_map/ppermute | solution.py:19
  80.3 7.8 %collective-permute-done.14 = bf16[2,256,192]{1,2,0:T(8,128)(2,1)S(1)} collective-permute-done((bf16[2,256,192]{1,2,0:T(8,128)(2,1)S(1)}, bf16[2,256,192]{1,2,0:T(8,128)(2,1)S(1)}, u32[]{:S(2)}, u32[]{:S(2)}) %collective-permute-start.14) | collective-permute-done | bytes 196640 | tf_op jit(solution)/shard_map/ppermute | solution.py:19
  89.1 3.0 %fusion = (f32[16,256,192]{1,2,0:T(8,128)}, bf16[16,1,256,192]{2,3,0,1:T(8,128)(2,1)}) fusion(bf16[32,2,256,192]{2,3,0,1:T(8,128)(2,1)S(1)} %bitcast_dynamic-update-slice_fusion.31, s32[]{:T(128)S(6)} %select_n.194, s32[]{:T(128)S(6)} %add.522), kind=kLoop, calls=%fused_computation.41 | loop fusion | flops 786432 | bytes 7864328 | tf_op jit(solution)/shard_map/convert_element_type | solution.py:124
  92.7 3.7 %copy.234 = f32[256,3072]{1,0:T(8,128)} copy(f32[256,3072]{0,1:T(8,128)} %bitcast.339) | data formatting | bytes 6291456 | tf_op jit(solution)/shard_map/convert_element_type | solution.py:124
  96.4 2.0 multiply_convert_fusion.1
  102.1 2.3 fusion.5
  104.4 4.4 %convolution_add_fusion.1 = f32[256,3072]{1,0:T(8,128)} fusion(f32[256,3072]{1,0:T(8,128)} %fusion.5, bf16[256,2,128]{0,2,1:T(8,128)(2,1)S(1)} %bitcast.349, bf16[2,256,256]{1,2,0:T(8,128)(2,1)S(1)} %fusion.61, bf16[1,3072,128]{2,1,0:T(8,128)(2,1)S(1)} %copy-done.5), kind=kOutput, calls=%fused_computation.33 | convolution fusion | flops 235700224 | bytes 7471104 | tf_op jit(solution)/shard_map/dot_general | solution.py:195
  108.8 6.2 %multiply_reduce_fusion.1 = (f32[256]{0:T(256)S(1)}, f32[3072]{0:T(1024)S(1)}, f32[256,3072]{1,0:T(8,128)}) fusion(f32[256,3072]{1,0:T(8,128)} %copy.234, f32[256]{0:T(256)} %copy-done.16, f32[3072]{0:T(1024)S(1)} %bitcast.354, f32[256,3072]{1,0:T(8,128)} %convolution_add_fusion.1, bf16[1,3072,128]{2,1,0:T(8,128)(2,1)} %param.17, ...), kind=kOutput, calls=%fused_computation.36 | convolution fusion | flops 240939776 | bytes 10975232 | tf_op jit(solution)/shard_map/dot_general | solution.py:196
  115.4 4.9 %multiply_convert_fusion = bf16[256,3072]{1,0:T(8,128)(2,1)} fusion(f32[256,3072]{1,0:T(8,128)} %get-tuple-element.83, f32[256,3072]{1,0:T(8,128)} %copy.234, f32[256]{0:T(256)S(1)} %broadcast_multiply_fusion, f32[256]{0:T(256)S(1)} %copy-done.17, f32[3072]{0:T(1024)S(1)} %bitcast.355), kind=kLoop, calls=%fused_computation.35 | loop fusion | flops 4718592 | bytes 7878656 | tf_op jit(solution)/shard_map/convert_element_type | solution.py:201
  122.1 2.5 %copy.236 = bf16[256,16,192]{2,0,1:T(8,128)(2,1)} copy(bf16[256,16,192]{0,2,1:T(8,128)(2,1)S(1)} %bitcast.340) | data formatting | bytes 3145728 | tf_op jit(solution)/shard_map/reshape | solution.py:202
  124.6 3.7 %fusion.3 = f32[256,3072]{0,1} fusion(bf16[256,256]{0,1:T(8,128)(2,1)S(1)} %bitcast.353, bf16[1,256,3072]{2,1,0:T(8,128)(2,1)} %param.18), kind=kOutput, calls=%fused_computation.44 | convolution fusion | flops 402653184 | bytes 4849664
  128.3 4.3 %copy.228 = bf16[256,16,192]{2,0,1:T(8,128)(2,1)} copy(f32[256,16,192]{0,2,1:T(8,128)} %bitcast.335) | data formatting | bytes 4718592 | tf_op jit(solution)/shard_map/lc,cmf->mlf/dot_general | solution.py:163
  136.1 4.8 %collective-permute-start.17 = (bf16[528,192]{1,0:T(8,128)(2,1)S(1)}, bf16[528,192]{1,0:T(8,128)(2,1)S(1)}, u32[]{:S(2)}, u32[]{:S(2)}) collective-permute-start(bf16[528,192]{1,0:T(8,128)(2,1)S(1)} %get-tuple-element.77), channel_id=1, source_target_pairs={{0,30},{2,0},{4,2},{6,4},{8,6},{10,8},{12,10},{14,12},{16,14},{18,... | collective-permute-start | bytes 608264 | tf_op jit(solution)/shard_map/ppermute | solution.py:19
  145.8 4.6 %collective-permute-start.19 = (bf16[528,192]{1,0:T(8,128)(2,1)S(1)}, bf16[528,192]{1,0:T(8,128)(2,1)S(1)}, u32[]{:S(2)}, u32[]{:S(2)}) collective-permute-start(bf16[528,192]{1,0:T(8,128)(2,1)S(1)} %maximum_maximum_fusion.3), channel_id=1, source_target_pairs={{0,30},{2,0},{4,2},{6,4},{8,6},{10,8},{12,10},{14,12},{16,14},{18,... | collective-permute-start | bytes 608264 | tf_op jit(solution)/shard_map/ppermute | solution.py:19
  150.4 4.8 %collective-permute-done.16 = bf16[528,192]{1,0:T(8,128)(2,1)S(1)} collective-permute-done((bf16[528,192]{1,0:T(8,128)(2,1)S(1)}, bf16[528,192]{1,0:T(8,128)(2,1)S(1)}, u32[]{:S(2)}, u32[]{:S(2)}) %collective-permute-start.16) | collective-permute-done | bytes 202784 | tf_op jit(solution)/shard_map/ppermute | solution.py:19
  155.4 2.1 collective-permute-start.18
  157.8 4.6 %collective-permute-start.21 = (bf16[528,192]{1,0:T(8,128)(2,1)S(1)}, bf16[528,192]{1,0:T(8,128)(2,1)S(1)}, u32[]{:S(2)}, u32[]{:S(2)}) collective-permute-start(bf16[528,192]{1,0:T(8,128)(2,1)S(1)} %maximum_maximum_fusion.5), channel_id=1, source_target_pairs={{0,30},{2,0},{4,2},{6,4},{8,6},{10,8},{12,10},{14,12},{16,14},{18,... | collective-permute-start | bytes 608264 | tf_op jit(solution)/shard_map/ppermute | solution.py:19
  162.4 2.8 %collective-permute-done.18 = bf16[528,192]{1,0:T(8,128)(2,1)S(1)} collective-permute-done((bf16[528,192]{1,0:T(8,128)(2,1)S(1)}, bf16[528,192]{1,0:T(8,128)(2,1)S(1)}, u32[]{:S(2)}, u32[]{:S(2)}) %collective-permute-start.18) | collective-permute-done | bytes 202784 | tf_op jit(solution)/shard_map/ppermute | solution.py:19
  167.6 4.6 %collective-permute-start.23 = (bf16[528,192]{1,0:T(8,128)(2,1)S(1)}, bf16[528,192]{1,0:T(8,128)(2,1)S(1)}, u32[]{:S(2)}, u32[]{:S(2)}) collective-permute-start(bf16[528,192]{1,0:T(8,128)(2,1)S(1)} %maximum_maximum_fusion.7), channel_id=1, source_target_pairs={{0,30},{2,0},{4,2},{6,4},{8,6},{10,8},{12,10},{14,12},{16,14},{18,... | collective-permute-start | bytes 608264 | tf_op jit(solution)/shard_map/ppermute | solution.py:19
  176.7 4.6 %collective-permute-start.25 = (bf16[528,192]{1,0:T(8,128)(2,1)S(1)}, bf16[528,192]{1,0:T(8,128)(2,1)S(1)}, u32[]{:S(2)}, u32[]{:S(2)}) collective-permute-start(bf16[528,192]{1,0:T(8,128)(2,1)S(1)} %maximum_maximum_fusion.9), channel_id=1, source_target_pairs={{0,30},{2,0},{4,2},{6,4},{8,6},{10,8},{12,10},{14,12},{16,14},{18,... | collective-permute-start | bytes 608264 | tf_op jit(solution)/shard_map/ppermute | solution.py:19
  185.3 4.6 %collective-permute-start.27 = (bf16[528,192]{1,0:T(8,128)(2,1)S(1)}, bf16[528,192]{1,0:T(8,128)(2,1)S(1)}, u32[]{:S(2)}, u32[]{:S(2)}) collective-permute-start(bf16[528,192]{1,0:T(8,128)(2,1)S(1)} %maximum_maximum_fusion.11), channel_id=1, source_target_pairs={{0,30},{2,0},{4,2},{6,4},{8,6},{10,8},{12,10},{14,12},{16,14},{18,... | collective-permute-start | bytes 608264 | tf_op jit(solution)/shard_map/ppermute | solution.py:19
  194.0 4.6 %collective-permute-start.29 = (bf16[528,192]{1,0:T(8,128)(2,1)S(1)}, bf16[528,192]{1,0:T(8,128)(2,1)S(1)}, u32[]{:S(2)}, u32[]{:S(2)}) collective-permute-start(bf16[528,192]{1,0:T(8,128)(2,1)S(1)} %maximum_maximum_fusion.13), channel_id=1, source_target_pairs={{0,30},{2,0},{4,2},{6,4},{8,6},{10,8},{12,10},{14,12},{16,14},{18,... | collective-permute-start | bytes 608264 | tf_op jit(solution)/shard_map/ppermute | solution.py:19
  202.7 6.4 %collective-permute-done.28 = bf16[528,192]{1,0:T(8,128)(2,1)S(1)} collective-permute-done((bf16[528,192]{1,0:T(8,128)(2,1)S(1)}, bf16[528,192]{1,0:T(8,128)(2,1)S(1)}, u32[]{:S(2)}, u32[]{:S(2)}) %collective-permute-start.28) | collective-permute-done | bytes 202784 | tf_op jit(solution)/shard_map/ppermute | solution.py:19
  210.3 19.5 %collective-permute-start.30 = (bf16[2,256,192]{2,1,0:T(8,128)(2,1)S(1)}, bf16[2,256,192]{2,1,0:T(8,128)(2,1)S(1)}, u32[]{:S(2)}, u32[]{:S(2)}) collective-permute-start(bf16[2,256,192]{2,1,0:T(8,128)(2,1)S(1)} %pad_maximum_fusion), channel_id=1, source_target_pairs={{32,0},{64,32},{96,64},{128,96},{160,128},{192,160},{224,192},{256... | collective-permute-start | bytes 589832 | tf_op jit(solution)/shard_map/ppermute | solution.py:14
  229.8 4.6 %collective-permute-start.31 = (f32[192]{0:T(256)S(1)}, f32[192]{0:T(256)S(1)}, u32[]{:S(2)}, u32[]{:S(2)}) collective-permute-start(f32[192]{0:T(256)S(1)} %bitcast.356), channel_id=1, source_target_pairs={{0,1},{1,0},{2,3},{3,2},{4,5},{5,4},{6,7},{7,6},{8,9},{9,8},{10,11... | collective-permute-start | bytes 2312 | tf_op jit(solution)/shard_map/ppermute | solution.py:19
  (201 shorter events, 63.3 us)
Async XLA Ops:
  1.8 24.8 %collective-permute-start = (bf16[2,256,192]{1,2,0:T(8,128)(2,1)S(1)}, bf16[2,256,192]{1,2,0:T(8,128)(2,1)S(1)}, u32[]{:S(2)}, u32[]{:S(2)}) collective-permute-start(bf16[2,256,192]{1,2,0:T(8,128)(2,1)S(1)} %pad_maximum_fusion.1), channel_id=1, source_target_pairs={{0,30},{2,0},{4,2},{6,4},{8,6},{10,8},{12,10},{14,12},{16,14},{18,... | collective-permute-start | bytes 589832 | tf_op jit(solution)/shard_map/ppermute | solution.py:19
  20.5 10.6 %collective-permute-start.7 = (bf16[2,256,192]{1,2,0:T(8,128)(2,1)S(1)}, bf16[2,256,192]{1,2,0:T(8,128)(2,1)S(1)}, u32[]{:S(2)}, u32[]{:S(2)}) collective-permute-start(bf16[2,256,192]{1,2,0:T(8,128)(2,1)S(1)} %pad_maximum_fusion.1), channel_id=1, source_target_pairs={{0,2},{2,4},{4,6},{6,8},{8,10},{10,12},{12,14},{14,16},{16,18},{18... | collective-permute-start | bytes 589832 | tf_op jit(solution)/shard_map/ppermute | solution.py:19
  26.6 7.5 %collective-permute-start.1 = (bf16[2,256,192]{1,2,0:T(8,128)(2,1)S(1)}, bf16[2,256,192]{1,2,0:T(8,128)(2,1)S(1)}, u32[]{:S(2)}, u32[]{:S(2)}) collective-permute-start(bf16[2,256,192]{1,2,0:T(8,128)(2,1)S(1)} %collective-permute-done), channel_id=1, source_target_pairs={{0,30},{2,0},{4,2},{6,4},{8,6},{10,8},{12,10},{14,12},{16,14},{18,... | collective-permute-start | bytes 589832 | tf_op jit(solution)/shard_map/ppermute | solution.py:19
  31.2 8.2 %collective-permute-start.8 = (bf16[2,256,192]{1,2,0:T(8,128)(2,1)S(1)}, bf16[2,256,192]{1,2,0:T(8,128)(2,1)S(1)}, u32[]{:S(2)}, u32[]{:S(2)}) collective-permute-start(bf16[2,256,192]{1,2,0:T(8,128)(2,1)S(1)} %collective-permute-done.7), channel_id=1, source_target_pairs={{0,2},{2,4},{4,6},{6,8},{8,10},{10,12},{12,14},{14,16},{16,18},{18... | collective-permute-start | bytes 589832 | tf_op jit(solution)/shard_map/ppermute | solution.py:19
  34.1 7.9 %collective-permute-start.2 = (bf16[2,256,192]{1,2,0:T(8,128)(2,1)S(1)}, bf16[2,256,192]{1,2,0:T(8,128)(2,1)S(1)}, u32[]{:S(2)}, u32[]{:S(2)}) collective-permute-start(bf16[2,256,192]{1,2,0:T(8,128)(2,1)S(1)} %collective-permute-done.1), channel_id=1, source_target_pairs={{0,30},{2,0},{4,2},{6,4},{8,6},{10,8},{12,10},{14,12},{16,14},{18,... | collective-permute-start | bytes 589832 | tf_op jit(solution)/shard_map/ppermute | solution.py:19
  39.4 7.6 %collective-permute-start.9 = (bf16[2,256,192]{1,2,0:T(8,128)(2,1)S(1)}, bf16[2,256,192]{1,2,0:T(8,128)(2,1)S(1)}, u32[]{:S(2)}, u32[]{:S(2)}) collective-permute-start(bf16[2,256,192]{1,2,0:T(8,128)(2,1)S(1)} %collective-permute-done.8), channel_id=1, source_target_pairs={{0,2},{2,4},{4,6},{6,8},{8,10},{10,12},{12,14},{14,16},{16,18},{18... | collective-permute-start | bytes 589832 | tf_op jit(solution)/shard_map/ppermute | solution.py:19
  42.0 7.6 %collective-permute-start.3 = (bf16[2,256,192]{1,2,0:T(8,128)(2,1)S(1)}, bf16[2,256,192]{1,2,0:T(8,128)(2,1)S(1)}, u32[]{:S(2)}, u32[]{:S(2)}) collective-permute-start(bf16[2,256,192]{1,2,0:T(8,128)(2,1)S(1)} %collective-permute-done.2), channel_id=1, source_target_pairs={{0,30},{2,0},{4,2},{6,4},{8,6},{10,8},{12,10},{14,12},{16,14},{18,... | collective-permute-start | bytes 589832 | tf_op jit(solution)/shard_map/ppermute | solution.py:19
  47.0 7.6 %collective-permute-start.10 = (bf16[2,256,192]{1,2,0:T(8,128)(2,1)S(1)}, bf16[2,256,192]{1,2,0:T(8,128)(2,1)S(1)}, u32[]{:S(2)}, u32[]{:S(2)}) collective-permute-start(bf16[2,256,192]{1,2,0:T(8,128)(2,1)S(1)} %collective-permute-done.9), channel_id=1, source_target_pairs={{0,2},{2,4},{4,6},{6,8},{8,10},{10,12},{12,14},{14,16},{16,18},{18... | collective-permute-start | bytes 589832 | tf_op jit(solution)/shard_map/ppermute | solution.py:19
  49.6 7.6 %collective-permute-start.4 = (bf16[2,256,192]{1,2,0:T(8,128)(2,1)S(1)}, bf16[2,256,192]{1,2,0:T(8,128)(2,1)S(1)}, u32[]{:S(2)}, u32[]{:S(2)}) collective-permute-start(bf16[2,256,192]{1,2,0:T(8,128)(2,1)S(1)} %collective-permute-done.3), channel_id=1, source_target_pairs={{0,30},{2,0},{4,2},{6,4},{8,6},{10,8},{12,10},{14,12},{16,14},{18,... | collective-permute-start | bytes 589832 | tf_op jit(solution)/shard_map/ppermute | solution.py:19
  54.7 7.6 %collective-permute-start.11 = (bf16[2,256,192]{1,2,0:T(8,128)(2,1)S(1)}, bf16[2,256,192]{1,2,0:T(8,128)(2,1)S(1)}, u32[]{:S(2)}, u32[]{:S(2)}) collective-permute-start(bf16[2,256,192]{1,2,0:T(8,128)(2,1)S(1)} %collective-permute-done.10), channel_id=1, source_target_pairs={{0,2},{2,4},{4,6},{6,8},{8,10},{10,12},{12,14},{14,16},{16,18},{18... | collective-permute-start | bytes 589832 | tf_op jit(solution)/shard_map/ppermute | solution.py:19
  57.2 7.6 %collective-permute-start.5 = (bf16[2,256,192]{1,2,0:T(8,128)(2,1)S(1)}, bf16[2,256,192]{1,2,0:T(8,128)(2,1)S(1)}, u32[]{:S(2)}, u32[]{:S(2)}) collective-permute-start(bf16[2,256,192]{1,2,0:T(8,128)(2,1)S(1)} %collective-permute-done.4), channel_id=1, source_target_pairs={{0,30},{2,0},{4,2},{6,4},{8,6},{10,8},{12,10},{14,12},{16,14},{18,... | collective-permute-start | bytes 589832 | tf_op jit(solution)/shard_map/ppermute | solution.py:19
  62.3 7.6 %collective-permute-start.12 = (bf16[2,256,192]{1,2,0:T(8,128)(2,1)S(1)}, bf16[2,256,192]{1,2,0:T(8,128)(2,1)S(1)}, u32[]{:S(2)}, u32[]{:S(2)}) collective-permute-start(bf16[2,256,192]{1,2,0:T(8,128)(2,1)S(1)} %collective-permute-done.11), channel_id=1, source_target_pairs={{0,2},{2,4},{4,6},{6,8},{8,10},{10,12},{12,14},{14,16},{16,18},{18... | collective-permute-start | bytes 589832 | tf_op jit(solution)/shard_map/ppermute | solution.py:19
  64.8 15.4 %collective-permute-start.6 = (bf16[2,256,192]{1,2,0:T(8,128)(2,1)S(1)}, bf16[2,256,192]{1,2,0:T(8,128)(2,1)S(1)}, u32[]{:S(2)}, u32[]{:S(2)}) collective-permute-start(bf16[2,256,192]{1,2,0:T(8,128)(2,1)S(1)} %collective-permute-done.5), channel_id=1, source_target_pairs={{0,30},{2,0},{4,2},{6,4},{8,6},{10,8},{12,10},{14,12},{16,14},{18,... | collective-permute-start | bytes 589832 | tf_op jit(solution)/shard_map/ppermute | solution.py:19
  69.9 8.5 %collective-permute-start.13 = (bf16[2,256,192]{1,2,0:T(8,128)(2,1)S(1)}, bf16[2,256,192]{1,2,0:T(8,128)(2,1)S(1)}, u32[]{:S(2)}, u32[]{:S(2)}) collective-permute-start(bf16[2,256,192]{1,2,0:T(8,128)(2,1)S(1)} %collective-permute-done.12), channel_id=1, source_target_pairs={{0,2},{2,4},{4,6},{6,8},{8,10},{10,12},{12,14},{14,16},{16,18},{18... | collective-permute-start | bytes 589832 | tf_op jit(solution)/shard_map/ppermute | solution.py:19
  78.3 9.7 %collective-permute-start.14 = (bf16[2,256,192]{1,2,0:T(8,128)(2,1)S(1)}, bf16[2,256,192]{1,2,0:T(8,128)(2,1)S(1)}, u32[]{:S(2)}, u32[]{:S(2)}) collective-permute-start(bf16[2,256,192]{1,2,0:T(8,128)(2,1)S(1)} %collective-permute-done.13), channel_id=1, source_target_pairs={{0,2},{2,4},{4,6},{6,8},{8,10},{10,12},{12,14},{14,16},{16,18},{18... | collective-permute-start | bytes 589832 | tf_op jit(solution)/shard_map/ppermute | solution.py:19
  134.0 8.4 %collective-permute-start.15 = (bf16[528,192]{1,0:T(8,128)(2,1)S(1)}, bf16[528,192]{1,0:T(8,128)(2,1)S(1)}, u32[]{:S(2)}, u32[]{:S(2)}) collective-permute-start(bf16[528,192]{1,0:T(8,128)(2,1)S(1)} %get-tuple-element.78), channel_id=1, source_target_pairs={{0,2},{2,4},{4,6},{6,8},{8,10},{10,12},{12,14},{14,16},{16,18},{18... | collective-permute-start | bytes 608264 | tf_op jit(solution)/shard_map/ppermute | solution.py:19
  136.1 9.4 %collective-permute-start.17 = (bf16[528,192]{1,0:T(8,128)(2,1)S(1)}, bf16[528,192]{1,0:T(8,128)(2,1)S(1)}, u32[]{:S(2)}, u32[]{:S(2)}) collective-permute-start(bf16[528,192]{1,0:T(8,128)(2,1)S(1)} %get-tuple-element.77), channel_id=1, source_target_pairs={{0,30},{2,0},{4,2},{6,4},{8,6},{10,8},{12,10},{14,12},{16,14},{18,... | collective-permute-start | bytes 608264 | tf_op jit(solution)/shard_map/ppermute | solution.py:19
  143.6 11.6 %collective-permute-start.16 = (bf16[528,192]{1,0:T(8,128)(2,1)S(1)}, bf16[528,192]{1,0:T(8,128)(2,1)S(1)}, u32[]{:S(2)}, u32[]{:S(2)}) collective-permute-start(bf16[528,192]{1,0:T(8,128)(2,1)S(1)} %maximum_maximum_fusion.2), channel_id=1, source_target_pairs={{0,2},{2,4},{4,6},{6,8},{8,10},{10,12},{12,14},{14,16},{16,18},{18... | collective-permute-start | bytes 608264 | tf_op jit(solution)/shard_map/ppermute | solution.py:19
  145.8 11.7 %collective-permute-start.19 = (bf16[528,192]{1,0:T(8,128)(2,1)S(1)}, bf16[528,192]{1,0:T(8,128)(2,1)S(1)}, u32[]{:S(2)}, u32[]{:S(2)}) collective-permute-start(bf16[528,192]{1,0:T(8,128)(2,1)S(1)} %maximum_maximum_fusion.3), channel_id=1, source_target_pairs={{0,30},{2,0},{4,2},{6,4},{8,6},{10,8},{12,10},{14,12},{16,14},{18,... | collective-permute-start | bytes 608264 | tf_op jit(solution)/shard_map/ppermute | solution.py:19
  155.4 9.7 %collective-permute-start.18 = (bf16[528,192]{1,0:T(8,128)(2,1)S(1)}, bf16[528,192]{1,0:T(8,128)(2,1)S(1)}, u32[]{:S(2)}, u32[]{:S(2)}) collective-permute-start(bf16[528,192]{1,0:T(8,128)(2,1)S(1)} %maximum_maximum_fusion.4), channel_id=1, source_target_pairs={{0,2},{2,4},{4,6},{6,8},{8,10},{10,12},{12,14},{14,16},{16,18},{18... | collective-permute-start | bytes 608264 | tf_op jit(solution)/shard_map/ppermute | solution.py:19
  157.8 9.5 %collective-permute-start.21 = (bf16[528,192]{1,0:T(8,128)(2,1)S(1)}, bf16[528,192]{1,0:T(8,128)(2,1)S(1)}, u32[]{:S(2)}, u32[]{:S(2)}) collective-permute-start(bf16[528,192]{1,0:T(8,128)(2,1)S(1)} %maximum_maximum_fusion.5), channel_id=1, source_target_pairs={{0,30},{2,0},{4,2},{6,4},{8,6},{10,8},{12,10},{14,12},{16,14},{18,... | collective-permute-start | bytes 608264 | tf_op jit(solution)/shard_map/ppermute | solution.py:19
  165.4 8.8 %collective-permute-start.20 = (bf16[528,192]{1,0:T(8,128)(2,1)S(1)}, bf16[528,192]{1,0:T(8,128)(2,1)S(1)}, u32[]{:S(2)}, u32[]{:S(2)}) collective-permute-start(bf16[528,192]{1,0:T(8,128)(2,1)S(1)} %maximum_maximum_fusion.6), channel_id=1, source_target_pairs={{0,2},{2,4},{4,6},{6,8},{8,10},{10,12},{12,14},{14,16},{16,18},{18... | collective-permute-start | bytes 608264 | tf_op jit(solution)/shard_map/ppermute | solution.py:19
  167.6 8.8 %collective-permute-start.23 = (bf16[528,192]{1,0:T(8,128)(2,1)S(1)}, bf16[528,192]{1,0:T(8,128)(2,1)S(1)}, u32[]{:S(2)}, u32[]{:S(2)}) collective-permute-start(bf16[528,192]{1,0:T(8,128)(2,1)S(1)} %maximum_maximum_fusion.7), channel_id=1, source_target_pairs={{0,30},{2,0},{4,2},{6,4},{8,6},{10,8},{12,10},{14,12},{16,14},{18,... | collective-permute-start | bytes 608264 | tf_op jit(solution)/shard_map/ppermute | solution.py:19
  174.5 8.4 %collective-permute-start.22 = (bf16[528,192]{1,0:T(8,128)(2,1)S(1)}, bf16[528,192]{1,0:T(8,128)(2,1)S(1)}, u32[]{:S(2)}, u32[]{:S(2)}) collective-permute-start(bf16[528,192]{1,0:T(8,128)(2,1)S(1)} %maximum_maximum_fusion.8), channel_id=1, source_target_pairs={{0,2},{2,4},{4,6},{6,8},{8,10},{10,12},{12,14},{14,16},{16,18},{18... | collective-permute-start | bytes 608264 | tf_op jit(solution)/shard_map/ppermute | solution.py:19
  176.7 8.4 %collective-permute-start.25 = (bf16[528,192]{1,0:T(8,128)(2,1)S(1)}, bf16[528,192]{1,0:T(8,128)(2,1)S(1)}, u32[]{:S(2)}, u32[]{:S(2)}) collective-permute-start(bf16[528,192]{1,0:T(8,128)(2,1)S(1)} %maximum_maximum_fusion.9), channel_id=1, source_target_pairs={{0,30},{2,0},{4,2},{6,4},{8,6},{10,8},{12,10},{14,12},{16,14},{18,... | collective-permute-start | bytes 608264 | tf_op jit(solution)/shard_map/ppermute | solution.py:19
  183.1 8.4 %collective-permute-start.24 = (bf16[528,192]{1,0:T(8,128)(2,1)S(1)}, bf16[528,192]{1,0:T(8,128)(2,1)S(1)}, u32[]{:S(2)}, u32[]{:S(2)}) collective-permute-start(bf16[528,192]{1,0:T(8,128)(2,1)S(1)} %maximum_maximum_fusion.10), channel_id=1, source_target_pairs={{0,2},{2,4},{4,6},{6,8},{8,10},{10,12},{12,14},{14,16},{16,18},{18... | collective-permute-start | bytes 608264 | tf_op jit(solution)/shard_map/ppermute | solution.py:19
  185.3 8.4 %collective-permute-start.27 = (bf16[528,192]{1,0:T(8,128)(2,1)S(1)}, bf16[528,192]{1,0:T(8,128)(2,1)S(1)}, u32[]{:S(2)}, u32[]{:S(2)}) collective-permute-start(bf16[528,192]{1,0:T(8,128)(2,1)S(1)} %maximum_maximum_fusion.11), channel_id=1, source_target_pairs={{0,30},{2,0},{4,2},{6,4},{8,6},{10,8},{12,10},{14,12},{16,14},{18,... | collective-permute-start | bytes 608264 | tf_op jit(solution)/shard_map/ppermute | solution.py:19
  191.8 8.4 %collective-permute-start.26 = (bf16[528,192]{1,0:T(8,128)(2,1)S(1)}, bf16[528,192]{1,0:T(8,128)(2,1)S(1)}, u32[]{:S(2)}, u32[]{:S(2)}) collective-permute-start(bf16[528,192]{1,0:T(8,128)(2,1)S(1)} %maximum_maximum_fusion.12), channel_id=1, source_target_pairs={{0,2},{2,4},{4,6},{6,8},{8,10},{10,12},{12,14},{14,16},{16,18},{18... | collective-permute-start | bytes 608264 | tf_op jit(solution)/shard_map/ppermute | solution.py:19
  194.0 8.6 %collective-permute-start.29 = (bf16[528,192]{1,0:T(8,128)(2,1)S(1)}, bf16[528,192]{1,0:T(8,128)(2,1)S(1)}, u32[]{:S(2)}, u32[]{:S(2)}) collective-permute-start(bf16[528,192]{1,0:T(8,128)(2,1)S(1)} %maximum_maximum_fusion.13), channel_id=1, source_target_pairs={{0,30},{2,0},{4,2},{6,4},{8,6},{10,8},{12,10},{14,12},{16,14},{18,... | collective-permute-start | bytes 608264 | tf_op jit(solution)/shard_map/ppermute | solution.py:19
  200.5 8.6 %collective-permute-start.28 = (bf16[528,192]{1,0:T(8,128)(2,1)S(1)}, bf16[528,192]{1,0:T(8,128)(2,1)S(1)}, u32[]{:S(2)}, u32[]{:S(2)}) collective-permute-start(bf16[528,192]{1,0:T(8,128)(2,1)S(1)} %maximum_maximum_fusion.14), channel_id=1, source_target_pairs={{0,2},{2,4},{4,6},{6,8},{8,10},{10,12},{12,14},{14,16},{16,18},{18... | collective-permute-start | bytes 608264 | tf_op jit(solution)/shard_map/ppermute | solution.py:19
  210.3 26.1 %collective-permute-start.30 = (bf16[2,256,192]{2,1,0:T(8,128)(2,1)S(1)}, bf16[2,256,192]{2,1,0:T(8,128)(2,1)S(1)}, u32[]{:S(2)}, u32[]{:S(2)}) collective-permute-start(bf16[2,256,192]{2,1,0:T(8,128)(2,1)S(1)} %pad_maximum_fusion), channel_id=1, source_target_pairs={{32,0},{64,32},{96,64},{128,96},{160,128},{192,160},{224,192},{256... | collective-permute-start | bytes 589832 | tf_op jit(solution)/shard_map/ppermute | solution.py:14
  229.8 6.1 %collective-permute-start.31 = (f32[192]{0:T(256)S(1)}, f32[192]{0:T(256)S(1)}, u32[]{:S(2)}, u32[]{:S(2)}) collective-permute-start(f32[192]{0:T(256)S(1)} %bitcast.356), channel_id=1, source_target_pairs={{0,1},{1,0},{2,3},{3,2},{4,5},{5,4},{6,7},{7,6},{8,9},{9,8},{10,11... | collective-permute-start | bytes 2312 | tf_op jit(solution)/shard_map/ppermute | solution.py:19
  (18 other events, 350.5 us)

commit v5 on v4

--- a/solution.py
+++ b/solution.py
@@ -46,8 +46,11 @@
     forward_steps = n // 2
     backward_steps = n - 1 - forward_steps
 
+    parts = jnp.roll(parts, -me, axis=0)
+    exact = jnp.roll(exact, -me, axis=0)
+
     def pick(stack, offset):
-        return lax.dynamic_index_in_dim(stack, (me + offset) % n, 0, keepdims=False)
+        return stack[offset % n]
 
     def own(offset):
         return pick(parts, offset).astype(jnp.float32), pick(exact, offset)
@@ -201,13 +204,14 @@
     grad_parts = ((weighted - unit_rows * row_stat) * inverse).astype(jnp.bfloat16)
     grad_parts = jnp.transpose(grad_parts.reshape(length, n_mp, share), (1, 0, 2))
     gain_parts = jnp.sum(normed_grad * unit_rows, axis=0).reshape(n_mp, share)
+    gain_parts = gain_parts + shift(gain_parts, "dp", 1)
     shares, gain_share = ring_reduce_scatter(
         jnp.concatenate([out_parts, grad_parts], axis=1), gain_parts, "mp"
     )
     out_share, grad_share = shares[:length], shares[length:]
     rebuilt = (lower_out[0, 0].astype(jnp.float32) - out_share).astype(jnp.bfloat16)
     lower_rows = upper_grad[0, 0].astype(jnp.float32) + grad_share
-    gain_grad = gain_share + shift(gain_share, "dp", 1)
+    gain_grad = gain_share
     entering = lower_rows.astype(jnp.bfloat16)
     sent = from_behind(jnp.stack([rebuilt, entering]), "section", -1)
     return (sent[0][None, None], sent[1][None, None], gain_grad[None])

time: 239 us -> 257 us (1.075)
  waiting for transfers between devices: 41.5 us -> 54.6 us
  starting transfers between devices: 136 us -> 140 us
    ppermute x31, waiting for transfers between devices: 41.5 us -> 51 us  [shift(): lax.ppermute(x, axis, [(i, (i + by) % length) for i in range(length)])]
    concatenate x0 -> x2, other arithmetic: none -> 5.12 us  [the longest x1 5.1 us: ring_reduce_scatter(): parts = jnp.roll(parts, -me, axis=0)]
    ppermute x1, waiting for transfers between devices: 0.01 us -> 3.64 us  [from_behind(): return lax.ppermute(x, axis, pairs)]
    ppermute x31, starting transfers between devices: 117 us -> 120 us  [shift(): lax.ppermute(x, axis, [(i, (i + by) % length) for i in range(length)])]
  transfers between devices with their start and end apart: 32 -> 32, of which waited for: 16 -> 22; matrix products, arithmetic and copies ran while one was open for 4% -> 5% of each run, Pallas kernels for 0% -> 0%
where the time goes in v5:
time: 257 us; the launch traced here: 254 us
  starting transfers between devices  140 us (54%)
  waiting for transfers between devices  54.6 us (21%)
  other arithmetic  22.5 us (9%)
  matrix products  20.4 us (8%)
  local copies, waits for them, and re-layouts  15 us (6%)
    ppermute x31, starting transfers between devices, shift(): lax.ppermute(x, axis, [(i, (i + by) % length) for i in range(length)])  120 us
    ppermute x31, waiting for transfers between devices, shift(): lax.ppermute(x, axis, [(i, (i + by) % length) for i in range(length)])  51 us
    ppermute x1, starting transfers between devices, from_behind(): return lax.ppermute(x, axis, pairs)  19.8 us
    dot_general x1, matrix products, local(): jnp.dot(value_gradient, w_value.T, preferred_element_type=jnp.float32)  5.9 us
  transfers between devices with their start and end apart: 32, of which 22 were waited for; matrix products, arithmetic and copies ran while one was open for 5% of the time, Pallas kernels for 0%

profile of v5, /device:TPU:1, one launch (start us, length us, event | category | flops | bytes accessed | tf_op | source)
XLA Modules:
  0.0 254.1 jit_solution(2411413662512096539)
XLA Ops:
  1.8 18.8 %collective-permute-start = (bf16[2,256,192]{1,2,0:T(8,128)(2,1)S(1)}, bf16[2,256,192]{1,2,0:T(8,128)(2,1)S(1)}, u32[]{:S(2)}, u32[]{:S(2)}) collective-permute-start(bf16[2,256,192]{1,2,0:T(8,128)(2,1)S(1)} %pad_maximum_fusion.1), channel_id=1, source_target_pairs={{0,30},{2,0},{4,2},{6,4},{8,6},{10,8},{12,10},{14,12},{16,14},{18,... | collective-permute-start | bytes 589832 | tf_op jit(solution)/shard_map/ppermute | solution.py:19
  26.6 4.6 %collective-permute-start.1 = (bf16[2,256,192]{1,2,0:T(8,128)(2,1)S(1)}, bf16[2,256,192]{1,2,0:T(8,128)(2,1)S(1)}, u32[]{:S(2)}, u32[]{:S(2)}) collective-permute-start(bf16[2,256,192]{1,2,0:T(8,128)(2,1)S(1)} %collective-permute-done), channel_id=1, source_target_pairs={{0,30},{2,0},{4,2},{6,4},{8,6},{10,8},{12,10},{14,12},{16,14},{18,... | collective-permute-start | bytes 589832 | tf_op jit(solution)/shard_map/ppermute | solution.py:19
  34.1 5.3 %collective-permute-start.2 = (bf16[2,256,192]{1,2,0:T(8,128)(2,1)S(1)}, bf16[2,256,192]{1,2,0:T(8,128)(2,1)S(1)}, u32[]{:S(2)}, u32[]{:S(2)}) collective-permute-start(bf16[2,256,192]{1,2,0:T(8,128)(2,1)S(1)} %collective-permute-done.1), channel_id=1, source_target_pairs={{0,30},{2,0},{4,2},{6,4},{8,6},{10,8},{12,10},{14,12},{16,14},{18,... | collective-permute-start | bytes 589832 | tf_op jit(solution)/shard_map/ppermute | solution.py:19
  42.0 5.0 %collective-permute-start.3 = (bf16[2,256,192]{1,2,0:T(8,128)(2,1)S(1)}, bf16[2,256,192]{1,2,0:T(8,128)(2,1)S(1)}, u32[]{:S(2)}, u32[]{:S(2)}) collective-permute-start(bf16[2,256,192]{1,2,0:T(8,128)(2,1)S(1)} %collective-permute-done.2), channel_id=1, source_target_pairs={{0,30},{2,0},{4,2},{6,4},{8,6},{10,8},{12,10},{14,12},{16,14},{18,... | collective-permute-start | bytes 589832 | tf_op jit(solution)/shard_map/ppermute | solution.py:19
  49.6 5.0 %collective-permute-start.4 = (bf16[2,256,192]{1,2,0:T(8,128)(2,1)S(1)}, bf16[2,256,192]{1,2,0:T(8,128)(2,1)S(1)}, u32[]{:S(2)}, u32[]{:S(2)}) collective-permute-start(bf16[2,256,192]{1,2,0:T(8,128)(2,1)S(1)} %collective-permute-done.3), channel_id=1, source_target_pairs={{0,30},{2,0},{4,2},{6,4},{8,6},{10,8},{12,10},{14,12},{16,14},{18,... | collective-permute-start | bytes 589832 | tf_op jit(solution)/shard_map/ppermute | solution.py:19
  57.2 5.0 %collective-permute-start.5 = (bf16[2,256,192]{1,2,0:T(8,128)(2,1)S(1)}, bf16[2,256,192]{1,2,0:T(8,128)(2,1)S(1)}, u32[]{:S(2)}, u32[]{:S(2)}) collective-permute-start(bf16[2,256,192]{1,2,0:T(8,128)(2,1)S(1)} %collective-permute-done.4), channel_id=1, source_target_pairs={{0,30},{2,0},{4,2},{6,4},{8,6},{10,8},{12,10},{14,12},{16,14},{18,... | collective-permute-start | bytes 589832 | tf_op jit(solution)/shard_map/ppermute | solution.py:19
  64.8 5.0 %collective-permute-start.6 = (bf16[2,256,192]{1,2,0:T(8,128)(2,1)S(1)}, bf16[2,256,192]{1,2,0:T(8,128)(2,1)S(1)}, u32[]{:S(2)}, u32[]{:S(2)}) collective-permute-start(bf16[2,256,192]{1,2,0:T(8,128)(2,1)S(1)} %collective-permute-done.5), channel_id=1, source_target_pairs={{0,30},{2,0},{4,2},{6,4},{8,6},{10,8},{12,10},{14,12},{16,14},{18,... | collective-permute-start | bytes 589832 | tf_op jit(solution)/shard_map/ppermute | solution.py:19
  71.8 6.5 %collective-permute-done.13 = bf16[2,256,192]{1,2,0:T(8,128)(2,1)S(1)} collective-permute-done((bf16[2,256,192]{1,2,0:T(8,128)(2,1)S(1)}, bf16[2,256,192]{1,2,0:T(8,128)(2,1)S(1)}, u32[]{:S(2)}, u32[]{:S(2)}) %collective-permute-start.13) | collective-permute-done | bytes 196640 | tf_op jit(solution)/shard_map/ppermute | solution.py:19
  80.3 7.8 %collective-permute-done.14 = bf16[2,256,192]{1,2,0:T(8,128)(2,1)S(1)} collective-permute-done((bf16[2,256,192]{1,2,0:T(8,128)(2,1)S(1)}, bf16[2,256,192]{1,2,0:T(8,128)(2,1)S(1)}, u32[]{:S(2)}, u32[]{:S(2)}) %collective-permute-start.14) | collective-permute-done | bytes 196640 | tf_op jit(solution)/shard_map/ppermute | solution.py:19
  98.0 4.5 %convolution_add_fusion.1 = f32[256,3072]{1,0:T(8,128)} fusion(f32[256,3072]{1,0:T(8,128)} %fusion.8, bf16[256,2,128]{0,2,1:T(8,128)(2,1)S(1)} %bitcast.347, bf16[2,256,256]{1,2,0:T(8,128)(2,1)S(1)} %fusion.48, bf16[1,3072,128]{2,1,0:T(8,128)(2,1)S(1)} %copy-done.3), kind=kOutput, calls=%fused_computation.8 | convolution fusion | flops 235700224 | bytes 7471104 | tf_op jit(solution)/shard_map/dot_general | solution.py:198
  102.5 3.7 %copy.253 = f32[256,3072]{1,0:T(8,128)} copy(f32[256,3072]{0,1:T(8,128)} %bitcast.335) | data formatting | bytes 6291456 | tf_op jit(solution)/shard_map/convert_element_type | solution.py:127
  106.2 5.9 %multiply_reduce_fusion.1 = (f32[256]{0:T(256)S(1)}, f32[3072]{0:T(1024)S(1)}, f32[256,3072]{1,0:T(8,128)}) fusion(f32[256,3072]{1,0:T(8,128)} %copy.253, f32[256]{0:T(256)S(1)} %add_rsqrt_fusion, f32[3072]{0:T(1024)S(1)} %bitcast.352, f32[256,3072]{1,0:T(8,128)} %convolution_add_fusion.1, bf16[1,3072,128]{2,1,0:T(8,128)(2,1)S(1)} %copy-done.5, ...), kind=kOutput, calls=%fused_computation.11 | convolution fusion | flops 240939776 | bytes 10975232 | tf_op jit(solution)/shard_map/dot_general | solution.py:199
  112.1 4.9 %multiply_convert_fusion = bf16[256,3072]{1,0:T(8,128)(2,1)} fusion(f32[256,3072]{1,0:T(8,128)} %get-tuple-element.95, f32[256,3072]{1,0:T(8,128)} %copy.253, f32[256]{0:T(256)S(1)} %broadcast_multiply_fusion, f32[256]{0:T(256)S(1)} %add_rsqrt_fusion, f32[3072]{0:T(1024)S(1)} %bitcast.353), kind=kLoop, calls=%fused_computation.10 | loop fusion | flops 4718592 | bytes 7878656 | tf_op jit(solution)/shard_map/convert_element_type | solution.py:204
  118.7 2.5 copy.255
  121.3 3.7 %fusion.6 = f32[256,3072]{0,1} fusion(bf16[256,256]{0,1:T(8,128)(2,1)S(1)} %bitcast.349, bf16[1,256,3072]{2,1,0:T(8,128)(2,1)} %param.18), kind=kOutput, calls=%fused_computation.19 | convolution fusion | flops 402653184 | bytes 4849664
  125.0 4.3 %copy.247 = bf16[256,16,192]{2,0,1:T(8,128)(2,1)} copy(f32[256,16,192]{0,2,1:T(8,128)} %bitcast.331) | data formatting | bytes 4718592 | tf_op jit(solution)/shard_map/lc,cmf->mlf/dot_general | solution.py:166
  129.4 4.8 %collective-permute-start.15 = (f32[16,192]{1,0:T(8,128)S(1)}, f32[16,192]{1,0:T(8,128)S(1)}, u32[]{:S(2)}, u32[]{:S(2)}) collective-permute-start(f32[16,192]{1,0:T(8,128)S(1)} %reshape.194), channel_id=1, source_target_pairs={{0,1},{1,0},{2,3},{3,2},{4,5},{5,4},{6,7},{7,6},{8,9},{9,8},{10,11... | collective-permute-start | bytes 36872 | tf_op jit(solution)/shard_map/ppermute | solution.py:19
  134.2 5.1 %fusion.1 = bf16[16,512,192]{2,1,0:T(8,128)(2,1)S(1)} fusion(s32[]{:T(128)S(6)} %select_n.53, bf16[16,256,192]{2,1,0:T(8,128)(2,1)} %bitcast.337, bf16[16,256,192]{2,1,0:T(8,128)(2,1)} %bitcast.336), kind=kLoop, calls=%fused_computation.5 | loop fusion | flops 12582912 | bytes 6291460 | tf_op jit(solution)/shard_map/jit(_roll_dynamic)/concatenate | solution.py:49
  141.6 4.6 %collective-permute-start.18 = (bf16[528,192]{1,0:T(8,128)(2,1)S(1)}, bf16[528,192]{1,0:T(8,128)(2,1)S(1)}, u32[]{:S(2)}, u32[]{:S(2)}) collective-permute-start(bf16[528,192]{1,0:T(8,128)(2,1)S(1)} %get-tuple-element.89), channel_id=1, source_target_pairs={{0,30},{2,0},{4,2},{6,4},{8,6},{10,8},{12,10},{14,12},{16,14},{18,... | collective-permute-start | bytes 608264 | tf_op jit(solution)/shard_map/ppermute | solution.py:19
  151.7 5.0 %collective-permute-start.20 = (bf16[528,192]{1,0:T(8,128)(2,1)S(1)}, bf16[528,192]{1,0:T(8,128)(2,1)S(1)}, u32[]{:S(2)}, u32[]{:S(2)}) collective-permute-start(bf16[528,192]{1,0:T(8,128)(2,1)S(1)} %maximum_maximum_fusion.3), channel_id=1, source_target_pairs={{0,30},{2,0},{4,2},{6,4},{8,6},{10,8},{12,10},{14,12},{16,14},{18,... | collective-permute-start | bytes 608264 | tf_op jit(solution)/shard_map/ppermute | solution.py:19
  156.7 4.1 %collective-permute-done.17 = bf16[528,192]{1,0:T(8,128)(2,1)S(1)} collective-permute-done((bf16[528,192]{1,0:T(8,128)(2,1)S(1)}, bf16[528,192]{1,0:T(8,128)(2,1)S(1)}, u32[]{:S(2)}, u32[]{:S(2)}) %collective-permute-start.17) | collective-permute-done | bytes 202784 | tf_op jit(solution)/shard_map/ppermute | solution.py:19
  164.9 5.0 %collective-permute-start.22 = (bf16[528,192]{1,0:T(8,128)(2,1)S(1)}, bf16[528,192]{1,0:T(8,128)(2,1)S(1)}, u32[]{:S(2)}, u32[]{:S(2)}) collective-permute-start(bf16[528,192]{1,0:T(8,128)(2,1)S(1)} %maximum_maximum_fusion.5), channel_id=1, source_target_pairs={{0,30},{2,0},{4,2},{6,4},{8,6},{10,8},{12,10},{14,12},{16,14},{18,... | collective-permute-start | bytes 608264 | tf_op jit(solution)/shard_map/ppermute | solution.py:19
  170.0 4.6 %collective-permute-done.19 = bf16[528,192]{1,0:T(8,128)(2,1)S(1)} collective-permute-done((bf16[528,192]{1,0:T(8,128)(2,1)S(1)}, bf16[528,192]{1,0:T(8,128)(2,1)S(1)}, u32[]{:S(2)}, u32[]{:S(2)}) %collective-permute-start.19) | collective-permute-done | bytes 202784 | tf_op jit(solution)/shard_map/ppermute | solution.py:19
  177.8 5.3 %collective-permute-start.24 = (bf16[528,192]{1,0:T(8,128)(2,1)S(1)}, bf16[528,192]{1,0:T(8,128)(2,1)S(1)}, u32[]{:S(2)}, u32[]{:S(2)}) collective-permute-start(bf16[528,192]{1,0:T(8,128)(2,1)S(1)} %maximum_maximum_fusion.7), channel_id=1, source_target_pairs={{0,30},{2,0},{4,2},{6,4},{8,6},{10,8},{12,10},{14,12},{16,14},{18,... | collective-permute-start | bytes 608264 | tf_op jit(solution)/shard_map/ppermute | solution.py:19
  183.1 3.6 %collective-permute-done.21 = bf16[528,192]{1,0:T(8,128)(2,1)S(1)} collective-permute-done((bf16[528,192]{1,0:T(8,128)(2,1)S(1)}, bf16[528,192]{1,0:T(8,128)(2,1)S(1)}, u32[]{:S(2)}, u32[]{:S(2)}) %collective-permute-start.21) | collective-permute-done | bytes 202784 | tf_op jit(solution)/shard_map/ppermute | solution.py:19
  189.9 5.3 %collective-permute-start.26 = (bf16[528,192]{1,0:T(8,128)(2,1)S(1)}, bf16[528,192]{1,0:T(8,128)(2,1)S(1)}, u32[]{:S(2)}, u32[]{:S(2)}) collective-permute-start(bf16[528,192]{1,0:T(8,128)(2,1)S(1)} %maximum_maximum_fusion.9), channel_id=1, source_target_pairs={{0,30},{2,0},{4,2},{6,4},{8,6},{10,8},{12,10},{14,12},{16,14},{18,... | collective-permute-start | bytes 608264 | tf_op jit(solution)/shard_map/ppermute | solution.py:19
  195.2 2.6 %collective-permute-done.23 = bf16[528,192]{1,0:T(8,128)(2,1)S(1)} collective-permute-done((bf16[528,192]{1,0:T(8,128)(2,1)S(1)}, bf16[528,192]{1,0:T(8,128)(2,1)S(1)}, u32[]{:S(2)}, u32[]{:S(2)}) %collective-permute-start.23) | collective-permute-done | bytes 202784 | tf_op jit(solution)/shard_map/ppermute | solution.py:19
  201.1 5.3 %collective-permute-start.28 = (bf16[528,192]{1,0:T(8,128)(2,1)S(1)}, bf16[528,192]{1,0:T(8,128)(2,1)S(1)}, u32[]{:S(2)}, u32[]{:S(2)}) collective-permute-start(bf16[528,192]{1,0:T(8,128)(2,1)S(1)} %maximum_maximum_fusion.11), channel_id=1, source_target_pairs={{0,30},{2,0},{4,2},{6,4},{8,6},{10,8},{12,10},{14,12},{16,14},{18,... | collective-permute-start | bytes 608264 | tf_op jit(solution)/shard_map/ppermute | solution.py:19
  212.0 5.0 %collective-permute-start.30 = (bf16[528,192]{1,0:T(8,128)(2,1)S(1)}, bf16[528,192]{1,0:T(8,128)(2,1)S(1)}, u32[]{:S(2)}, u32[]{:S(2)}) collective-permute-start(bf16[528,192]{1,0:T(8,128)(2,1)S(1)} %maximum_maximum_fusion.13), channel_id=1, source_target_pairs={{0,30},{2,0},{4,2},{6,4},{8,6},{10,8},{12,10},{14,12},{16,14},{18,... | collective-permute-start | bytes 608264 | tf_op jit(solution)/shard_map/ppermute | solution.py:19
  221.2 6.2 %collective-permute-done.29 = bf16[528,192]{1,0:T(8,128)(2,1)S(1)} collective-permute-done((bf16[528,192]{1,0:T(8,128)(2,1)S(1)}, bf16[528,192]{1,0:T(8,128)(2,1)S(1)}, u32[]{:S(2)}, u32[]{:S(2)}) %collective-permute-start.29) | collective-permute-done | bytes 202784 | tf_op jit(solution)/shard_map/ppermute | solution.py:19
  228.6 19.8 %collective-permute-start.31 = (bf16[2,256,192]{2,1,0:T(8,128)(2,1)S(1)}, bf16[2,256,192]{2,1,0:T(8,128)(2,1)S(1)}, u32[]{:S(2)}, u32[]{:S(2)}) collective-permute-start(bf16[2,256,192]{2,1,0:T(8,128)(2,1)S(1)} %pad_maximum_fusion), channel_id=1, source_target_pairs={{32,0},{64,32},{96,64},{128,96},{160,128},{192,160},{224,192},{256... | collective-permute-start | bytes 589832 | tf_op jit(solution)/shard_map/ppermute | solution.py:14
  249.0 3.6 %collective-permute-done.31 = bf16[2,256,192]{2,1,0:T(8,128)(2,1)S(1)} collective-permute-done((bf16[2,256,192]{2,1,0:T(8,128)(2,1)S(1)}, bf16[2,256,192]{2,1,0:T(8,128)(2,1)S(1)}, u32[]{:S(2)}, u32[]{:S(2)}) %collective-permute-start.31) | collective-permute-done | bytes 196640 | tf_op jit(solution)/shard_map/ppermute | solution.py:14
  (191 shorter events, 69.6 us)
Async XLA Ops:
  1.8 24.8 %collective-permute-start = (bf16[2,256,192]{1,2,0:T(8,128)(2,1)S(1)}, bf16[2,256,192]{1,2,0:T(8,128)(2,1)S(1)}, u32[]{:S(2)}, u32[]{:S(2)}) collective-permute-start(bf16[2,256,192]{1,2,0:T(8,128)(2,1)S(1)} %pad_maximum_fusion.1), channel_id=1, source_target_pairs={{0,30},{2,0},{4,2},{6,4},{8,6},{10,8},{12,10},{14,12},{16,14},{18,... | collective-permute-start | bytes 589832 | tf_op jit(solution)/shard_map/ppermute | solution.py:19
  20.5 10.6 %collective-permute-start.7 = (bf16[2,256,192]{1,2,0:T(8,128)(2,1)S(1)}, bf16[2,256,192]{1,2,0:T(8,128)(2,1)S(1)}, u32[]{:S(2)}, u32[]{:S(2)}) collective-permute-start(bf16[2,256,192]{1,2,0:T(8,128)(2,1)S(1)} %pad_maximum_fusion.1), channel_id=1, source_target_pairs={{0,2},{2,4},{4,6},{6,8},{8,10},{10,12},{12,14},{14,16},{16,18},{18... | collective-permute-start | bytes 589832 | tf_op jit(solution)/shard_map/ppermute | solution.py:19
  26.6 7.5 %collective-permute-start.1 = (bf16[2,256,192]{1,2,0:T(8,128)(2,1)S(1)}, bf16[2,256,192]{1,2,0:T(8,128)(2,1)S(1)}, u32[]{:S(2)}, u32[]{:S(2)}) collective-permute-start(bf16[2,256,192]{1,2,0:T(8,128)(2,1)S(1)} %collective-permute-done), channel_id=1, source_target_pairs={{0,30},{2,0},{4,2},{6,4},{8,6},{10,8},{12,10},{14,12},{16,14},{18,... | collective-permute-start | bytes 589832 | tf_op jit(solution)/shard_map/ppermute | solution.py:19
  31.2 8.2 %collective-permute-start.8 = (bf16[2,256,192]{1,2,0:T(8,128)(2,1)S(1)}, bf16[2,256,192]{1,2,0:T(8,128)(2,1)S(1)}, u32[]{:S(2)}, u32[]{:S(2)}) collective-permute-start(bf16[2,256,192]{1,2,0:T(8,128)(2,1)S(1)} %collective-permute-done.7), channel_id=1, source_target_pairs={{0,2},{2,4},{4,6},{6,8},{8,10},{10,12},{12,14},{14,16},{16,18},{18... | collective-permute-start | bytes 589832 | tf_op jit(solution)/shard_map/ppermute | solution.py:19
  34.1 7.9 %collective-permute-start.2 = (bf16[2,256,192]{1,2,0:T(8,128)(2,1)S(1)}, bf16[2,256,192]{1,2,0:T(8,128)(2,1)S(1)}, u32[]{:S(2)}, u32[]{:S(2)}) collective-permute-start(bf16[2,256,192]{1,2,0:T(8,128)(2,1)S(1)} %collective-permute-done.1), channel_id=1, source_target_pairs={{0,30},{2,0},{4,2},{6,4},{8,6},{10,8},{12,10},{14,12},{16,14},{18,... | collective-permute-start | bytes 589832 | tf_op jit(solution)/shard_map/ppermute | solution.py:19
  39.4 7.6 %collective-permute-start.9 = (bf16[2,256,192]{1,2,0:T(8,128)(2,1)S(1)}, bf16[2,256,192]{1,2,0:T(8,128)(2,1)S(1)}, u32[]{:S(2)}, u32[]{:S(2)}) collective-permute-start(bf16[2,256,192]{1,2,0:T(8,128)(2,1)S(1)} %collective-permute-done.8), channel_id=1, source_target_pairs={{0,2},{2,4},{4,6},{6,8},{8,10},{10,12},{12,14},{14,16},{16,18},{18... | collective-permute-start | bytes 589832 | tf_op jit(solution)/shard_map/ppermute | solution.py:19
  42.0 7.6 %collective-permute-start.3 = (bf16[2,256,192]{1,2,0:T(8,128)(2,1)S(1)}, bf16[2,256,192]{1,2,0:T(8,128)(2,1)S(1)}, u32[]{:S(2)}, u32[]{:S(2)}) collective-permute-start(bf16[2,256,192]{1,2,0:T(8,128)(2,1)S(1)} %collective-permute-done.2), channel_id=1, source_target_pairs={{0,30},{2,0},{4,2},{6,4},{8,6},{10,8},{12,10},{14,12},{16,14},{18,... | collective-permute-start | bytes 589832 | tf_op jit(solution)/shard_map/ppermute | solution.py:19
  47.0 7.6 %collective-permute-start.10 = (bf16[2,256,192]{1,2,0:T(8,128)(2,1)S(1)}, bf16[2,256,192]{1,2,0:T(8,128)(2,1)S(1)}, u32[]{:S(2)}, u32[]{:S(2)}) collective-permute-start(bf16[2,256,192]{1,2,0:T(8,128)(2,1)S(1)} %collective-permute-done.9), channel_id=1, source_target_pairs={{0,2},{2,4},{4,6},{6,8},{8,10},{10,12},{12,14},{14,16},{16,18},{18... | collective-permute-start | bytes 589832 | tf_op jit(solution)/shard_map/ppermute | solution.py:19
  49.6 7.6 %collective-permute-start.4 = (bf16[2,256,192]{1,2,0:T(8,128)(2,1)S(1)}, bf16[2,256,192]{1,2,0:T(8,128)(2,1)S(1)}, u32[]{:S(2)}, u32[]{:S(2)}) collective-permute-start(bf16[2,256,192]{1,2,0:T(8,128)(2,1)S(1)} %collective-permute-done.3), channel_id=1, source_target_pairs={{0,30},{2,0},{4,2},{6,4},{8,6},{10,8},{12,10},{14,12},{16,14},{18,... | collective-permute-start | bytes 589832 | tf_op jit(solution)/shard_map/ppermute | solution.py:19
  54.6 7.6 %collective-permute-start.11 = (bf16[2,256,192]{1,2,0:T(8,128)(2,1)S(1)}, bf16[2,256,192]{1,2,0:T(8,128)(2,1)S(1)}, u32[]{:S(2)}, u32[]{:S(2)}) collective-permute-start(bf16[2,256,192]{1,2,0:T(8,128)(2,1)S(1)} %collective-permute-done.10), channel_id=1, source_target_pairs={{0,2},{2,4},{4,6},{6,8},{8,10},{10,12},{12,14},{14,16},{16,18},{18... | collective-permute-start | bytes 589832 | tf_op jit(solution)/shard_map/ppermute | solution.py:19
  57.2 7.6 %collective-permute-start.5 = (bf16[2,256,192]{1,2,0:T(8,128)(2,1)S(1)}, bf16[2,256,192]{1,2,0:T(8,128)(2,1)S(1)}, u32[]{:S(2)}, u32[]{:S(2)}) collective-permute-start(bf16[2,256,192]{1,2,0:T(8,128)(2,1)S(1)} %collective-permute-done.4), channel_id=1, source_target_pairs={{0,30},{2,0},{4,2},{6,4},{8,6},{10,8},{12,10},{14,12},{16,14},{18,... | collective-permute-start | bytes 589832 | tf_op jit(solution)/shard_map/ppermute | solution.py:19
  62.3 7.6 %collective-permute-start.12 = (bf16[2,256,192]{1,2,0:T(8,128)(2,1)S(1)}, bf16[2,256,192]{1,2,0:T(8,128)(2,1)S(1)}, u32[]{:S(2)}, u32[]{:S(2)}) collective-permute-start(bf16[2,256,192]{1,2,0:T(8,128)(2,1)S(1)} %collective-permute-done.11), channel_id=1, source_target_pairs={{0,2},{2,4},{4,6},{6,8},{8,10},{10,12},{12,14},{14,16},{16,18},{18... | collective-permute-start | bytes 589832 | tf_op jit(solution)/shard_map/ppermute | solution.py:19
  64.8 15.4 %collective-permute-start.6 = (bf16[2,256,192]{1,2,0:T(8,128)(2,1)S(1)}, bf16[2,256,192]{1,2,0:T(8,128)(2,1)S(1)}, u32[]{:S(2)}, u32[]{:S(2)}) collective-permute-start(bf16[2,256,192]{1,2,0:T(8,128)(2,1)S(1)} %collective-permute-done.5), channel_id=1, source_target_pairs={{0,30},{2,0},{4,2},{6,4},{8,6},{10,8},{12,10},{14,12},{16,14},{18,... | collective-permute-start | bytes 589832 | tf_op jit(solution)/shard_map/ppermute | solution.py:19
  69.9 8.5 %collective-permute-start.13 = (bf16[2,256,192]{1,2,0:T(8,128)(2,1)S(1)}, bf16[2,256,192]{1,2,0:T(8,128)(2,1)S(1)}, u32[]{:S(2)}, u32[]{:S(2)}) collective-permute-start(bf16[2,256,192]{1,2,0:T(8,128)(2,1)S(1)} %collective-permute-done.12), channel_id=1, source_target_pairs={{0,2},{2,4},{4,6},{6,8},{8,10},{10,12},{12,14},{14,16},{16,18},{18... | collective-permute-start | bytes 589832 | tf_op jit(solution)/shard_map/ppermute | solution.py:19
  78.3 9.7 %collective-permute-start.14 = (bf16[2,256,192]{1,2,0:T(8,128)(2,1)S(1)}, bf16[2,256,192]{1,2,0:T(8,128)(2,1)S(1)}, u32[]{:S(2)}, u32[]{:S(2)}) collective-permute-start(bf16[2,256,192]{1,2,0:T(8,128)(2,1)S(1)} %collective-permute-done.13), channel_id=1, source_target_pairs={{0,2},{2,4},{4,6},{6,8},{8,10},{10,12},{12,14},{14,16},{16,18},{18... | collective-permute-start | bytes 589832 | tf_op jit(solution)/shard_map/ppermute | solution.py:19
  129.4 10.0 %collective-permute-start.15 = (f32[16,192]{1,0:T(8,128)S(1)}, f32[16,192]{1,0:T(8,128)S(1)}, u32[]{:S(2)}, u32[]{:S(2)}) collective-permute-start(f32[16,192]{1,0:T(8,128)S(1)} %reshape.194), channel_id=1, source_target_pairs={{0,1},{1,0},{2,3},{3,2},{4,5},{5,4},{6,7},{7,6},{8,9},{9,8},{10,11... | collective-permute-start | bytes 36872 | tf_op jit(solution)/shard_map/ppermute | solution.py:19
  139.6 8.4 %collective-permute-start.16 = (bf16[528,192]{1,0:T(8,128)(2,1)S(1)}, bf16[528,192]{1,0:T(8,128)(2,1)S(1)}, u32[]{:S(2)}, u32[]{:S(2)}) collective-permute-start(bf16[528,192]{1,0:T(8,128)(2,1)S(1)} %get-tuple-element.90), channel_id=1, source_target_pairs={{0,2},{2,4},{4,6},{6,8},{8,10},{10,12},{12,14},{14,16},{16,18},{18... | collective-permute-start | bytes 608264 | tf_op jit(solution)/shard_map/ppermute | solution.py:19
  141.6 8.0 %collective-permute-start.18 = (bf16[528,192]{1,0:T(8,128)(2,1)S(1)}, bf16[528,192]{1,0:T(8,128)(2,1)S(1)}, u32[]{:S(2)}, u32[]{:S(2)}) collective-permute-start(bf16[528,192]{1,0:T(8,128)(2,1)S(1)} %get-tuple-element.89), channel_id=1, source_target_pairs={{0,30},{2,0},{4,2},{6,4},{8,6},{10,8},{12,10},{14,12},{16,14},{18,... | collective-permute-start | bytes 608264 | tf_op jit(solution)/shard_map/ppermute | solution.py:19
  149.6 11.2 %collective-permute-start.17 = (bf16[528,192]{1,0:T(8,128)(2,1)S(1)}, bf16[528,192]{1,0:T(8,128)(2,1)S(1)}, u32[]{:S(2)}, u32[]{:S(2)}) collective-permute-start(bf16[528,192]{1,0:T(8,128)(2,1)S(1)} %maximum_maximum_fusion.2), channel_id=1, source_target_pairs={{0,2},{2,4},{4,6},{6,8},{8,10},{10,12},{12,14},{14,16},{16,18},{18... | collective-permute-start | bytes 608264 | tf_op jit(solution)/shard_map/ppermute | solution.py:19
  151.7 10.9 %collective-permute-start.20 = (bf16[528,192]{1,0:T(8,128)(2,1)S(1)}, bf16[528,192]{1,0:T(8,128)(2,1)S(1)}, u32[]{:S(2)}, u32[]{:S(2)}) collective-permute-start(bf16[528,192]{1,0:T(8,128)(2,1)S(1)} %maximum_maximum_fusion.3), channel_id=1, source_target_pairs={{0,30},{2,0},{4,2},{6,4},{8,6},{10,8},{12,10},{14,12},{16,14},{18,... | collective-permute-start | bytes 608264 | tf_op jit(solution)/shard_map/ppermute | solution.py:19
  162.7 11.9 %collective-permute-start.19 = (bf16[528,192]{1,0:T(8,128)(2,1)S(1)}, bf16[528,192]{1,0:T(8,128)(2,1)S(1)}, u32[]{:S(2)}, u32[]{:S(2)}) collective-permute-start(bf16[528,192]{1,0:T(8,128)(2,1)S(1)} %maximum_maximum_fusion.4), channel_id=1, source_target_pairs={{0,2},{2,4},{4,6},{6,8},{8,10},{10,12},{12,14},{14,16},{16,18},{18... | collective-permute-start | bytes 608264 | tf_op jit(solution)/shard_map/ppermute | solution.py:19
  164.9 10.7 %collective-permute-start.22 = (bf16[528,192]{1,0:T(8,128)(2,1)S(1)}, bf16[528,192]{1,0:T(8,128)(2,1)S(1)}, u32[]{:S(2)}, u32[]{:S(2)}) collective-permute-start(bf16[528,192]{1,0:T(8,128)(2,1)S(1)} %maximum_maximum_fusion.5), channel_id=1, source_target_pairs={{0,30},{2,0},{4,2},{6,4},{8,6},{10,8},{12,10},{14,12},{16,14},{18,... | collective-permute-start | bytes 608264 | tf_op jit(solution)/shard_map/ppermute | solution.py:19
  175.7 11.0 %collective-permute-start.21 = (bf16[528,192]{1,0:T(8,128)(2,1)S(1)}, bf16[528,192]{1,0:T(8,128)(2,1)S(1)}, u32[]{:S(2)}, u32[]{:S(2)}) collective-permute-start(bf16[528,192]{1,0:T(8,128)(2,1)S(1)} %maximum_maximum_fusion.6), channel_id=1, source_target_pairs={{0,2},{2,4},{4,6},{6,8},{8,10},{10,12},{12,14},{14,16},{16,18},{18... | collective-permute-start | bytes 608264 | tf_op jit(solution)/shard_map/ppermute | solution.py:19
  177.8 9.9 %collective-permute-start.24 = (bf16[528,192]{1,0:T(8,128)(2,1)S(1)}, bf16[528,192]{1,0:T(8,128)(2,1)S(1)}, u32[]{:S(2)}, u32[]{:S(2)}) collective-permute-start(bf16[528,192]{1,0:T(8,128)(2,1)S(1)} %maximum_maximum_fusion.7), channel_id=1, source_target_pairs={{0,30},{2,0},{4,2},{6,4},{8,6},{10,8},{12,10},{14,12},{16,14},{18,... | collective-permute-start | bytes 608264 | tf_op jit(solution)/shard_map/ppermute | solution.py:19
  187.8 10.0 %collective-permute-start.23 = (bf16[528,192]{1,0:T(8,128)(2,1)S(1)}, bf16[528,192]{1,0:T(8,128)(2,1)S(1)}, u32[]{:S(2)}, u32[]{:S(2)}) collective-permute-start(bf16[528,192]{1,0:T(8,128)(2,1)S(1)} %maximum_maximum_fusion.8), channel_id=1, source_target_pairs={{0,2},{2,4},{4,6},{6,8},{8,10},{10,12},{12,14},{14,16},{16,18},{18... | collective-permute-start | bytes 608264 | tf_op jit(solution)/shard_map/ppermute | solution.py:19
  189.9 9.0 %collective-permute-start.26 = (bf16[528,192]{1,0:T(8,128)(2,1)S(1)}, bf16[528,192]{1,0:T(8,128)(2,1)S(1)}, u32[]{:S(2)}, u32[]{:S(2)}) collective-permute-start(bf16[528,192]{1,0:T(8,128)(2,1)S(1)} %maximum_maximum_fusion.9), channel_id=1, source_target_pairs={{0,30},{2,0},{4,2},{6,4},{8,6},{10,8},{12,10},{14,12},{16,14},{18,... | collective-permute-start | bytes 608264 | tf_op jit(solution)/shard_map/ppermute | solution.py:19
  199.0 9.2 %collective-permute-start.25 = (bf16[528,192]{1,0:T(8,128)(2,1)S(1)}, bf16[528,192]{1,0:T(8,128)(2,1)S(1)}, u32[]{:S(2)}, u32[]{:S(2)}) collective-permute-start(bf16[528,192]{1,0:T(8,128)(2,1)S(1)} %maximum_maximum_fusion.10), channel_id=1, source_target_pairs={{0,2},{2,4},{4,6},{6,8},{8,10},{10,12},{12,14},{14,16},{16,18},{18... | collective-permute-start | bytes 608264 | tf_op jit(solution)/shard_map/ppermute | solution.py:19
  201.1 8.7 %collective-permute-start.28 = (bf16[528,192]{1,0:T(8,128)(2,1)S(1)}, bf16[528,192]{1,0:T(8,128)(2,1)S(1)}, u32[]{:S(2)}, u32[]{:S(2)}) collective-permute-start(bf16[528,192]{1,0:T(8,128)(2,1)S(1)} %maximum_maximum_fusion.11), channel_id=1, source_target_pairs={{0,30},{2,0},{4,2},{6,4},{8,6},{10,8},{12,10},{14,12},{16,14},{18,... | collective-permute-start | bytes 608264 | tf_op jit(solution)/shard_map/ppermute | solution.py:19
  209.9 8.9 %collective-permute-start.27 = (bf16[528,192]{1,0:T(8,128)(2,1)S(1)}, bf16[528,192]{1,0:T(8,128)(2,1)S(1)}, u32[]{:S(2)}, u32[]{:S(2)}) collective-permute-start(bf16[528,192]{1,0:T(8,128)(2,1)S(1)} %maximum_maximum_fusion.12), channel_id=1, source_target_pairs={{0,2},{2,4},{4,6},{6,8},{8,10},{10,12},{12,14},{14,16},{16,18},{18... | collective-permute-start | bytes 608264 | tf_op jit(solution)/shard_map/ppermute | solution.py:19
  212.0 9.2 %collective-permute-start.30 = (bf16[528,192]{1,0:T(8,128)(2,1)S(1)}, bf16[528,192]{1,0:T(8,128)(2,1)S(1)}, u32[]{:S(2)}, u32[]{:S(2)}) collective-permute-start(bf16[528,192]{1,0:T(8,128)(2,1)S(1)} %maximum_maximum_fusion.13), channel_id=1, source_target_pairs={{0,30},{2,0},{4,2},{6,4},{8,6},{10,8},{12,10},{14,12},{16,14},{18,... | collective-permute-start | bytes 608264 | tf_op jit(solution)/shard_map/ppermute | solution.py:19
  219.0 8.4 %collective-permute-start.29 = (bf16[528,192]{1,0:T(8,128)(2,1)S(1)}, bf16[528,192]{1,0:T(8,128)(2,1)S(1)}, u32[]{:S(2)}, u32[]{:S(2)}) collective-permute-start(bf16[528,192]{1,0:T(8,128)(2,1)S(1)} %maximum_maximum_fusion.14), channel_id=1, source_target_pairs={{0,2},{2,4},{4,6},{6,8},{8,10},{10,12},{12,14},{14,16},{16,18},{18... | collective-permute-start | bytes 608264 | tf_op jit(solution)/shard_map/ppermute | solution.py:19
  228.6 24.0 %collective-permute-start.31 = (bf16[2,256,192]{2,1,0:T(8,128)(2,1)S(1)}, bf16[2,256,192]{2,1,0:T(8,128)(2,1)S(1)}, u32[]{:S(2)}, u32[]{:S(2)}) collective-permute-start(bf16[2,256,192]{2,1,0:T(8,128)(2,1)S(1)} %pad_maximum_fusion), channel_id=1, source_target_pairs={{32,0},{64,32},{96,64},{128,96},{160,128},{192,160},{224,192},{256... | collective-permute-start | bytes 589832 | tf_op jit(solution)/shard_map/ppermute | solution.py:14
  (12 other events, 473.6 us)

commit v6 on v4

--- a/solution.py
+++ b/solution.py
@@ -161,9 +161,9 @@
     )
     attended = attended.astype(jnp.bfloat16).reshape(length, -1)
     out_parts = jnp.einsum(
-        "lc,cmf->mlf",
+        "lc,mcf->mlf",
         attended,
-        w_output.reshape(w_output.shape[0], n_mp, share),
+        jnp.transpose(w_output.reshape(w_output.shape[0], n_mp, share), (1, 0, 2)),
         preferred_element_type=jnp.float32,
     ).astype(jnp.bfloat16)
     attention_gradient = jnp.dot(whole_grad, w_output.T, preferred_element_type=jnp.float32).astype(
@@ -191,16 +191,23 @@
         "munr,nmuy->rmy", score_gradient, query_head_split, preferred_element_type=jnp.float32
     )
     key_gradient = key_gradient.astype(jnp.bfloat16).reshape(length, -1)
-    normed_grad = jnp.dot(query_grad, w_query.T, preferred_element_type=jnp.float32)
-    normed_grad = normed_grad + jnp.dot(key_gradient, w_key.T, preferred_element_type=jnp.float32)
-    normed_grad = normed_grad + jnp.dot(
-        value_gradient, w_value.T, preferred_element_type=jnp.float32
-    )
-    weighted = gain_rows * normed_grad
-    row_stat = jnp.mean(unit_rows * weighted, axis=1, keepdims=True)
-    grad_parts = ((weighted - unit_rows * row_stat) * inverse).astype(jnp.bfloat16)
-    grad_parts = jnp.transpose(grad_parts.reshape(length, n_mp, share), (1, 0, 2))
-    gain_parts = jnp.sum(normed_grad * unit_rows, axis=0).reshape(n_mp, share)
+    unit_chunks = gathered[:, 0].astype(jnp.float32) * inverse.reshape(1, length, 1)
+    gain_chunks = gain_rows.reshape(n_mp, 1, share)
+    normed_grad = jnp.einsum(
+        "th,mfh->mtf", query_grad, w_query.reshape(n_mp, share, -1), preferred_element_type=jnp.float32
+    )
+    normed_grad = normed_grad + jnp.einsum(
+        "th,mfh->mtf", key_gradient, w_key.reshape(n_mp, share, -1), preferred_element_type=jnp.float32
+    )
+    normed_grad = normed_grad + jnp.einsum(
+        "th,mfh->mtf", value_gradient, w_value.reshape(n_mp, share, -1), preferred_element_type=jnp.float32
+    )
+    weighted = gain_chunks * normed_grad
+    row_stat = jnp.sum(unit_chunks * weighted, axis=(0, 2), keepdims=True) / (n_mp * share)
+    grad_parts = ((weighted - unit_chunks * row_stat) * inverse.reshape(1, length, 1)).astype(
+        jnp.bfloat16
+    )
+    gain_parts = jnp.sum(normed_grad * unit_chunks, axis=1)
     shares, gain_share = ring_reduce_scatter(
         jnp.concatenate([out_parts, grad_parts], axis=1), gain_parts, "mp"
     )

time: 239 us -> 266 us (1.11)
  waiting for transfers between devices: 41.5 us -> 56.7 us
  other arithmetic: 22.1 us -> 14.5 us
  local copies, waits for them, and re-layouts: 15.6 us -> 23.1 us
  matrix products: 20.5 us -> 27.1 us
  starting transfers between devices: 136 us -> 141 us
    ppermute x31, waiting for transfers between devices: 41.5 us -> 56.7 us  [shift(): lax.ppermute(x, axis, [(i, (i + by) % length) for i in range(length)])]
    transpose x0 -> x2, local copies, waits for them, and re-layouts: none -> 7.03 us  [local(): jnp.transpose(gathered[:, 1], (1, 0, 2)).reshape(length, n_mp * share)]
    unnamed x69 -> x67, local copies, waits for them, and re-layouts: 2.9 us -> 8.34 us
    ppermute x31, starting transfers between devices: 117 us -> 121 us  [shift(): lax.ppermute(x, axis, [(i, (i + by) % length) for i in range(length)])]
    convert_element_type x4 -> x2, other arithmetic: 9.39 us -> 5.91 us  [the longest x1 3.97 us: local(): ((weighted - unit_chunks * row_stat) * inverse.reshape(1, length, 1)).ast...]
    dot_general x3, matrix products: 12.9 us -> 16.3 us  [the longest x1 8.11 us: local(): jnp.einsum('th,mfh->mtf', query_grad, w_query.reshape(n_mp, share, -1), p...]
    convert_element_type x2 -> x1, local copies, waits for them, and re-layouts: 5.36 us -> 3.06 us  [local(): normed = (unit_rows * gain_rows).astype(jnp.bfloat16)]
  transfers between devices with their start and end apart: 32 -> 32, of which waited for: 16 -> 23; matrix products, arithmetic and copies ran while one was open for 4% -> 3% of each run, Pallas kernels for 0% -> 0%
where the time goes in v6:
time: 266 us; the launch traced here: 265 us
  starting transfers between devices  141 us (53%)
  waiting for transfers between devices  56.7 us (21%)
  matrix products  27.1 us (10%)
  local copies, waits for them, and re-layouts  23.1 us (9%)
  other arithmetic  14.5 us (5%)
    ppermute x31, starting transfers between devices, shift(): lax.ppermute(x, axis, [(i, (i + by) % length) for i in range(length)])  121 us
    ppermute x31, waiting for transfers between devices, shift(): lax.ppermute(x, axis, [(i, (i + by) % length) for i in range(length)])  56.7 us
    ppermute x1, starting transfers between devices, from_behind(): return lax.ppermute(x, axis, pairs)  19.9 us
    unnamed x67, local copies, waits for them, and re-layouts  8.34 us
    dot_general x1, matrix products, local(): jnp.einsum('th,mfh->mtf', query_grad, w_query.reshape(n_mp, share, -1), p...  8.11 us
    transpose x2, local copies, waits for them, and re-layouts, local(): jnp.transpose(gathered[:, 1], (1, 0, 2)).reshape(length, n_mp * share)  7.03 us
  transfers between devices with their start and end apart: 32, of which 23 were waited for; matrix products, arithmetic and copies ran while one was open for 3% of the time, Pallas kernels for 0%

profile of v6, /device:TPU:1, one launch (start us, length us, event | category | flops | bytes accessed | tf_op | source)
XLA Modules:
  0.0 264.9 jit_solution(16424268350755955373)
XLA Ops:
  2.8 18.8 %collective-permute-start = (bf16[2,256,192]{2,1,0:T(8,128)(2,1)S(1)}, bf16[2,256,192]{2,1,0:T(8,128)(2,1)S(1)}, u32[]{:S(2)}, u32[]{:S(2)}) collective-permute-start(bf16[2,256,192]{2,1,0:T(8,128)(2,1)S(1)} %pad_maximum_fusion), channel_id=1, source_target_pairs={{0,30},{2,0},{4,2},{6,4},{8,6},{10,8},{12,10},{14,12},{16,14},{18,... | collective-permute-start | bytes 589832 | tf_op jit(solution)/shard_map/ppermute | solution.py:19
  26.5 5.3 %collective-permute-start.1 = (bf16[2,256,192]{2,1,0:T(8,128)(2,1)S(1)}, bf16[2,256,192]{2,1,0:T(8,128)(2,1)S(1)}, u32[]{:S(2)}, u32[]{:S(2)}) collective-permute-start(bf16[2,256,192]{2,1,0:T(8,128)(2,1)S(1)} %collective-permute-done), channel_id=1, source_target_pairs={{0,30},{2,0},{4,2},{6,4},{8,6},{10,8},{12,10},{14,12},{16,14},{18,... | collective-permute-start | bytes 589832 | tf_op jit(solution)/shard_map/ppermute | solution.py:19
  35.9 5.3 %collective-permute-start.2 = (bf16[2,256,192]{2,1,0:T(8,128)(2,1)S(1)}, bf16[2,256,192]{2,1,0:T(8,128)(2,1)S(1)}, u32[]{:S(2)}, u32[]{:S(2)}) collective-permute-start(bf16[2,256,192]{2,1,0:T(8,128)(2,1)S(1)} %collective-permute-done.1), channel_id=1, source_target_pairs={{0,30},{2,0},{4,2},{6,4},{8,6},{10,8},{12,10},{14,12},{16,14},{18,... | collective-permute-start | bytes 589832 | tf_op jit(solution)/shard_map/ppermute | solution.py:19
  44.5 5.0 %collective-permute-start.3 = (bf16[2,256,192]{2,1,0:T(8,128)(2,1)S(1)}, bf16[2,256,192]{2,1,0:T(8,128)(2,1)S(1)}, u32[]{:S(2)}, u32[]{:S(2)}) collective-permute-start(bf16[2,256,192]{2,1,0:T(8,128)(2,1)S(1)} %collective-permute-done.2), channel_id=1, source_target_pairs={{0,30},{2,0},{4,2},{6,4},{8,6},{10,8},{12,10},{14,12},{16,14},{18,... | collective-permute-start | bytes 589832 | tf_op jit(solution)/shard_map/ppermute | solution.py:19
  52.8 5.0 %collective-permute-start.4 = (bf16[2,256,192]{2,1,0:T(8,128)(2,1)S(1)}, bf16[2,256,192]{2,1,0:T(8,128)(2,1)S(1)}, u32[]{:S(2)}, u32[]{:S(2)}) collective-permute-start(bf16[2,256,192]{2,1,0:T(8,128)(2,1)S(1)} %collective-permute-done.3), channel_id=1, source_target_pairs={{0,30},{2,0},{4,2},{6,4},{8,6},{10,8},{12,10},{14,12},{16,14},{18,... | collective-permute-start | bytes 589832 | tf_op jit(solution)/shard_map/ppermute | solution.py:19
  61.1 5.0 %collective-permute-start.5 = (bf16[2,256,192]{2,1,0:T(8,128)(2,1)S(1)}, bf16[2,256,192]{2,1,0:T(8,128)(2,1)S(1)}, u32[]{:S(2)}, u32[]{:S(2)}) collective-permute-start(bf16[2,256,192]{2,1,0:T(8,128)(2,1)S(1)} %collective-permute-done.4), channel_id=1, source_target_pairs={{0,30},{2,0},{4,2},{6,4},{8,6},{10,8},{12,10},{14,12},{16,14},{18,... | collective-permute-start | bytes 589832 | tf_op jit(solution)/shard_map/ppermute | solution.py:19
  69.5 5.0 %collective-permute-start.6 = (bf16[2,256,192]{2,1,0:T(8,128)(2,1)S(1)}, bf16[2,256,192]{2,1,0:T(8,128)(2,1)S(1)}, u32[]{:S(2)}, u32[]{:S(2)}) collective-permute-start(bf16[2,256,192]{2,1,0:T(8,128)(2,1)S(1)} %collective-permute-done.5), channel_id=1, source_target_pairs={{0,30},{2,0},{4,2},{6,4},{8,6},{10,8},{12,10},{14,12},{16,14},{18,... | collective-permute-start | bytes 589832 | tf_op jit(solution)/shard_map/ppermute | solution.py:19
  76.4 7.5 %collective-permute-done.13 = bf16[2,256,192]{2,1,0:T(8,128)(2,1)S(1)} collective-permute-done((bf16[2,256,192]{2,1,0:T(8,128)(2,1)S(1)}, bf16[2,256,192]{2,1,0:T(8,128)(2,1)S(1)}, u32[]{:S(2)}, u32[]{:S(2)}) %collective-permute-start.13) | collective-permute-done | bytes 196640 | tf_op jit(solution)/shard_map/ppermute | solution.py:19
  86.1 8.4 %collective-permute-done.14 = bf16[2,256,192]{2,1,0:T(8,128)(2,1)S(1)} collective-permute-done((bf16[2,256,192]{2,1,0:T(8,128)(2,1)S(1)}, bf16[2,256,192]{2,1,0:T(8,128)(2,1)S(1)}, u32[]{:S(2)}, u32[]{:S(2)}) %collective-permute-start.14) | collective-permute-done | bytes 196640 | tf_op jit(solution)/shard_map/ppermute | solution.py:19
  95.8 2.7 %copy-done.5 = bf16[32,2,256,192]{3,2,0,1:T(8,128)(2,1)} copy-done((bf16[32,2,256,192]{3,2,0,1:T(8,128)(2,1)}, bf16[32,2,256,192]{3,2,0,1:T(8,128)(2,1)S(1)}, u32[]{:S(2)}) %copy-start.5) | copy-done | bytes 6291480
  100.4 3.1 %copy.309 = bf16[256,16,192]{0,2,1:T(8,128)(2,1)S(1)} copy(bf16[256,16,192]{2,0,1:T(8,128)(2,1)} %fusion.11) | data formatting | bytes 3145728 | tf_op jit(solution)/shard_map/convert_element_type | solution.py:128
  106.6 3.1 %dynamic-slice_bitcast_fusion = bf16[256,16,192]{2,0,1:T(8,128)(2,1)} fusion(bf16[32,2,256,192]{3,2,0,1:T(8,128)(2,1)} %copy-done.5, s32[]{:T(128)S(6)} %select_n.194, s32[]{:T(128)S(6)} %add.531), kind=kLoop, calls=%fused_computation.48 | loop fusion | bytes 3145736 | tf_op jit(solution)/shard_map/transpose | solution.py:123
  109.8 3.9 %copy.317 = bf16[256,16,192]{0,2,1:T(8,128)(2,1)} copy(bf16[256,16,192]{2,0,1:T(8,128)(2,1)} %dynamic-slice_bitcast_fusion) | data formatting | bytes 3145728 | tf_op jit(solution)/shard_map/transpose | solution.py:123
  119.0 4.1 %fusion.36 = f32[256,16,192]{2,0,1:T(8,128)} fusion(bf16[16,192,128]{2,1,0:T(8,128)(2,1)} %bitcast.333, bf16[256,2,128]{0,2,1:T(8,128)(2,1)S(1)} %bitcast.343, bf16[2,256,256]{1,2,0:T(8,128)(2,1)S(1)} %fusion.70), kind=kOutput, calls=%fused_computation.79 | convolution fusion | flops 234913792 | bytes 4325376 | tf_op jit(solution)/shard_map/th,mfh->mtf/dot_general | solution.py:199
  123.1 4.0 %fusion.37 = f32[256,16,192]{2,0,1:T(8,128)} fusion(bf16[16,192,128]{2,1,0:T(8,128)(2,1)S(1)} %bitcast.332, bf16[256,2,128]{0,2,1:T(8,128)(2,1)} %bitcast.346, f32[1,2,256,256]{2,3,1,0:T(8,128)S(1)} %get-tuple-element.78, f32[2,256]{1,0:T(2,128)S(1)} %fusion.53, f32[2,256]{1,0:T(2,128)S(1)} %get-tuple-element.77, pred[256,256]{0,1:T(8,128)(4,1)S(1)} %copy.310), kind=kOutput, calls=%fused_computation.80 | convolution fusion | flops 235438080 | bytes 4657152 | tf_op jit(solution)/shard_map/th,mfh->mtf/dot_general | solution.py:202
  127.1 8.1 %fusion.5 = (f32[256]{0:T(256)S(1)}, f32[16,192]{1,0:T(8,128)S(1)}, f32[256,16,192]{2,0,1:T(8,128)}) fusion(f32[16,192]{1,0:T(8,128)S(1)} %copy-done.10, f32[256]{0:T(256)S(1)} %add_rsqrt_fusion, bf16[32,2,256,192]{3,2,0,1:T(8,128)(2,1)} %copy-done.5, s32[]{:T(128)S(6)} %select_n.194, f32[256,16,192]{2,0,1:T(8,128)} %fusion.37, ...), kind=kOutput, calls=%fused_computation.39 | convolution fusion | flops 409727744 | bytes 12740612 | tf_op jit(solution)/shard_map/th,mfh->mtf/dot_general | solution.py:196
  137.6 4.3 %copy.316 = bf16[256,16,192]{2,0,1:T(8,128)(2,1)} copy(f32[256,16,192]{0,2,1:T(8,128)} %bitcast.328) | data formatting | bytes 4718592 | tf_op jit(solution)/shard_map/lc,mcf->mlf/dot_general | solution.py:163
  141.9 4.0 %fusion.8 = bf16[16,256,192]{2,1,0:T(8,128)(2,1)S(1)} fusion(f32[256,16,192]{2,0,1:T(8,128)} %get-tuple-element.81, f32[256]{0:T(256)S(1)} %broadcast_multiply_fusion, f32[16,192]{1,0:T(8,128)S(1)} %copy-done.10, f32[256]{0:T(256)S(1)} %add_rsqrt_fusion, bf16[32,2,256,192]{3,2,0,1:T(8,128)(2,1)} %copy-done.5, s32[]{:T(128)S(6)} %select_n.194), kind=kLoop, calls=%fused_computation.42 | loop fusion | flops 5505024 | bytes 6305796 | tf_op jit(solution)/shard_map/convert_element_type | solution.py:207
  149.6 5.1 %collective-permute-start.17 = (bf16[528,192]{1,0:T(8,128)(2,1)S(1)}, bf16[528,192]{1,0:T(8,128)(2,1)S(1)}, u32[]{:S(2)}, u32[]{:S(2)}) collective-permute-start(bf16[528,192]{1,0:T(8,128)(2,1)S(1)} %get-tuple-element.75), channel_id=1, source_target_pairs={{0,30},{2,0},{4,2},{6,4},{8,6},{10,8},{12,10},{14,12},{16,14},{18,... | collective-permute-start | bytes 608264 | tf_op jit(solution)/shard_map/ppermute | solution.py:19
  160.0 5.0 %collective-permute-start.19 = (bf16[528,192]{1,0:T(8,128)(2,1)S(1)}, bf16[528,192]{1,0:T(8,128)(2,1)S(1)}, u32[]{:S(2)}, u32[]{:S(2)}) collective-permute-start(bf16[528,192]{1,0:T(8,128)(2,1)S(1)} %maximum_maximum_fusion.3), channel_id=1, source_target_pairs={{0,30},{2,0},{4,2},{6,4},{8,6},{10,8},{12,10},{14,12},{16,14},{18,... | collective-permute-start | bytes 608264 | tf_op jit(solution)/shard_map/ppermute | solution.py:19
  165.0 3.8 %collective-permute-done.16 = bf16[528,192]{1,0:T(8,128)(2,1)S(1)} collective-permute-done((bf16[528,192]{1,0:T(8,128)(2,1)S(1)}, bf16[528,192]{1,0:T(8,128)(2,1)S(1)}, u32[]{:S(2)}, u32[]{:S(2)}) %collective-permute-start.16) | collective-permute-done | bytes 202784 | tf_op jit(solution)/shard_map/ppermute | solution.py:19
  173.3 5.1 %collective-permute-start.21 = (bf16[528,192]{1,0:T(8,128)(2,1)S(1)}, bf16[528,192]{1,0:T(8,128)(2,1)S(1)}, u32[]{:S(2)}, u32[]{:S(2)}) collective-permute-start(bf16[528,192]{1,0:T(8,128)(2,1)S(1)} %maximum_maximum_fusion.5), channel_id=1, source_target_pairs={{0,30},{2,0},{4,2},{6,4},{8,6},{10,8},{12,10},{14,12},{16,14},{18,... | collective-permute-start | bytes 608264 | tf_op jit(solution)/shard_map/ppermute | solution.py:19
  178.3 4.4 %collective-permute-done.18 = bf16[528,192]{1,0:T(8,128)(2,1)S(1)} collective-permute-done((bf16[528,192]{1,0:T(8,128)(2,1)S(1)}, bf16[528,192]{1,0:T(8,128)(2,1)S(1)}, u32[]{:S(2)}, u32[]{:S(2)}) %collective-permute-start.18) | collective-permute-done | bytes 202784 | tf_op jit(solution)/shard_map/ppermute | solution.py:19
  186.0 5.3 %collective-permute-start.23 = (bf16[528,192]{1,0:T(8,128)(2,1)S(1)}, bf16[528,192]{1,0:T(8,128)(2,1)S(1)}, u32[]{:S(2)}, u32[]{:S(2)}) collective-permute-start(bf16[528,192]{1,0:T(8,128)(2,1)S(1)} %maximum_maximum_fusion.7), channel_id=1, source_target_pairs={{0,30},{2,0},{4,2},{6,4},{8,6},{10,8},{12,10},{14,12},{16,14},{18,... | collective-permute-start | bytes 608264 | tf_op jit(solution)/shard_map/ppermute | solution.py:19
  191.3 3.5 %collective-permute-done.20 = bf16[528,192]{1,0:T(8,128)(2,1)S(1)} collective-permute-done((bf16[528,192]{1,0:T(8,128)(2,1)S(1)}, bf16[528,192]{1,0:T(8,128)(2,1)S(1)}, u32[]{:S(2)}, u32[]{:S(2)}) %collective-permute-start.20) | collective-permute-done | bytes 202784 | tf_op jit(solution)/shard_map/ppermute | solution.py:19
  198.0 5.3 %collective-permute-start.25 = (bf16[528,192]{1,0:T(8,128)(2,1)S(1)}, bf16[528,192]{1,0:T(8,128)(2,1)S(1)}, u32[]{:S(2)}, u32[]{:S(2)}) collective-permute-start(bf16[528,192]{1,0:T(8,128)(2,1)S(1)} %maximum_maximum_fusion.9), channel_id=1, source_target_pairs={{0,30},{2,0},{4,2},{6,4},{8,6},{10,8},{12,10},{14,12},{16,14},{18,... | collective-permute-start | bytes 608264 | tf_op jit(solution)/shard_map/ppermute | solution.py:19
  203.3 2.5 collective-permute-done.22
  208.9 5.5 %collective-permute-start.27 = (bf16[528,192]{1,0:T(8,128)(2,1)S(1)}, bf16[528,192]{1,0:T(8,128)(2,1)S(1)}, u32[]{:S(2)}, u32[]{:S(2)}) collective-permute-start(bf16[528,192]{1,0:T(8,128)(2,1)S(1)} %maximum_maximum_fusion.11), channel_id=1, source_target_pairs={{0,30},{2,0},{4,2},{6,4},{8,6},{10,8},{12,10},{14,12},{16,14},{18,... | collective-permute-start | bytes 608264 | tf_op jit(solution)/shard_map/ppermute | solution.py:19
  220.1 5.0 %collective-permute-start.29 = (bf16[528,192]{1,0:T(8,128)(2,1)S(1)}, bf16[528,192]{1,0:T(8,128)(2,1)S(1)}, u32[]{:S(2)}, u32[]{:S(2)}) collective-permute-start(bf16[528,192]{1,0:T(8,128)(2,1)S(1)} %maximum_maximum_fusion.13), channel_id=1, source_target_pairs={{0,30},{2,0},{4,2},{6,4},{8,6},{10,8},{12,10},{14,12},{16,14},{18,... | collective-permute-start | bytes 608264 | tf_op jit(solution)/shard_map/ppermute | solution.py:19
  229.4 6.2 %collective-permute-done.28 = bf16[528,192]{1,0:T(8,128)(2,1)S(1)} collective-permute-done((bf16[528,192]{1,0:T(8,128)(2,1)S(1)}, bf16[528,192]{1,0:T(8,128)(2,1)S(1)}, u32[]{:S(2)}, u32[]{:S(2)}) %collective-permute-start.28) | collective-permute-done | bytes 202784 | tf_op jit(solution)/shard_map/ppermute | solution.py:19
  236.8 19.9 %collective-permute-start.30 = (bf16[2,256,192]{2,1,0:T(8,128)(2,1)S(1)}, bf16[2,256,192]{2,1,0:T(8,128)(2,1)S(1)}, u32[]{:S(2)}, u32[]{:S(2)}) collective-permute-start(bf16[2,256,192]{2,1,0:T(8,128)(2,1)S(1)} %pad_maximum_fusion.1), channel_id=1, source_target_pairs={{32,0},{64,32},{96,64},{128,96},{160,128},{192,160},{224,192},{256... | collective-permute-start | bytes 589832 | tf_op jit(solution)/shard_map/ppermute | solution.py:14
  256.7 4.7 %collective-permute-start.31 = (f32[192]{0:T(256)S(1)}, f32[192]{0:T(256)S(1)}, u32[]{:S(2)}, u32[]{:S(2)}) collective-permute-start(f32[192]{0:T(256)S(1)} %bitcast.347), channel_id=1, source_target_pairs={{0,1},{1,0},{2,3},{3,2},{4,5},{5,4},{6,7},{7,6},{8,9},{9,8},{10,11... | collective-permute-start | bytes 2312 | tf_op jit(solution)/shard_map/ppermute | solution.py:19
  (196 shorter events, 78.7 us)
Async XLA Ops:
  2.8 23.7 %collective-permute-start = (bf16[2,256,192]{2,1,0:T(8,128)(2,1)S(1)}, bf16[2,256,192]{2,1,0:T(8,128)(2,1)S(1)}, u32[]{:S(2)}, u32[]{:S(2)}) collective-permute-start(bf16[2,256,192]{2,1,0:T(8,128)(2,1)S(1)} %pad_maximum_fusion), channel_id=1, source_target_pairs={{0,30},{2,0},{4,2},{6,4},{8,6},{10,8},{12,10},{14,12},{16,14},{18,... | collective-permute-start | bytes 589832 | tf_op jit(solution)/shard_map/ppermute | solution.py:19
  21.6 10.3 %collective-permute-start.7 = (bf16[2,256,192]{2,1,0:T(8,128)(2,1)S(1)}, bf16[2,256,192]{2,1,0:T(8,128)(2,1)S(1)}, u32[]{:S(2)}, u32[]{:S(2)}) collective-permute-start(bf16[2,256,192]{2,1,0:T(8,128)(2,1)S(1)} %pad_maximum_fusion), channel_id=1, source_target_pairs={{0,2},{2,4},{4,6},{6,8},{8,10},{10,12},{12,14},{14,16},{16,18},{18... | collective-permute-start | bytes 589832 | tf_op jit(solution)/shard_map/ppermute | solution.py:19
  26.5 9.3 %collective-permute-start.1 = (bf16[2,256,192]{2,1,0:T(8,128)(2,1)S(1)}, bf16[2,256,192]{2,1,0:T(8,128)(2,1)S(1)}, u32[]{:S(2)}, u32[]{:S(2)}) collective-permute-start(bf16[2,256,192]{2,1,0:T(8,128)(2,1)S(1)} %collective-permute-done), channel_id=1, source_target_pairs={{0,30},{2,0},{4,2},{6,4},{8,6},{10,8},{12,10},{14,12},{16,14},{18,... | collective-permute-start | bytes 589832 | tf_op jit(solution)/shard_map/ppermute | solution.py:19
  31.9 9.3 %collective-permute-start.8 = (bf16[2,256,192]{2,1,0:T(8,128)(2,1)S(1)}, bf16[2,256,192]{2,1,0:T(8,128)(2,1)S(1)}, u32[]{:S(2)}, u32[]{:S(2)}) collective-permute-start(bf16[2,256,192]{2,1,0:T(8,128)(2,1)S(1)} %collective-permute-done.7), channel_id=1, source_target_pairs={{0,2},{2,4},{4,6},{6,8},{8,10},{10,12},{12,14},{14,16},{16,18},{18... | collective-permute-start | bytes 589832 | tf_op jit(solution)/shard_map/ppermute | solution.py:19
  35.9 8.6 %collective-permute-start.2 = (bf16[2,256,192]{2,1,0:T(8,128)(2,1)S(1)}, bf16[2,256,192]{2,1,0:T(8,128)(2,1)S(1)}, u32[]{:S(2)}, u32[]{:S(2)}) collective-permute-start(bf16[2,256,192]{2,1,0:T(8,128)(2,1)S(1)} %collective-permute-done.1), channel_id=1, source_target_pairs={{0,30},{2,0},{4,2},{6,4},{8,6},{10,8},{12,10},{14,12},{16,14},{18,... | collective-permute-start | bytes 589832 | tf_op jit(solution)/shard_map/ppermute | solution.py:19
  41.2 8.3 %collective-permute-start.9 = (bf16[2,256,192]{2,1,0:T(8,128)(2,1)S(1)}, bf16[2,256,192]{2,1,0:T(8,128)(2,1)S(1)}, u32[]{:S(2)}, u32[]{:S(2)}) collective-permute-start(bf16[2,256,192]{2,1,0:T(8,128)(2,1)S(1)} %collective-permute-done.8), channel_id=1, source_target_pairs={{0,2},{2,4},{4,6},{6,8},{8,10},{10,12},{12,14},{14,16},{16,18},{18... | collective-permute-start | bytes 589832 | tf_op jit(solution)/shard_map/ppermute | solution.py:19
  44.5 8.3 %collective-permute-start.3 = (bf16[2,256,192]{2,1,0:T(8,128)(2,1)S(1)}, bf16[2,256,192]{2,1,0:T(8,128)(2,1)S(1)}, u32[]{:S(2)}, u32[]{:S(2)}) collective-permute-start(bf16[2,256,192]{2,1,0:T(8,128)(2,1)S(1)} %collective-permute-done.2), channel_id=1, source_target_pairs={{0,30},{2,0},{4,2},{6,4},{8,6},{10,8},{12,10},{14,12},{16,14},{18,... | collective-permute-start | bytes 589832 | tf_op jit(solution)/shard_map/ppermute | solution.py:19
  49.5 8.3 %collective-permute-start.10 = (bf16[2,256,192]{2,1,0:T(8,128)(2,1)S(1)}, bf16[2,256,192]{2,1,0:T(8,128)(2,1)S(1)}, u32[]{:S(2)}, u32[]{:S(2)}) collective-permute-start(bf16[2,256,192]{2,1,0:T(8,128)(2,1)S(1)} %collective-permute-done.9), channel_id=1, source_target_pairs={{0,2},{2,4},{4,6},{6,8},{8,10},{10,12},{12,14},{14,16},{16,18},{18... | collective-permute-start | bytes 589832 | tf_op jit(solution)/shard_map/ppermute | solution.py:19
  52.8 8.3 %collective-permute-start.4 = (bf16[2,256,192]{2,1,0:T(8,128)(2,1)S(1)}, bf16[2,256,192]{2,1,0:T(8,128)(2,1)S(1)}, u32[]{:S(2)}, u32[]{:S(2)}) collective-permute-start(bf16[2,256,192]{2,1,0:T(8,128)(2,1)S(1)} %collective-permute-done.3), channel_id=1, source_target_pairs={{0,30},{2,0},{4,2},{6,4},{8,6},{10,8},{12,10},{14,12},{16,14},{18,... | collective-permute-start | bytes 589832 | tf_op jit(solution)/shard_map/ppermute | solution.py:19
  57.9 8.3 %collective-permute-start.11 = (bf16[2,256,192]{2,1,0:T(8,128)(2,1)S(1)}, bf16[2,256,192]{2,1,0:T(8,128)(2,1)S(1)}, u32[]{:S(2)}, u32[]{:S(2)}) collective-permute-start(bf16[2,256,192]{2,1,0:T(8,128)(2,1)S(1)} %collective-permute-done.10), channel_id=1, source_target_pairs={{0,2},{2,4},{4,6},{6,8},{8,10},{10,12},{12,14},{14,16},{16,18},{18... | collective-permute-start | bytes 589832 | tf_op jit(solution)/shard_map/ppermute | solution.py:19
  61.1 8.3 %collective-permute-start.5 = (bf16[2,256,192]{2,1,0:T(8,128)(2,1)S(1)}, bf16[2,256,192]{2,1,0:T(8,128)(2,1)S(1)}, u32[]{:S(2)}, u32[]{:S(2)}) collective-permute-start(bf16[2,256,192]{2,1,0:T(8,128)(2,1)S(1)} %collective-permute-done.4), channel_id=1, source_target_pairs={{0,30},{2,0},{4,2},{6,4},{8,6},{10,8},{12,10},{14,12},{16,14},{18,... | collective-permute-start | bytes 589832 | tf_op jit(solution)/shard_map/ppermute | solution.py:19
  66.2 8.3 %collective-permute-start.12 = (bf16[2,256,192]{2,1,0:T(8,128)(2,1)S(1)}, bf16[2,256,192]{2,1,0:T(8,128)(2,1)S(1)}, u32[]{:S(2)}, u32[]{:S(2)}) collective-permute-start(bf16[2,256,192]{2,1,0:T(8,128)(2,1)S(1)} %collective-permute-done.11), channel_id=1, source_target_pairs={{0,2},{2,4},{4,6},{6,8},{8,10},{10,12},{12,14},{14,16},{16,18},{18... | collective-permute-start | bytes 589832 | tf_op jit(solution)/shard_map/ppermute | solution.py:19
  69.5 16.6 %collective-permute-start.6 = (bf16[2,256,192]{2,1,0:T(8,128)(2,1)S(1)}, bf16[2,256,192]{2,1,0:T(8,128)(2,1)S(1)}, u32[]{:S(2)}, u32[]{:S(2)}) collective-permute-start(bf16[2,256,192]{2,1,0:T(8,128)(2,1)S(1)} %collective-permute-done.5), channel_id=1, source_target_pairs={{0,30},{2,0},{4,2},{6,4},{8,6},{10,8},{12,10},{14,12},{16,14},{18,... | collective-permute-start | bytes 589832 | tf_op jit(solution)/shard_map/ppermute | solution.py:19
  74.5 9.5 %collective-permute-start.13 = (bf16[2,256,192]{2,1,0:T(8,128)(2,1)S(1)}, bf16[2,256,192]{2,1,0:T(8,128)(2,1)S(1)}, u32[]{:S(2)}, u32[]{:S(2)}) collective-permute-start(bf16[2,256,192]{2,1,0:T(8,128)(2,1)S(1)} %collective-permute-done.12), channel_id=1, source_target_pairs={{0,2},{2,4},{4,6},{6,8},{8,10},{10,12},{12,14},{14,16},{16,18},{18... | collective-permute-start | bytes 589832 | tf_op jit(solution)/shard_map/ppermute | solution.py:19
  84.0 10.5 %collective-permute-start.14 = (bf16[2,256,192]{2,1,0:T(8,128)(2,1)S(1)}, bf16[2,256,192]{2,1,0:T(8,128)(2,1)S(1)}, u32[]{:S(2)}, u32[]{:S(2)}) collective-permute-start(bf16[2,256,192]{2,1,0:T(8,128)(2,1)S(1)} %collective-permute-done.13), channel_id=1, source_target_pairs={{0,2},{2,4},{4,6},{6,8},{8,10},{10,12},{12,14},{14,16},{16,18},{18... | collective-permute-start | bytes 589832 | tf_op jit(solution)/shard_map/ppermute | solution.py:19
  147.5 8.4 %collective-permute-start.15 = (bf16[528,192]{1,0:T(8,128)(2,1)S(1)}, bf16[528,192]{1,0:T(8,128)(2,1)S(1)}, u32[]{:S(2)}, u32[]{:S(2)}) collective-permute-start(bf16[528,192]{1,0:T(8,128)(2,1)S(1)} %get-tuple-element.76), channel_id=1, source_target_pairs={{0,2},{2,4},{4,6},{6,8},{8,10},{10,12},{12,14},{14,16},{16,18},{18... | collective-permute-start | bytes 608264 | tf_op jit(solution)/shard_map/ppermute | solution.py:19
  149.6 8.2 %collective-permute-start.17 = (bf16[528,192]{1,0:T(8,128)(2,1)S(1)}, bf16[528,192]{1,0:T(8,128)(2,1)S(1)}, u32[]{:S(2)}, u32[]{:S(2)}) collective-permute-start(bf16[528,192]{1,0:T(8,128)(2,1)S(1)} %get-tuple-element.75), channel_id=1, source_target_pairs={{0,30},{2,0},{4,2},{6,4},{8,6},{10,8},{12,10},{14,12},{16,14},{18,... | collective-permute-start | bytes 608264 | tf_op jit(solution)/shard_map/ppermute | solution.py:19
  157.9 10.9 %collective-permute-start.16 = (bf16[528,192]{1,0:T(8,128)(2,1)S(1)}, bf16[528,192]{1,0:T(8,128)(2,1)S(1)}, u32[]{:S(2)}, u32[]{:S(2)}) collective-permute-start(bf16[528,192]{1,0:T(8,128)(2,1)S(1)} %maximum_maximum_fusion.2), channel_id=1, source_target_pairs={{0,2},{2,4},{4,6},{6,8},{8,10},{10,12},{12,14},{14,16},{16,18},{18... | collective-permute-start | bytes 608264 | tf_op jit(solution)/shard_map/ppermute | solution.py:19
  160.0 11.1 %collective-permute-start.19 = (bf16[528,192]{1,0:T(8,128)(2,1)S(1)}, bf16[528,192]{1,0:T(8,128)(2,1)S(1)}, u32[]{:S(2)}, u32[]{:S(2)}) collective-permute-start(bf16[528,192]{1,0:T(8,128)(2,1)S(1)} %maximum_maximum_fusion.3), channel_id=1, source_target_pairs={{0,30},{2,0},{4,2},{6,4},{8,6},{10,8},{12,10},{14,12},{16,14},{18,... | collective-permute-start | bytes 608264 | tf_op jit(solution)/shard_map/ppermute | solution.py:19
  171.2 11.6 %collective-permute-start.18 = (bf16[528,192]{1,0:T(8,128)(2,1)S(1)}, bf16[528,192]{1,0:T(8,128)(2,1)S(1)}, u32[]{:S(2)}, u32[]{:S(2)}) collective-permute-start(bf16[528,192]{1,0:T(8,128)(2,1)S(1)} %maximum_maximum_fusion.4), channel_id=1, source_target_pairs={{0,2},{2,4},{4,6},{6,8},{8,10},{10,12},{12,14},{14,16},{16,18},{18... | collective-permute-start | bytes 608264 | tf_op jit(solution)/shard_map/ppermute | solution.py:19
  173.3 10.5 %collective-permute-start.21 = (bf16[528,192]{1,0:T(8,128)(2,1)S(1)}, bf16[528,192]{1,0:T(8,128)(2,1)S(1)}, u32[]{:S(2)}, u32[]{:S(2)}) collective-permute-start(bf16[528,192]{1,0:T(8,128)(2,1)S(1)} %maximum_maximum_fusion.5), channel_id=1, source_target_pairs={{0,30},{2,0},{4,2},{6,4},{8,6},{10,8},{12,10},{14,12},{16,14},{18,... | collective-permute-start | bytes 608264 | tf_op jit(solution)/shard_map/ppermute | solution.py:19
  183.9 10.9 %collective-permute-start.20 = (bf16[528,192]{1,0:T(8,128)(2,1)S(1)}, bf16[528,192]{1,0:T(8,128)(2,1)S(1)}, u32[]{:S(2)}, u32[]{:S(2)}) collective-permute-start(bf16[528,192]{1,0:T(8,128)(2,1)S(1)} %maximum_maximum_fusion.6), channel_id=1, source_target_pairs={{0,2},{2,4},{4,6},{6,8},{8,10},{10,12},{12,14},{14,16},{16,18},{18... | collective-permute-start | bytes 608264 | tf_op jit(solution)/shard_map/ppermute | solution.py:19
  186.0 9.8 %collective-permute-start.23 = (bf16[528,192]{1,0:T(8,128)(2,1)S(1)}, bf16[528,192]{1,0:T(8,128)(2,1)S(1)}, u32[]{:S(2)}, u32[]{:S(2)}) collective-permute-start(bf16[528,192]{1,0:T(8,128)(2,1)S(1)} %maximum_maximum_fusion.7), channel_id=1, source_target_pairs={{0,30},{2,0},{4,2},{6,4},{8,6},{10,8},{12,10},{14,12},{16,14},{18,... | collective-permute-start | bytes 608264 | tf_op jit(solution)/shard_map/ppermute | solution.py:19
  195.9 9.9 %collective-permute-start.22 = (bf16[528,192]{1,0:T(8,128)(2,1)S(1)}, bf16[528,192]{1,0:T(8,128)(2,1)S(1)}, u32[]{:S(2)}, u32[]{:S(2)}) collective-permute-start(bf16[528,192]{1,0:T(8,128)(2,1)S(1)} %maximum_maximum_fusion.8), channel_id=1, source_target_pairs={{0,2},{2,4},{4,6},{6,8},{8,10},{10,12},{12,14},{14,16},{16,18},{18... | collective-permute-start | bytes 608264 | tf_op jit(solution)/shard_map/ppermute | solution.py:19
  198.0 8.7 %collective-permute-start.25 = (bf16[528,192]{1,0:T(8,128)(2,1)S(1)}, bf16[528,192]{1,0:T(8,128)(2,1)S(1)}, u32[]{:S(2)}, u32[]{:S(2)}) collective-permute-start(bf16[528,192]{1,0:T(8,128)(2,1)S(1)} %maximum_maximum_fusion.9), channel_id=1, source_target_pairs={{0,30},{2,0},{4,2},{6,4},{8,6},{10,8},{12,10},{14,12},{16,14},{18,... | collective-permute-start | bytes 608264 | tf_op jit(solution)/shard_map/ppermute | solution.py:19
  206.8 9.4 %collective-permute-start.24 = (bf16[528,192]{1,0:T(8,128)(2,1)S(1)}, bf16[528,192]{1,0:T(8,128)(2,1)S(1)}, u32[]{:S(2)}, u32[]{:S(2)}) collective-permute-start(bf16[528,192]{1,0:T(8,128)(2,1)S(1)} %maximum_maximum_fusion.10), channel_id=1, source_target_pairs={{0,2},{2,4},{4,6},{6,8},{8,10},{10,12},{12,14},{14,16},{16,18},{18... | collective-permute-start | bytes 608264 | tf_op jit(solution)/shard_map/ppermute | solution.py:19
  208.9 8.9 %collective-permute-start.27 = (bf16[528,192]{1,0:T(8,128)(2,1)S(1)}, bf16[528,192]{1,0:T(8,128)(2,1)S(1)}, u32[]{:S(2)}, u32[]{:S(2)}) collective-permute-start(bf16[528,192]{1,0:T(8,128)(2,1)S(1)} %maximum_maximum_fusion.11), channel_id=1, source_target_pairs={{0,30},{2,0},{4,2},{6,4},{8,6},{10,8},{12,10},{14,12},{16,14},{18,... | collective-permute-start | bytes 608264 | tf_op jit(solution)/shard_map/ppermute | solution.py:19
  217.9 9.0 %collective-permute-start.26 = (bf16[528,192]{1,0:T(8,128)(2,1)S(1)}, bf16[528,192]{1,0:T(8,128)(2,1)S(1)}, u32[]{:S(2)}, u32[]{:S(2)}) collective-permute-start(bf16[528,192]{1,0:T(8,128)(2,1)S(1)} %maximum_maximum_fusion.12), channel_id=1, source_target_pairs={{0,2},{2,4},{4,6},{6,8},{8,10},{10,12},{12,14},{14,16},{16,18},{18... | collective-permute-start | bytes 608264 | tf_op jit(solution)/shard_map/ppermute | solution.py:19
  220.1 9.2 %collective-permute-start.29 = (bf16[528,192]{1,0:T(8,128)(2,1)S(1)}, bf16[528,192]{1,0:T(8,128)(2,1)S(1)}, u32[]{:S(2)}, u32[]{:S(2)}) collective-permute-start(bf16[528,192]{1,0:T(8,128)(2,1)S(1)} %maximum_maximum_fusion.13), channel_id=1, source_target_pairs={{0,30},{2,0},{4,2},{6,4},{8,6},{10,8},{12,10},{14,12},{16,14},{18,... | collective-permute-start | bytes 608264 | tf_op jit(solution)/shard_map/ppermute | solution.py:19
  227.2 8.4 %collective-permute-start.28 = (bf16[528,192]{1,0:T(8,128)(2,1)S(1)}, bf16[528,192]{1,0:T(8,128)(2,1)S(1)}, u32[]{:S(2)}, u32[]{:S(2)}) collective-permute-start(bf16[528,192]{1,0:T(8,128)(2,1)S(1)} %maximum_maximum_fusion.14), channel_id=1, source_target_pairs={{0,2},{2,4},{4,6},{6,8},{8,10},{10,12},{12,14},{14,16},{16,18},{18... | collective-permute-start | bytes 608264 | tf_op jit(solution)/shard_map/ppermute | solution.py:19
  236.8 26.6 %collective-permute-start.30 = (bf16[2,256,192]{2,1,0:T(8,128)(2,1)S(1)}, bf16[2,256,192]{2,1,0:T(8,128)(2,1)S(1)}, u32[]{:S(2)}, u32[]{:S(2)}) collective-permute-start(bf16[2,256,192]{2,1,0:T(8,128)(2,1)S(1)} %pad_maximum_fusion.1), channel_id=1, source_target_pairs={{32,0},{64,32},{96,64},{128,96},{160,128},{192,160},{224,192},{256... | collective-permute-start | bytes 589832 | tf_op jit(solution)/shard_map/ppermute | solution.py:14
  256.7 6.1 %collective-permute-start.31 = (f32[192]{0:T(256)S(1)}, f32[192]{0:T(256)S(1)}, u32[]{:S(2)}, u32[]{:S(2)}) collective-permute-start(f32[192]{0:T(256)S(1)} %bitcast.347), channel_id=1, source_target_pairs={{0,1},{1,0},{2,3},{3,2},{4,5},{5,4},{6,7},{7,6},{8,9},{9,8},{10,11... | collective-permute-start | bytes 2312 | tf_op jit(solution)/shard_map/ppermute | solution.py:19
  (16 other events, 258.1 us)

commit v7 on v4

--- a/solution.py
+++ b/solution.py
@@ -201,13 +201,14 @@
     grad_parts = ((weighted - unit_rows * row_stat) * inverse).astype(jnp.bfloat16)
     grad_parts = jnp.transpose(grad_parts.reshape(length, n_mp, share), (1, 0, 2))
     gain_parts = jnp.sum(normed_grad * unit_rows, axis=0).reshape(n_mp, share)
+    gain_parts = gain_parts + shift(gain_parts, "dp", 1)
     shares, gain_share = ring_reduce_scatter(
         jnp.concatenate([out_parts, grad_parts], axis=1), gain_parts, "mp"
     )
     out_share, grad_share = shares[:length], shares[length:]
     rebuilt = (lower_out[0, 0].astype(jnp.float32) - out_share).astype(jnp.bfloat16)
     lower_rows = upper_grad[0, 0].astype(jnp.float32) + grad_share
-    gain_grad = gain_share + shift(gain_share, "dp", 1)
+    gain_grad = gain_share
     entering = lower_rows.astype(jnp.bfloat16)
     sent = from_behind(jnp.stack([rebuilt, entering]), "section", -1)
     return (sent[0][None, None], sent[1][None, None], gain_grad[None])

time: 239 us -> 243 us (1.017)
    ppermute x1, waiting for transfers between devices: 0.01 us -> 3.67 us  [from_behind(): return lax.ppermute(x, axis, pairs)]
  transfers between devices with their start and end apart: 32 -> 32, of which waited for: 16 -> 16; matrix products, arithmetic and copies ran while one was open for 4% -> 11% of each run, Pallas kernels for 0% -> 0%
where the time goes in v7:
time: 243 us; the launch traced here: 240 us
  starting transfers between devices  136 us (56%)
  waiting for transfers between devices  43.6 us (18%)
  other arithmetic  22.1 us (9%)
  matrix products  20.6 us (8%)
  local copies, waits for them, and re-layouts  15.7 us (6%)
    ppermute x31, starting transfers between devices, shift(): lax.ppermute(x, axis, [(i, (i + by) % length) for i in range(length)])  116 us
    ppermute x31, waiting for transfers between devices, shift(): lax.ppermute(x, axis, [(i, (i + by) % length) for i in range(length)])  39.9 us
    ppermute x1, starting transfers between devices, from_behind(): return lax.ppermute(x, axis, pairs)  20 us
    dot_general x1, matrix products, local(): jnp.dot(value_gradient, w_value.T, preferred_element_type=jnp.float32)  6.15 us
    convert_element_type x1, other arithmetic, local(): ((weighted - unit_rows * row_stat) * inverse).astype(jnp.bfloat16)  4.93 us
  transfers between devices with their start and end apart: 32, of which 16 were waited for; matrix products, arithmetic and copies ran while one was open for 11% of the time, Pallas kernels for 0%

profile of v7, /device:TPU:1, one launch (start us, length us, event | category | flops | bytes accessed | tf_op | source)
XLA Modules:
  0.0 240.5 jit_solution(11442647483854663582)
XLA Ops:
  1.8 18.8 %collective-permute-start = (bf16[2,256,192]{1,2,0:T(8,128)(2,1)S(1)}, bf16[2,256,192]{1,2,0:T(8,128)(2,1)S(1)}, u32[]{:S(2)}, u32[]{:S(2)}) collective-permute-start(bf16[2,256,192]{1,2,0:T(8,128)(2,1)S(1)} %pad_maximum_fusion.1), channel_id=1, source_target_pairs={{0,30},{2,0},{4,2},{6,4},{8,6},{10,8},{12,10},{14,12},{16,14},{18,... | collective-permute-start | bytes 589832 | tf_op jit(solution)/shard_map/ppermute | solution.py:19
  26.6 4.6 %collective-permute-start.1 = (bf16[2,256,192]{1,2,0:T(8,128)(2,1)S(1)}, bf16[2,256,192]{1,2,0:T(8,128)(2,1)S(1)}, u32[]{:S(2)}, u32[]{:S(2)}) collective-permute-start(bf16[2,256,192]{1,2,0:T(8,128)(2,1)S(1)} %collective-permute-done), channel_id=1, source_target_pairs={{0,30},{2,0},{4,2},{6,4},{8,6},{10,8},{12,10},{14,12},{16,14},{18,... | collective-permute-start | bytes 589832 | tf_op jit(solution)/shard_map/ppermute | solution.py:19
  34.1 5.3 %collective-permute-start.2 = (bf16[2,256,192]{1,2,0:T(8,128)(2,1)S(1)}, bf16[2,256,192]{1,2,0:T(8,128)(2,1)S(1)}, u32[]{:S(2)}, u32[]{:S(2)}) collective-permute-start(bf16[2,256,192]{1,2,0:T(8,128)(2,1)S(1)} %collective-permute-done.1), channel_id=1, source_target_pairs={{0,30},{2,0},{4,2},{6,4},{8,6},{10,8},{12,10},{14,12},{16,14},{18,... | collective-permute-start | bytes 589832 | tf_op jit(solution)/shard_map/ppermute | solution.py:19
  42.0 5.0 %collective-permute-start.3 = (bf16[2,256,192]{1,2,0:T(8,128)(2,1)S(1)}, bf16[2,256,192]{1,2,0:T(8,128)(2,1)S(1)}, u32[]{:S(2)}, u32[]{:S(2)}) collective-permute-start(bf16[2,256,192]{1,2,0:T(8,128)(2,1)S(1)} %collective-permute-done.2), channel_id=1, source_target_pairs={{0,30},{2,0},{4,2},{6,4},{8,6},{10,8},{12,10},{14,12},{16,14},{18,... | collective-permute-start | bytes 589832 | tf_op jit(solution)/shard_map/ppermute | solution.py:19
  49.6 5.0 %collective-permute-start.4 = (bf16[2,256,192]{1,2,0:T(8,128)(2,1)S(1)}, bf16[2,256,192]{1,2,0:T(8,128)(2,1)S(1)}, u32[]{:S(2)}, u32[]{:S(2)}) collective-permute-start(bf16[2,256,192]{1,2,0:T(8,128)(2,1)S(1)} %collective-permute-done.3), channel_id=1, source_target_pairs={{0,30},{2,0},{4,2},{6,4},{8,6},{10,8},{12,10},{14,12},{16,14},{18,... | collective-permute-start | bytes 589832 | tf_op jit(solution)/shard_map/ppermute | solution.py:19
  57.2 5.0 %collective-permute-start.5 = (bf16[2,256,192]{1,2,0:T(8,128)(2,1)S(1)}, bf16[2,256,192]{1,2,0:T(8,128)(2,1)S(1)}, u32[]{:S(2)}, u32[]{:S(2)}) collective-permute-start(bf16[2,256,192]{1,2,0:T(8,128)(2,1)S(1)} %collective-permute-done.4), channel_id=1, source_target_pairs={{0,30},{2,0},{4,2},{6,4},{8,6},{10,8},{12,10},{14,12},{16,14},{18,... | collective-permute-start | bytes 589832 | tf_op jit(solution)/shard_map/ppermute | solution.py:19
  64.8 5.0 %collective-permute-start.6 = (bf16[2,256,192]{1,2,0:T(8,128)(2,1)S(1)}, bf16[2,256,192]{1,2,0:T(8,128)(2,1)S(1)}, u32[]{:S(2)}, u32[]{:S(2)}) collective-permute-start(bf16[2,256,192]{1,2,0:T(8,128)(2,1)S(1)} %collective-permute-done.5), channel_id=1, source_target_pairs={{0,30},{2,0},{4,2},{6,4},{8,6},{10,8},{12,10},{14,12},{16,14},{18,... | collective-permute-start | bytes 589832 | tf_op jit(solution)/shard_map/ppermute | solution.py:19
  71.8 6.5 %collective-permute-done.13 = bf16[2,256,192]{1,2,0:T(8,128)(2,1)S(1)} collective-permute-done((bf16[2,256,192]{1,2,0:T(8,128)(2,1)S(1)}, bf16[2,256,192]{1,2,0:T(8,128)(2,1)S(1)}, u32[]{:S(2)}, u32[]{:S(2)}) %collective-permute-start.13) | collective-permute-done | bytes 196640 | tf_op jit(solution)/shard_map/ppermute | solution.py:19
  80.3 7.8 %collective-permute-done.14 = bf16[2,256,192]{1,2,0:T(8,128)(2,1)S(1)} collective-permute-done((bf16[2,256,192]{1,2,0:T(8,128)(2,1)S(1)}, bf16[2,256,192]{1,2,0:T(8,128)(2,1)S(1)}, u32[]{:S(2)}, u32[]{:S(2)}) %collective-permute-start.14) | collective-permute-done | bytes 196640 | tf_op jit(solution)/shard_map/ppermute | solution.py:19
  89.1 3.0 %fusion = (f32[16,256,192]{1,2,0:T(8,128)}, bf16[16,1,256,192]{2,3,0,1:T(8,128)(2,1)}) fusion(bf16[32,2,256,192]{2,3,0,1:T(8,128)(2,1)S(1)} %bitcast_dynamic-update-slice_fusion.31, s32[]{:T(128)S(6)} %select_n.194, s32[]{:T(128)S(6)} %add.519), kind=kLoop, calls=%fused_computation.41 | loop fusion | flops 786432 | bytes 7864328 | tf_op jit(solution)/shard_map/convert_element_type | solution.py:124
  92.7 3.6 %copy.209 = f32[256,3072]{1,0:T(8,128)} copy(f32[256,3072]{0,1:T(8,128)} %bitcast.337) | data formatting | bytes 6291456 | tf_op jit(solution)/shard_map/convert_element_type | solution.py:124
  96.3 2.0 multiply_convert_fusion.1
  102.4 2.3 fusion.5
  104.7 4.4 %convolution_add_fusion.1 = f32[256,3072]{1,0:T(8,128)} fusion(f32[256,3072]{1,0:T(8,128)} %fusion.5, bf16[256,2,128]{0,2,1:T(8,128)(2,1)S(1)} %bitcast.347, bf16[2,256,256]{1,2,0:T(8,128)(2,1)S(1)} %fusion.61, bf16[1,3072,128]{2,1,0:T(8,128)(2,1)S(1)} %copy-done.5), kind=kOutput, calls=%fused_computation.33 | convolution fusion | flops 235700224 | bytes 7471104 | tf_op jit(solution)/shard_map/dot_general | solution.py:195
  109.2 6.2 %multiply_reduce_fusion.1 = (f32[256]{0:T(256)S(1)}, f32[3072]{0:T(1024)S(1)}, f32[256,3072]{1,0:T(8,128)}) fusion(f32[256,3072]{1,0:T(8,128)} %copy.209, f32[256]{0:T(256)S(1)} %add_rsqrt_fusion, f32[3072]{0:T(1024)S(1)} %bitcast.352, f32[256,3072]{1,0:T(8,128)} %convolution_add_fusion.1, bf16[1,3072,128]{2,1,0:T(8,128)(2,1)} %param.17, ...), kind=kOutput, calls=%fused_computation.36 | convolution fusion | flops 240939776 | bytes 10975232 | tf_op jit(solution)/shard_map/dot_general | solution.py:196
  115.4 4.8 %collective-permute-start.15 = (f32[16,192]{1,0:T(8,128)S(1)}, f32[16,192]{1,0:T(8,128)S(1)}, u32[]{:S(2)}, u32[]{:S(2)}) collective-permute-start(f32[16,192]{1,0:T(8,128)S(1)} %reshape.194), channel_id=1, source_target_pairs={{0,1},{1,0},{2,3},{3,2},{4,5},{5,4},{6,7},{7,6},{8,9},{9,8},{10,11... | collective-permute-start | bytes 36872 | tf_op jit(solution)/shard_map/ppermute | solution.py:19
  120.2 4.9 %multiply_convert_fusion = bf16[256,3072]{1,0:T(8,128)(2,1)} fusion(f32[256,3072]{1,0:T(8,128)} %get-tuple-element.92, f32[256,3072]{1,0:T(8,128)} %copy.209, f32[256]{0:T(256)S(1)} %broadcast_multiply_fusion, f32[256]{0:T(256)S(1)} %add_rsqrt_fusion, f32[3072]{0:T(1024)S(1)} %bitcast.353), kind=kLoop, calls=%fused_computation.35 | loop fusion | flops 4718592 | bytes 7878656 | tf_op jit(solution)/shard_map/convert_element_type | solution.py:201
  126.8 2.5 %copy.211 = bf16[256,16,192]{2,0,1:T(8,128)(2,1)} copy(bf16[256,16,192]{0,2,1:T(8,128)(2,1)S(1)} %bitcast.338) | data formatting | bytes 3145728 | tf_op jit(solution)/shard_map/reshape | solution.py:202
  129.4 3.7 %fusion.3 = f32[256,3072]{0,1} fusion(bf16[256,256]{0,1:T(8,128)(2,1)S(1)} %bitcast.349, bf16[1,256,3072]{2,1,0:T(8,128)(2,1)} %param.18), kind=kOutput, calls=%fused_computation.44 | convolution fusion | flops 402653184 | bytes 4849664
  133.1 4.3 %copy.203 = bf16[256,16,192]{2,0,1:T(8,128)(2,1)} copy(f32[256,16,192]{0,2,1:T(8,128)} %bitcast.333) | data formatting | bytes 4718592 | tf_op jit(solution)/shard_map/lc,cmf->mlf/dot_general | solution.py:163
  141.0 4.8 %collective-permute-start.18 = (bf16[528,192]{1,0:T(8,128)(2,1)S(1)}, bf16[528,192]{1,0:T(8,128)(2,1)S(1)}, u32[]{:S(2)}, u32[]{:S(2)}) collective-permute-start(bf16[528,192]{1,0:T(8,128)(2,1)S(1)} %get-tuple-element.86), channel_id=1, source_target_pairs={{0,30},{2,0},{4,2},{6,4},{8,6},{10,8},{12,10},{14,12},{16,14},{18,... | collective-permute-start | bytes 608264 | tf_op jit(solution)/shard_map/ppermute | solution.py:19
  150.7 4.6 %collective-permute-start.20 = (bf16[528,192]{1,0:T(8,128)(2,1)S(1)}, bf16[528,192]{1,0:T(8,128)(2,1)S(1)}, u32[]{:S(2)}, u32[]{:S(2)}) collective-permute-start(bf16[528,192]{1,0:T(8,128)(2,1)S(1)} %maximum_maximum_fusion.3), channel_id=1, source_target_pairs={{0,30},{2,0},{4,2},{6,4},{8,6},{10,8},{12,10},{14,12},{16,14},{18,... | collective-permute-start | bytes 608264 | tf_op jit(solution)/shard_map/ppermute | solution.py:19
  155.3 4.5 %collective-permute-done.17 = bf16[528,192]{1,0:T(8,128)(2,1)S(1)} collective-permute-done((bf16[528,192]{1,0:T(8,128)(2,1)S(1)}, bf16[528,192]{1,0:T(8,128)(2,1)S(1)}, u32[]{:S(2)}, u32[]{:S(2)}) %collective-permute-start.17) | collective-permute-done | bytes 202784 | tf_op jit(solution)/shard_map/ppermute | solution.py:19
  162.3 4.6 %collective-permute-start.22 = (bf16[528,192]{1,0:T(8,128)(2,1)S(1)}, bf16[528,192]{1,0:T(8,128)(2,1)S(1)}, u32[]{:S(2)}, u32[]{:S(2)}) collective-permute-start(bf16[528,192]{1,0:T(8,128)(2,1)S(1)} %maximum_maximum_fusion.5), channel_id=1, source_target_pairs={{0,30},{2,0},{4,2},{6,4},{8,6},{10,8},{12,10},{14,12},{16,14},{18,... | collective-permute-start | bytes 608264 | tf_op jit(solution)/shard_map/ppermute | solution.py:19
  166.9 2.7 %collective-permute-done.19 = bf16[528,192]{1,0:T(8,128)(2,1)S(1)} collective-permute-done((bf16[528,192]{1,0:T(8,128)(2,1)S(1)}, bf16[528,192]{1,0:T(8,128)(2,1)S(1)}, u32[]{:S(2)}, u32[]{:S(2)}) %collective-permute-start.19) | collective-permute-done | bytes 202784 | tf_op jit(solution)/shard_map/ppermute | solution.py:19
  172.0 4.6 %collective-permute-start.24 = (bf16[528,192]{1,0:T(8,128)(2,1)S(1)}, bf16[528,192]{1,0:T(8,128)(2,1)S(1)}, u32[]{:S(2)}, u32[]{:S(2)}) collective-permute-start(bf16[528,192]{1,0:T(8,128)(2,1)S(1)} %maximum_maximum_fusion.7), channel_id=1, source_target_pairs={{0,30},{2,0},{4,2},{6,4},{8,6},{10,8},{12,10},{14,12},{16,14},{18,... | collective-permute-start | bytes 608264 | tf_op jit(solution)/shard_map/ppermute | solution.py:19
  180.7 4.6 %collective-permute-start.26 = (bf16[528,192]{1,0:T(8,128)(2,1)S(1)}, bf16[528,192]{1,0:T(8,128)(2,1)S(1)}, u32[]{:S(2)}, u32[]{:S(2)}) collective-permute-start(bf16[528,192]{1,0:T(8,128)(2,1)S(1)} %maximum_maximum_fusion.9), channel_id=1, source_target_pairs={{0,30},{2,0},{4,2},{6,4},{8,6},{10,8},{12,10},{14,12},{16,14},{18,... | collective-permute-start | bytes 608264 | tf_op jit(solution)/shard_map/ppermute | solution.py:19
  189.3 4.6 %collective-permute-start.28 = (bf16[528,192]{1,0:T(8,128)(2,1)S(1)}, bf16[528,192]{1,0:T(8,128)(2,1)S(1)}, u32[]{:S(2)}, u32[]{:S(2)}) collective-permute-start(bf16[528,192]{1,0:T(8,128)(2,1)S(1)} %maximum_maximum_fusion.11), channel_id=1, source_target_pairs={{0,30},{2,0},{4,2},{6,4},{8,6},{10,8},{12,10},{14,12},{16,14},{18,... | collective-permute-start | bytes 608264 | tf_op jit(solution)/shard_map/ppermute | solution.py:19
  198.0 4.6 %collective-permute-start.30 = (bf16[528,192]{1,0:T(8,128)(2,1)S(1)}, bf16[528,192]{1,0:T(8,128)(2,1)S(1)}, u32[]{:S(2)}, u32[]{:S(2)}) collective-permute-start(bf16[528,192]{1,0:T(8,128)(2,1)S(1)} %maximum_maximum_fusion.13), channel_id=1, source_target_pairs={{0,30},{2,0},{4,2},{6,4},{8,6},{10,8},{12,10},{14,12},{16,14},{18,... | collective-permute-start | bytes 608264 | tf_op jit(solution)/shard_map/ppermute | solution.py:19
  206.6 6.9 %collective-permute-done.29 = bf16[528,192]{1,0:T(8,128)(2,1)S(1)} collective-permute-done((bf16[528,192]{1,0:T(8,128)(2,1)S(1)}, bf16[528,192]{1,0:T(8,128)(2,1)S(1)}, u32[]{:S(2)}, u32[]{:S(2)}) %collective-permute-start.29) | collective-permute-done | bytes 202784 | tf_op jit(solution)/shard_map/ppermute | solution.py:19
  214.8 20.0 %collective-permute-start.31 = (bf16[2,256,192]{2,1,0:T(8,128)(2,1)S(1)}, bf16[2,256,192]{2,1,0:T(8,128)(2,1)S(1)}, u32[]{:S(2)}, u32[]{:S(2)}) collective-permute-start(bf16[2,256,192]{2,1,0:T(8,128)(2,1)S(1)} %pad_maximum_fusion), channel_id=1, source_target_pairs={{32,0},{64,32},{96,64},{128,96},{160,128},{192,160},{224,192},{256... | collective-permute-start | bytes 589832 | tf_op jit(solution)/shard_map/ppermute | solution.py:14
  235.3 3.7 %collective-permute-done.31 = bf16[2,256,192]{2,1,0:T(8,128)(2,1)S(1)} collective-permute-done((bf16[2,256,192]{2,1,0:T(8,128)(2,1)S(1)}, bf16[2,256,192]{2,1,0:T(8,128)(2,1)S(1)}, u32[]{:S(2)}, u32[]{:S(2)}) %collective-permute-start.31) | collective-permute-done | bytes 196640 | tf_op jit(solution)/shard_map/ppermute | solution.py:14
  (191 shorter events, 63.6 us)
Async XLA Ops:
  1.8 24.8 %collective-permute-start = (bf16[2,256,192]{1,2,0:T(8,128)(2,1)S(1)}, bf16[2,256,192]{1,2,0:T(8,128)(2,1)S(1)}, u32[]{:S(2)}, u32[]{:S(2)}) collective-permute-start(bf16[2,256,192]{1,2,0:T(8,128)(2,1)S(1)} %pad_maximum_fusion.1), channel_id=1, source_target_pairs={{0,30},{2,0},{4,2},{6,4},{8,6},{10,8},{12,10},{14,12},{16,14},{18,... | collective-permute-start | bytes 589832 | tf_op jit(solution)/shard_map/ppermute | solution.py:19
  20.5 10.6 %collective-permute-start.7 = (bf16[2,256,192]{1,2,0:T(8,128)(2,1)S(1)}, bf16[2,256,192]{1,2,0:T(8,128)(2,1)S(1)}, u32[]{:S(2)}, u32[]{:S(2)}) collective-permute-start(bf16[2,256,192]{1,2,0:T(8,128)(2,1)S(1)} %pad_maximum_fusion.1), channel_id=1, source_target_pairs={{0,2},{2,4},{4,6},{6,8},{8,10},{10,12},{12,14},{14,16},{16,18},{18... | collective-permute-start | bytes 589832 | tf_op jit(solution)/shard_map/ppermute | solution.py:19
  26.6 7.5 %collective-permute-start.1 = (bf16[2,256,192]{1,2,0:T(8,128)(2,1)S(1)}, bf16[2,256,192]{1,2,0:T(8,128)(2,1)S(1)}, u32[]{:S(2)}, u32[]{:S(2)}) collective-permute-start(bf16[2,256,192]{1,2,0:T(8,128)(2,1)S(1)} %collective-permute-done), channel_id=1, source_target_pairs={{0,30},{2,0},{4,2},{6,4},{8,6},{10,8},{12,10},{14,12},{16,14},{18,... | collective-permute-start | bytes 589832 | tf_op jit(solution)/shard_map/ppermute | solution.py:19
  31.2 8.2 %collective-permute-start.8 = (bf16[2,256,192]{1,2,0:T(8,128)(2,1)S(1)}, bf16[2,256,192]{1,2,0:T(8,128)(2,1)S(1)}, u32[]{:S(2)}, u32[]{:S(2)}) collective-permute-start(bf16[2,256,192]{1,2,0:T(8,128)(2,1)S(1)} %collective-permute-done.7), channel_id=1, source_target_pairs={{0,2},{2,4},{4,6},{6,8},{8,10},{10,12},{12,14},{14,16},{16,18},{18... | collective-permute-start | bytes 589832 | tf_op jit(solution)/shard_map/ppermute | solution.py:19
  34.1 7.9 %collective-permute-start.2 = (bf16[2,256,192]{1,2,0:T(8,128)(2,1)S(1)}, bf16[2,256,192]{1,2,0:T(8,128)(2,1)S(1)}, u32[]{:S(2)}, u32[]{:S(2)}) collective-permute-start(bf16[2,256,192]{1,2,0:T(8,128)(2,1)S(1)} %collective-permute-done.1), channel_id=1, source_target_pairs={{0,30},{2,0},{4,2},{6,4},{8,6},{10,8},{12,10},{14,12},{16,14},{18,... | collective-permute-start | bytes 589832 | tf_op jit(solution)/shard_map/ppermute | solution.py:19
  39.4 7.6 %collective-permute-start.9 = (bf16[2,256,192]{1,2,0:T(8,128)(2,1)S(1)}, bf16[2,256,192]{1,2,0:T(8,128)(2,1)S(1)}, u32[]{:S(2)}, u32[]{:S(2)}) collective-permute-start(bf16[2,256,192]{1,2,0:T(8,128)(2,1)S(1)} %collective-permute-done.8), channel_id=1, source_target_pairs={{0,2},{2,4},{4,6},{6,8},{8,10},{10,12},{12,14},{14,16},{16,18},{18... | collective-permute-start | bytes 589832 | tf_op jit(solution)/shard_map/ppermute | solution.py:19
  42.0 7.6 %collective-permute-start.3 = (bf16[2,256,192]{1,2,0:T(8,128)(2,1)S(1)}, bf16[2,256,192]{1,2,0:T(8,128)(2,1)S(1)}, u32[]{:S(2)}, u32[]{:S(2)}) collective-permute-start(bf16[2,256,192]{1,2,0:T(8,128)(2,1)S(1)} %collective-permute-done.2), channel_id=1, source_target_pairs={{0,30},{2,0},{4,2},{6,4},{8,6},{10,8},{12,10},{14,12},{16,14},{18,... | collective-permute-start | bytes 589832 | tf_op jit(solution)/shard_map/ppermute | solution.py:19
  47.0 7.6 %collective-permute-start.10 = (bf16[2,256,192]{1,2,0:T(8,128)(2,1)S(1)}, bf16[2,256,192]{1,2,0:T(8,128)(2,1)S(1)}, u32[]{:S(2)}, u32[]{:S(2)}) collective-permute-start(bf16[2,256,192]{1,2,0:T(8,128)(2,1)S(1)} %collective-permute-done.9), channel_id=1, source_target_pairs={{0,2},{2,4},{4,6},{6,8},{8,10},{10,12},{12,14},{14,16},{16,18},{18... | collective-permute-start | bytes 589832 | tf_op jit(solution)/shard_map/ppermute | solution.py:19
  49.6 7.6 %collective-permute-start.4 = (bf16[2,256,192]{1,2,0:T(8,128)(2,1)S(1)}, bf16[2,256,192]{1,2,0:T(8,128)(2,1)S(1)}, u32[]{:S(2)}, u32[]{:S(2)}) collective-permute-start(bf16[2,256,192]{1,2,0:T(8,128)(2,1)S(1)} %collective-permute-done.3), channel_id=1, source_target_pairs={{0,30},{2,0},{4,2},{6,4},{8,6},{10,8},{12,10},{14,12},{16,14},{18,... | collective-permute-start | bytes 589832 | tf_op jit(solution)/shard_map/ppermute | solution.py:19
  54.7 7.6 %collective-permute-start.11 = (bf16[2,256,192]{1,2,0:T(8,128)(2,1)S(1)}, bf16[2,256,192]{1,2,0:T(8,128)(2,1)S(1)}, u32[]{:S(2)}, u32[]{:S(2)}) collective-permute-start(bf16[2,256,192]{1,2,0:T(8,128)(2,1)S(1)} %collective-permute-done.10), channel_id=1, source_target_pairs={{0,2},{2,4},{4,6},{6,8},{8,10},{10,12},{12,14},{14,16},{16,18},{18... | collective-permute-start | bytes 589832 | tf_op jit(solution)/shard_map/ppermute | solution.py:19
  57.2 7.6 %collective-permute-start.5 = (bf16[2,256,192]{1,2,0:T(8,128)(2,1)S(1)}, bf16[2,256,192]{1,2,0:T(8,128)(2,1)S(1)}, u32[]{:S(2)}, u32[]{:S(2)}) collective-permute-start(bf16[2,256,192]{1,2,0:T(8,128)(2,1)S(1)} %collective-permute-done.4), channel_id=1, source_target_pairs={{0,30},{2,0},{4,2},{6,4},{8,6},{10,8},{12,10},{14,12},{16,14},{18,... | collective-permute-start | bytes 589832 | tf_op jit(solution)/shard_map/ppermute | solution.py:19
  62.3 7.6 %collective-permute-start.12 = (bf16[2,256,192]{1,2,0:T(8,128)(2,1)S(1)}, bf16[2,256,192]{1,2,0:T(8,128)(2,1)S(1)}, u32[]{:S(2)}, u32[]{:S(2)}) collective-permute-start(bf16[2,256,192]{1,2,0:T(8,128)(2,1)S(1)} %collective-permute-done.11), channel_id=1, source_target_pairs={{0,2},{2,4},{4,6},{6,8},{8,10},{10,12},{12,14},{14,16},{16,18},{18... | collective-permute-start | bytes 589832 | tf_op jit(solution)/shard_map/ppermute | solution.py:19
  64.8 15.4 %collective-permute-start.6 = (bf16[2,256,192]{1,2,0:T(8,128)(2,1)S(1)}, bf16[2,256,192]{1,2,0:T(8,128)(2,1)S(1)}, u32[]{:S(2)}, u32[]{:S(2)}) collective-permute-start(bf16[2,256,192]{1,2,0:T(8,128)(2,1)S(1)} %collective-permute-done.5), channel_id=1, source_target_pairs={{0,30},{2,0},{4,2},{6,4},{8,6},{10,8},{12,10},{14,12},{16,14},{18,... | collective-permute-start | bytes 589832 | tf_op jit(solution)/shard_map/ppermute | solution.py:19
  69.9 8.5 %collective-permute-start.13 = (bf16[2,256,192]{1,2,0:T(8,128)(2,1)S(1)}, bf16[2,256,192]{1,2,0:T(8,128)(2,1)S(1)}, u32[]{:S(2)}, u32[]{:S(2)}) collective-permute-start(bf16[2,256,192]{1,2,0:T(8,128)(2,1)S(1)} %collective-permute-done.12), channel_id=1, source_target_pairs={{0,2},{2,4},{4,6},{6,8},{8,10},{10,12},{12,14},{14,16},{16,18},{18... | collective-permute-start | bytes 589832 | tf_op jit(solution)/shard_map/ppermute | solution.py:19
  78.3 9.7 %collective-permute-start.14 = (bf16[2,256,192]{1,2,0:T(8,128)(2,1)S(1)}, bf16[2,256,192]{1,2,0:T(8,128)(2,1)S(1)}, u32[]{:S(2)}, u32[]{:S(2)}) collective-permute-start(bf16[2,256,192]{1,2,0:T(8,128)(2,1)S(1)} %collective-permute-done.13), channel_id=1, source_target_pairs={{0,2},{2,4},{4,6},{6,8},{8,10},{10,12},{12,14},{14,16},{16,18},{18... | collective-permute-start | bytes 589832 | tf_op jit(solution)/shard_map/ppermute | solution.py:19
  115.4 23.2 %collective-permute-start.15 = (f32[16,192]{1,0:T(8,128)S(1)}, f32[16,192]{1,0:T(8,128)S(1)}, u32[]{:S(2)}, u32[]{:S(2)}) collective-permute-start(f32[16,192]{1,0:T(8,128)S(1)} %reshape.194), channel_id=1, source_target_pairs={{0,1},{1,0},{2,3},{3,2},{4,5},{5,4},{6,7},{7,6},{8,9},{9,8},{10,11... | collective-permute-start | bytes 36872 | tf_op jit(solution)/shard_map/ppermute | solution.py:19
  138.9 8.4 %collective-permute-start.16 = (bf16[528,192]{1,0:T(8,128)(2,1)S(1)}, bf16[528,192]{1,0:T(8,128)(2,1)S(1)}, u32[]{:S(2)}, u32[]{:S(2)}) collective-permute-start(bf16[528,192]{1,0:T(8,128)(2,1)S(1)} %get-tuple-element.87), channel_id=1, source_target_pairs={{0,2},{2,4},{4,6},{6,8},{8,10},{10,12},{12,14},{14,16},{16,18},{18... | collective-permute-start | bytes 608264 | tf_op jit(solution)/shard_map/ppermute | solution.py:19
  141.0 9.4 %collective-permute-start.18 = (bf16[528,192]{1,0:T(8,128)(2,1)S(1)}, bf16[528,192]{1,0:T(8,128)(2,1)S(1)}, u32[]{:S(2)}, u32[]{:S(2)}) collective-permute-start(bf16[528,192]{1,0:T(8,128)(2,1)S(1)} %get-tuple-element.86), channel_id=1, source_target_pairs={{0,30},{2,0},{4,2},{6,4},{8,6},{10,8},{12,10},{14,12},{16,14},{18,... | collective-permute-start | bytes 608264 | tf_op jit(solution)/shard_map/ppermute | solution.py:19
  148.5 11.3 %collective-permute-start.17 = (bf16[528,192]{1,0:T(8,128)(2,1)S(1)}, bf16[528,192]{1,0:T(8,128)(2,1)S(1)}, u32[]{:S(2)}, u32[]{:S(2)}) collective-permute-start(bf16[528,192]{1,0:T(8,128)(2,1)S(1)} %maximum_maximum_fusion.2), channel_id=1, source_target_pairs={{0,2},{2,4},{4,6},{6,8},{8,10},{10,12},{12,14},{14,16},{16,18},{18... | collective-permute-start | bytes 608264 | tf_op jit(solution)/shard_map/ppermute | solution.py:19
  150.7 11.3 %collective-permute-start.20 = (bf16[528,192]{1,0:T(8,128)(2,1)S(1)}, bf16[528,192]{1,0:T(8,128)(2,1)S(1)}, u32[]{:S(2)}, u32[]{:S(2)}) collective-permute-start(bf16[528,192]{1,0:T(8,128)(2,1)S(1)} %maximum_maximum_fusion.3), channel_id=1, source_target_pairs={{0,30},{2,0},{4,2},{6,4},{8,6},{10,8},{12,10},{14,12},{16,14},{18,... | collective-permute-start | bytes 608264 | tf_op jit(solution)/shard_map/ppermute | solution.py:19
  160.1 9.4 %collective-permute-start.19 = (bf16[528,192]{1,0:T(8,128)(2,1)S(1)}, bf16[528,192]{1,0:T(8,128)(2,1)S(1)}, u32[]{:S(2)}, u32[]{:S(2)}) collective-permute-start(bf16[528,192]{1,0:T(8,128)(2,1)S(1)} %maximum_maximum_fusion.4), channel_id=1, source_target_pairs={{0,2},{2,4},{4,6},{6,8},{8,10},{10,12},{12,14},{14,16},{16,18},{18... | collective-permute-start | bytes 608264 | tf_op jit(solution)/shard_map/ppermute | solution.py:19
  162.3 9.4 %collective-permute-start.22 = (bf16[528,192]{1,0:T(8,128)(2,1)S(1)}, bf16[528,192]{1,0:T(8,128)(2,1)S(1)}, u32[]{:S(2)}, u32[]{:S(2)}) collective-permute-start(bf16[528,192]{1,0:T(8,128)(2,1)S(1)} %maximum_maximum_fusion.5), channel_id=1, source_target_pairs={{0,30},{2,0},{4,2},{6,4},{8,6},{10,8},{12,10},{14,12},{16,14},{18,... | collective-permute-start | bytes 608264 | tf_op jit(solution)/shard_map/ppermute | solution.py:19
  169.8 8.4 %collective-permute-start.21 = (bf16[528,192]{1,0:T(8,128)(2,1)S(1)}, bf16[528,192]{1,0:T(8,128)(2,1)S(1)}, u32[]{:S(2)}, u32[]{:S(2)}) collective-permute-start(bf16[528,192]{1,0:T(8,128)(2,1)S(1)} %maximum_maximum_fusion.6), channel_id=1, source_target_pairs={{0,2},{2,4},{4,6},{6,8},{8,10},{10,12},{12,14},{14,16},{16,18},{18... | collective-permute-start | bytes 608264 | tf_op jit(solution)/shard_map/ppermute | solution.py:19
  172.0 8.4 %collective-permute-start.24 = (bf16[528,192]{1,0:T(8,128)(2,1)S(1)}, bf16[528,192]{1,0:T(8,128)(2,1)S(1)}, u32[]{:S(2)}, u32[]{:S(2)}) collective-permute-start(bf16[528,192]{1,0:T(8,128)(2,1)S(1)} %maximum_maximum_fusion.7), channel_id=1, source_target_pairs={{0,30},{2,0},{4,2},{6,4},{8,6},{10,8},{12,10},{14,12},{16,14},{18,... | collective-permute-start | bytes 608264 | tf_op jit(solution)/shard_map/ppermute | solution.py:19
  178.5 8.4 %collective-permute-start.23 = (bf16[528,192]{1,0:T(8,128)(2,1)S(1)}, bf16[528,192]{1,0:T(8,128)(2,1)S(1)}, u32[]{:S(2)}, u32[]{:S(2)}) collective-permute-start(bf16[528,192]{1,0:T(8,128)(2,1)S(1)} %maximum_maximum_fusion.8), channel_id=1, source_target_pairs={{0,2},{2,4},{4,6},{6,8},{8,10},{10,12},{12,14},{14,16},{16,18},{18... | collective-permute-start | bytes 608264 | tf_op jit(solution)/shard_map/ppermute | solution.py:19
  180.7 8.4 %collective-permute-start.26 = (bf16[528,192]{1,0:T(8,128)(2,1)S(1)}, bf16[528,192]{1,0:T(8,128)(2,1)S(1)}, u32[]{:S(2)}, u32[]{:S(2)}) collective-permute-start(bf16[528,192]{1,0:T(8,128)(2,1)S(1)} %maximum_maximum_fusion.9), channel_id=1, source_target_pairs={{0,30},{2,0},{4,2},{6,4},{8,6},{10,8},{12,10},{14,12},{16,14},{18,... | collective-permute-start | bytes 608264 | tf_op jit(solution)/shard_map/ppermute | solution.py:19
  187.1 8.4 %collective-permute-start.25 = (bf16[528,192]{1,0:T(8,128)(2,1)S(1)}, bf16[528,192]{1,0:T(8,128)(2,1)S(1)}, u32[]{:S(2)}, u32[]{:S(2)}) collective-permute-start(bf16[528,192]{1,0:T(8,128)(2,1)S(1)} %maximum_maximum_fusion.10), channel_id=1, source_target_pairs={{0,2},{2,4},{4,6},{6,8},{8,10},{10,12},{12,14},{14,16},{16,18},{18... | collective-permute-start | bytes 608264 | tf_op jit(solution)/shard_map/ppermute | solution.py:19
  189.3 8.4 %collective-permute-start.28 = (bf16[528,192]{1,0:T(8,128)(2,1)S(1)}, bf16[528,192]{1,0:T(8,128)(2,1)S(1)}, u32[]{:S(2)}, u32[]{:S(2)}) collective-permute-start(bf16[528,192]{1,0:T(8,128)(2,1)S(1)} %maximum_maximum_fusion.11), channel_id=1, source_target_pairs={{0,30},{2,0},{4,2},{6,4},{8,6},{10,8},{12,10},{14,12},{16,14},{18,... | collective-permute-start | bytes 608264 | tf_op jit(solution)/shard_map/ppermute | solution.py:19
  195.8 8.4 %collective-permute-start.27 = (bf16[528,192]{1,0:T(8,128)(2,1)S(1)}, bf16[528,192]{1,0:T(8,128)(2,1)S(1)}, u32[]{:S(2)}, u32[]{:S(2)}) collective-permute-start(bf16[528,192]{1,0:T(8,128)(2,1)S(1)} %maximum_maximum_fusion.12), channel_id=1, source_target_pairs={{0,2},{2,4},{4,6},{6,8},{8,10},{10,12},{12,14},{14,16},{16,18},{18... | collective-permute-start | bytes 608264 | tf_op jit(solution)/shard_map/ppermute | solution.py:19
  198.0 8.6 %collective-permute-start.30 = (bf16[528,192]{1,0:T(8,128)(2,1)S(1)}, bf16[528,192]{1,0:T(8,128)(2,1)S(1)}, u32[]{:S(2)}, u32[]{:S(2)}) collective-permute-start(bf16[528,192]{1,0:T(8,128)(2,1)S(1)} %maximum_maximum_fusion.13), channel_id=1, source_target_pairs={{0,30},{2,0},{4,2},{6,4},{8,6},{10,8},{12,10},{14,12},{16,14},{18,... | collective-permute-start | bytes 608264 | tf_op jit(solution)/shard_map/ppermute | solution.py:19
  204.5 9.1 %collective-permute-start.29 = (bf16[528,192]{1,0:T(8,128)(2,1)S(1)}, bf16[528,192]{1,0:T(8,128)(2,1)S(1)}, u32[]{:S(2)}, u32[]{:S(2)}) collective-permute-start(bf16[528,192]{1,0:T(8,128)(2,1)S(1)} %maximum_maximum_fusion.14), channel_id=1, source_target_pairs={{0,2},{2,4},{4,6},{6,8},{8,10},{10,12},{12,14},{14,16},{16,18},{18... | collective-permute-start | bytes 608264 | tf_op jit(solution)/shard_map/ppermute | solution.py:19
  214.8 24.2 %collective-permute-start.31 = (bf16[2,256,192]{2,1,0:T(8,128)(2,1)S(1)}, bf16[2,256,192]{2,1,0:T(8,128)(2,1)S(1)}, u32[]{:S(2)}, u32[]{:S(2)}) collective-permute-start(bf16[2,256,192]{2,1,0:T(8,128)(2,1)S(1)} %pad_maximum_fusion), channel_id=1, source_target_pairs={{32,0},{64,32},{96,64},{128,96},{160,128},{192,160},{224,192},{256... | collective-permute-start | bytes 589832 | tf_op jit(solution)/shard_map/ppermute | solution.py:14
  (13 other events, 327.2 us)
